TPU v7x, 128 devices: a whole 4x4x4 slice. The times are simulated.
128 devices in a mesh: space: 16 (over x, y_hi, core), tm: 8 (over z, y_lo).
Axes of the slice: x: 4, y: 4 (y_hi: 2, y_lo: 2; y = y_hi * 2 + y_lo), z: 4, core: 2. Of those that a mesh axis runs over, the one named last changes fastest.
Arguments:
- source_snap: bfloat16 [32, 128, 64, 8, 256], P('space', 'tm'), may hold values from -1.796875 to 1.796875
- receiver_snap: bfloat16 [32, 128, 64, 8, 256], P('space', 'tm'), may hold values from -1.796875 to 1.796875
- start_tile: int32 [32], P('space'), may hold values from 0 to 14, as said below
Outputs:
- model_image: float32 [8, 64, 33, 2048], P('tm', None, None, 'space')
Inputs may be any that keep to these rules, and one draw needn't show every extreme that they name: `start_tile`: A shot held by index i of space (shots i * 2 to (i+1) * 2 - 1) has its first tile at i - 1 or i, limited to 0 .. 14; of the first two shots of each index, one is placed at i - 1 and the other at i before that limit.
All inputs are finite; a program needn't handle non-finite values.
Results may differ from a plain program's by a relative error of at most 0.0003.
Values may be sent and summed in bfloat16 or wider, within the bound.
No kernel may reach another device: no remote copies, remote signals or barrier semaphores. Data moves between devices by JAX's collectives and lax.ppermute only.
A program may use at most 128 MiB of HBM per device.

v0:
```python
import jax
import jax.numpy as jnp
from jax import lax
from jax.sharding import PartitionSpec as P

LAGS = 33
TILE = 128


def passed_along(block, axis, distance):
    devices = range(lax.axis_size(axis))
    route = [(i - distance, i) for i in devices if i - distance in devices]
    return lax.ppermute(block, axis, route)


def correlate(pair):
    src, rec = pair
    half = (LAGS - 1) // 2
    width = src.shape[4]
    pad_spec = ((0, 0), (0, 0), (0, 0), (0, 0), (half, half))
    src_pad = jnp.pad(src, pad_spec)
    rec_pad = jnp.pad(rec, pad_spec)

    def one_lag(lag):
        left = lax.dynamic_slice_in_dim(src_pad, half - (lag - half), width, 4)
        right = lax.dynamic_slice_in_dim(rec_pad, half + (lag - half), width, 4)
        return jnp.einsum("stczx,stczx->szcx", left, right, preferred_element_type=jnp.float32)

    planes = lax.map(one_lag, jnp.arange(LAGS, dtype=jnp.int32))
    return jnp.moveaxis(planes, 0, 3)


def place_tiles(image, first, base, slots):
    shots, depth_rows, chans, lags, width = image.shape
    blocks = image.reshape(shots, depth_rows, chans, lags, 2, TILE)
    target = first[:, None] + jnp.arange(2, dtype=jnp.int32)[None, :] - base
    onehot = (target[:, :, None] == jnp.arange(slots, dtype=jnp.int32)[None, None, :]).astype(
        jnp.float32
    )
    return jnp.einsum("szchax,sak->zchkx", blocks, onehot, precision=lax.Precision.HIGHEST)


def body(source_snap, receiver_snap, start_tile):
    moved = (
        lax.all_to_all(source_snap, "tm", split_axis=3, concat_axis=1, tiled=True),
        lax.all_to_all(receiver_snap, "tm", split_axis=3, concat_axis=1, tiled=True),
    )
    image = correlate(moved)
    owner = lax.axis_index("space")
    placed = place_tiles(image, start_tile, owner - 1, 3)
    own_part = placed[:, :, :, 1, :]
    right_part = passed_along(placed[:, :, :, 0, :], "space", -1)
    left_part = passed_along(placed[:, :, :, 2, :], "space", 1)
    return own_part + right_part + left_part


def solution(mesh):
    in_specs = (P("space", "tm", None, None, None), P("space", "tm", None, None, None), P("space"))
    out_specs = P("tm", None, None, "space")
    return jax.shard_map(body, mesh=mesh, in_specs=in_specs, out_specs=out_specs, check_vma=False)
```

profile of v0, /device:TPU:3, one launch (start us, length us, event | category | flops | bytes accessed | tf_op | source)
XLA Modules:
  0.0 795.1 jit_solution(17354770452854275581)
XLA Ops:
  0.0 8.6 %copy.16 = bf16[2,16,64,8,256]{4,2,1,0,3:T(8,128)(2,1)} copy(bf16[2,16,64,8,256]{4,3,2,1,0:T(8,128)(2,1)} %param.5) | data formatting | bytes 16777216 | tf_op args[0]
  8.6 6.0 all-to-all-start
  14.7 8.7 %copy.18 = bf16[2,16,64,8,256]{4,2,1,0,3:T(8,128)(2,1)} copy(bf16[2,16,64,8,256]{4,3,2,1,0:T(8,128)(2,1)} %param.6) | data formatting | bytes 16777216 | tf_op args[1]
  23.4 85.0 %all-to-all-done = bf16[2,16,64,8,256]{4,2,1,0,3:T(8,128)(2,1)} async-done(((bf16[2,16,64,8,256]{4,2,1,0,3:T(8,128)(2,1)}), bf16[2,16,64,8,256]{4,2,1,0,3:T(8,128)(2,1)}, u32[]{:S(2)}, u32[]{:S(2)}) %all-to-all-start) | async-done | bytes 8388640 | tf_op jit(solution)/shard_map/all_to_all | solution.py:45
  108.4 5.2 all-to-all-start.1
  113.6 8.4 %copy.17 = bf16[2,16,64,8,256]{4,2,1,3,0:T(8,128)(2,1)} copy(bf16[2,16,64,8,256]{4,2,1,0,3:T(8,128)(2,1)} %all-to-all-done) | data formatting | bytes 16777216 | tf_op jit(solution)/shard_map/all_to_all | solution.py:45
  122.0 11.4 %pad.7 = bf16[2,128,64,1,288]{4,2,1,0,3:T(8,128)(2,1)} pad(bf16[2,128,64,1,256]{4,2,1,0,3:T(8,128)(2,1)} %bitcast.60, bf16[]{:T(256)} %constant.65.clone.1), padding=0_0x0_0x0_0x0_0x16_16 | pad | bytes 17825794 | tf_op jit(solution)/shard_map/jit(_pad)/pad | solution.py:21
  133.4 72.7 %all-to-all-done.1 = bf16[2,16,64,8,256]{4,2,1,0,3:T(8,128)(2,1)} async-done(((bf16[2,16,64,8,256]{4,2,1,0,3:T(8,128)(2,1)}), bf16[2,16,64,8,256]{4,2,1,0,3:T(8,128)(2,1)}, u32[]{:S(2)}, u32[]{:S(2)}) %all-to-all-start.1) | async-done | bytes 8388640 | tf_op jit(solution)/shard_map/all_to_all | solution.py:46
  206.1 8.3 %copy.19 = bf16[2,16,64,8,256]{4,2,1,3,0:T(8,128)(2,1)} copy(bf16[2,16,64,8,256]{4,2,1,0,3:T(8,128)(2,1)} %all-to-all-done.1) | data formatting | bytes 16777216 | tf_op jit(solution)/shard_map/all_to_all | solution.py:46
  214.4 11.4 %pad.8 = bf16[2,128,64,1,288]{4,2,1,0,3:T(8,128)(2,1)} pad(bf16[2,128,64,1,256]{4,2,1,0,3:T(8,128)(2,1)} %bitcast.59, bf16[]{:T(256)} %constant.65.clone.1), padding=0_0x0_0x0_0x0_0x16_16 | pad | bytes 17825794 | tf_op jit(solution)/shard_map/jit(_pad)/pad | solution.py:22
  225.8 512.4 %while.15 = (s32[]{:T(128)}, f32[33,2,1,64,256]{4,3,2,1,0:T(8,128)}, s32[33]{0:T(128)S(1)}, bf16[2,128,64,1,288]{4,2,1,0,3:T(8,128)(2,1)}, bf16[2,128,64,1,288]{...) while((s32[]{:T(128)}, ...), condition=%wide.region_1.2_spmd, body=%wide.region_0.1_spmd.sunk | while | flops 16744458 | bytes 17171164 | solution.py:29
  228.9 11.7 %fusion.13 = f32[2,64,256]{2,1,0:T(8,128)S(1)} fusion(bf16[2,128,64,1,288]{4,2,1,0,3:T(8,128)(2,1)} %get-tuple-element.198, s32[]{:T(128)S(6)} %select_n.22, bf16[2,128,64,1,288]{4,2,1,0,3:T(8,128)(2,1)} %get-tuple-element.197, s32[]{:T(128)S(6)} %select_n.23), kind=kLoop, calls=%fused_computation.1.clone.1 | loop fusion | flops 16744448 | bytes 16908296 | tf_op jit(solution)/shard_map/while/body/eval_jaxpr/stczx,stczx->szcx/dot_general | solution.py:27
  244.4 11.7 %fusion.13 = f32[2,64,256]{2,1,0:T(8,128)S(1)} fusion(bf16[2,128,64,1,288]{4,2,1,0,3:T(8,128)(2,1)} %get-tuple-element.198, s32[]{:T(128)S(6)} %select_n.22, bf16[2,128,64,1,288]{4,2,1,0,3:T(8,128)(2,1)} %get-tuple-element.197, s32[]{:T(128)S(6)} %select_n.23), kind=kLoop, calls=%fused_computation.1.clone.1 | loop fusion | flops 16744448 | bytes 16908296 | tf_op jit(solution)/shard_map/while/body/eval_jaxpr/stczx,stczx->szcx/dot_general | solution.py:27
  259.9 11.7 %fusion.13 = f32[2,64,256]{2,1,0:T(8,128)S(1)} fusion(bf16[2,128,64,1,288]{4,2,1,0,3:T(8,128)(2,1)} %get-tuple-element.198, s32[]{:T(128)S(6)} %select_n.22, bf16[2,128,64,1,288]{4,2,1,0,3:T(8,128)(2,1)} %get-tuple-element.197, s32[]{:T(128)S(6)} %select_n.23), kind=kLoop, calls=%fused_computation.1.clone.1 | loop fusion | flops 16744448 | bytes 16908296 | tf_op jit(solution)/shard_map/while/body/eval_jaxpr/stczx,stczx->szcx/dot_general | solution.py:27
  275.5 11.7 %fusion.13 = f32[2,64,256]{2,1,0:T(8,128)S(1)} fusion(bf16[2,128,64,1,288]{4,2,1,0,3:T(8,128)(2,1)} %get-tuple-element.198, s32[]{:T(128)S(6)} %select_n.22, bf16[2,128,64,1,288]{4,2,1,0,3:T(8,128)(2,1)} %get-tuple-element.197, s32[]{:T(128)S(6)} %select_n.23), kind=kLoop, calls=%fused_computation.1.clone.1 | loop fusion | flops 16744448 | bytes 16908296 | tf_op jit(solution)/shard_map/while/body/eval_jaxpr/stczx,stczx->szcx/dot_general | solution.py:27
  291.0 11.7 %fusion.13 = f32[2,64,256]{2,1,0:T(8,128)S(1)} fusion(bf16[2,128,64,1,288]{4,2,1,0,3:T(8,128)(2,1)} %get-tuple-element.198, s32[]{:T(128)S(6)} %select_n.22, bf16[2,128,64,1,288]{4,2,1,0,3:T(8,128)(2,1)} %get-tuple-element.197, s32[]{:T(128)S(6)} %select_n.23), kind=kLoop, calls=%fused_computation.1.clone.1 | loop fusion | flops 16744448 | bytes 16908296 | tf_op jit(solution)/shard_map/while/body/eval_jaxpr/stczx,stczx->szcx/dot_general | solution.py:27
  306.5 11.7 %fusion.13 = f32[2,64,256]{2,1,0:T(8,128)S(1)} fusion(bf16[2,128,64,1,288]{4,2,1,0,3:T(8,128)(2,1)} %get-tuple-element.198, s32[]{:T(128)S(6)} %select_n.22, bf16[2,128,64,1,288]{4,2,1,0,3:T(8,128)(2,1)} %get-tuple-element.197, s32[]{:T(128)S(6)} %select_n.23), kind=kLoop, calls=%fused_computation.1.clone.1 | loop fusion | flops 16744448 | bytes 16908296 | tf_op jit(solution)/shard_map/while/body/eval_jaxpr/stczx,stczx->szcx/dot_general | solution.py:27
  322.0 11.7 %fusion.13 = f32[2,64,256]{2,1,0:T(8,128)S(1)} fusion(bf16[2,128,64,1,288]{4,2,1,0,3:T(8,128)(2,1)} %get-tuple-element.198, s32[]{:T(128)S(6)} %select_n.22, bf16[2,128,64,1,288]{4,2,1,0,3:T(8,128)(2,1)} %get-tuple-element.197, s32[]{:T(128)S(6)} %select_n.23), kind=kLoop, calls=%fused_computation.1.clone.1 | loop fusion | flops 16744448 | bytes 16908296 | tf_op jit(solution)/shard_map/while/body/eval_jaxpr/stczx,stczx->szcx/dot_general | solution.py:27
  337.6 11.7 %fusion.13 = f32[2,64,256]{2,1,0:T(8,128)S(1)} fusion(bf16[2,128,64,1,288]{4,2,1,0,3:T(8,128)(2,1)} %get-tuple-element.198, s32[]{:T(128)S(6)} %select_n.22, bf16[2,128,64,1,288]{4,2,1,0,3:T(8,128)(2,1)} %get-tuple-element.197, s32[]{:T(128)S(6)} %select_n.23), kind=kLoop, calls=%fused_computation.1.clone.1 | loop fusion | flops 16744448 | bytes 16908296 | tf_op jit(solution)/shard_map/while/body/eval_jaxpr/stczx,stczx->szcx/dot_general | solution.py:27
  353.1 11.7 %fusion.13 = f32[2,64,256]{2,1,0:T(8,128)S(1)} fusion(bf16[2,128,64,1,288]{4,2,1,0,3:T(8,128)(2,1)} %get-tuple-element.198, s32[]{:T(128)S(6)} %select_n.22, bf16[2,128,64,1,288]{4,2,1,0,3:T(8,128)(2,1)} %get-tuple-element.197, s32[]{:T(128)S(6)} %select_n.23), kind=kLoop, calls=%fused_computation.1.clone.1 | loop fusion | flops 16744448 | bytes 16908296 | tf_op jit(solution)/shard_map/while/body/eval_jaxpr/stczx,stczx->szcx/dot_general | solution.py:27
  368.7 11.7 %fusion.13 = f32[2,64,256]{2,1,0:T(8,128)S(1)} fusion(bf16[2,128,64,1,288]{4,2,1,0,3:T(8,128)(2,1)} %get-tuple-element.198, s32[]{:T(128)S(6)} %select_n.22, bf16[2,128,64,1,288]{4,2,1,0,3:T(8,128)(2,1)} %get-tuple-element.197, s32[]{:T(128)S(6)} %select_n.23), kind=kLoop, calls=%fused_computation.1.clone.1 | loop fusion | flops 16744448 | bytes 16908296 | tf_op jit(solution)/shard_map/while/body/eval_jaxpr/stczx,stczx->szcx/dot_general | solution.py:27
  384.2 11.7 %fusion.13 = f32[2,64,256]{2,1,0:T(8,128)S(1)} fusion(bf16[2,128,64,1,288]{4,2,1,0,3:T(8,128)(2,1)} %get-tuple-element.198, s32[]{:T(128)S(6)} %select_n.22, bf16[2,128,64,1,288]{4,2,1,0,3:T(8,128)(2,1)} %get-tuple-element.197, s32[]{:T(128)S(6)} %select_n.23), kind=kLoop, calls=%fused_computation.1.clone.1 | loop fusion | flops 16744448 | bytes 16908296 | tf_op jit(solution)/shard_map/while/body/eval_jaxpr/stczx,stczx->szcx/dot_general | solution.py:27
  399.7 11.7 %fusion.13 = f32[2,64,256]{2,1,0:T(8,128)S(1)} fusion(bf16[2,128,64,1,288]{4,2,1,0,3:T(8,128)(2,1)} %get-tuple-element.198, s32[]{:T(128)S(6)} %select_n.22, bf16[2,128,64,1,288]{4,2,1,0,3:T(8,128)(2,1)} %get-tuple-element.197, s32[]{:T(128)S(6)} %select_n.23), kind=kLoop, calls=%fused_computation.1.clone.1 | loop fusion | flops 16744448 | bytes 16908296 | tf_op jit(solution)/shard_map/while/body/eval_jaxpr/stczx,stczx->szcx/dot_general | solution.py:27
  415.2 11.7 %fusion.13 = f32[2,64,256]{2,1,0:T(8,128)S(1)} fusion(bf16[2,128,64,1,288]{4,2,1,0,3:T(8,128)(2,1)} %get-tuple-element.198, s32[]{:T(128)S(6)} %select_n.22, bf16[2,128,64,1,288]{4,2,1,0,3:T(8,128)(2,1)} %get-tuple-element.197, s32[]{:T(128)S(6)} %select_n.23), kind=kLoop, calls=%fused_computation.1.clone.1 | loop fusion | flops 16744448 | bytes 16908296 | tf_op jit(solution)/shard_map/while/body/eval_jaxpr/stczx,stczx->szcx/dot_general | solution.py:27
  430.7 11.7 %fusion.13 = f32[2,64,256]{2,1,0:T(8,128)S(1)} fusion(bf16[2,128,64,1,288]{4,2,1,0,3:T(8,128)(2,1)} %get-tuple-element.198, s32[]{:T(128)S(6)} %select_n.22, bf16[2,128,64,1,288]{4,2,1,0,3:T(8,128)(2,1)} %get-tuple-element.197, s32[]{:T(128)S(6)} %select_n.23), kind=kLoop, calls=%fused_computation.1.clone.1 | loop fusion | flops 16744448 | bytes 16908296 | tf_op jit(solution)/shard_map/while/body/eval_jaxpr/stczx,stczx->szcx/dot_general | solution.py:27
  446.3 11.7 %fusion.13 = f32[2,64,256]{2,1,0:T(8,128)S(1)} fusion(bf16[2,128,64,1,288]{4,2,1,0,3:T(8,128)(2,1)} %get-tuple-element.198, s32[]{:T(128)S(6)} %select_n.22, bf16[2,128,64,1,288]{4,2,1,0,3:T(8,128)(2,1)} %get-tuple-element.197, s32[]{:T(128)S(6)} %select_n.23), kind=kLoop, calls=%fused_computation.1.clone.1 | loop fusion | flops 16744448 | bytes 16908296 | tf_op jit(solution)/shard_map/while/body/eval_jaxpr/stczx,stczx->szcx/dot_general | solution.py:27
  461.8 11.7 %fusion.13 = f32[2,64,256]{2,1,0:T(8,128)S(1)} fusion(bf16[2,128,64,1,288]{4,2,1,0,3:T(8,128)(2,1)} %get-tuple-element.198, s32[]{:T(128)S(6)} %select_n.22, bf16[2,128,64,1,288]{4,2,1,0,3:T(8,128)(2,1)} %get-tuple-element.197, s32[]{:T(128)S(6)} %select_n.23), kind=kLoop, calls=%fused_computation.1.clone.1 | loop fusion | flops 16744448 | bytes 16908296 | tf_op jit(solution)/shard_map/while/body/eval_jaxpr/stczx,stczx->szcx/dot_general | solution.py:27
  477.3 11.7 %fusion.13 = f32[2,64,256]{2,1,0:T(8,128)S(1)} fusion(bf16[2,128,64,1,288]{4,2,1,0,3:T(8,128)(2,1)} %get-tuple-element.198, s32[]{:T(128)S(6)} %select_n.22, bf16[2,128,64,1,288]{4,2,1,0,3:T(8,128)(2,1)} %get-tuple-element.197, s32[]{:T(128)S(6)} %select_n.23), kind=kLoop, calls=%fused_computation.1.clone.1 | loop fusion | flops 16744448 | bytes 16908296 | tf_op jit(solution)/shard_map/while/body/eval_jaxpr/stczx,stczx->szcx/dot_general | solution.py:27
  492.8 11.7 %fusion.13 = f32[2,64,256]{2,1,0:T(8,128)S(1)} fusion(bf16[2,128,64,1,288]{4,2,1,0,3:T(8,128)(2,1)} %get-tuple-element.198, s32[]{:T(128)S(6)} %select_n.22, bf16[2,128,64,1,288]{4,2,1,0,3:T(8,128)(2,1)} %get-tuple-element.197, s32[]{:T(128)S(6)} %select_n.23), kind=kLoop, calls=%fused_computation.1.clone.1 | loop fusion | flops 16744448 | bytes 16908296 | tf_op jit(solution)/shard_map/while/body/eval_jaxpr/stczx,stczx->szcx/dot_general | solution.py:27
  508.4 11.7 %fusion.13 = f32[2,64,256]{2,1,0:T(8,128)S(1)} fusion(bf16[2,128,64,1,288]{4,2,1,0,3:T(8,128)(2,1)} %get-tuple-element.198, s32[]{:T(128)S(6)} %select_n.22, bf16[2,128,64,1,288]{4,2,1,0,3:T(8,128)(2,1)} %get-tuple-element.197, s32[]{:T(128)S(6)} %select_n.23), kind=kLoop, calls=%fused_computation.1.clone.1 | loop fusion | flops 16744448 | bytes 16908296 | tf_op jit(solution)/shard_map/while/body/eval_jaxpr/stczx,stczx->szcx/dot_general | solution.py:27
  523.9 11.7 %fusion.13 = f32[2,64,256]{2,1,0:T(8,128)S(1)} fusion(bf16[2,128,64,1,288]{4,2,1,0,3:T(8,128)(2,1)} %get-tuple-element.198, s32[]{:T(128)S(6)} %select_n.22, bf16[2,128,64,1,288]{4,2,1,0,3:T(8,128)(2,1)} %get-tuple-element.197, s32[]{:T(128)S(6)} %select_n.23), kind=kLoop, calls=%fused_computation.1.clone.1 | loop fusion | flops 16744448 | bytes 16908296 | tf_op jit(solution)/shard_map/while/body/eval_jaxpr/stczx,stczx->szcx/dot_general | solution.py:27
  539.4 11.7 %fusion.13 = f32[2,64,256]{2,1,0:T(8,128)S(1)} fusion(bf16[2,128,64,1,288]{4,2,1,0,3:T(8,128)(2,1)} %get-tuple-element.198, s32[]{:T(128)S(6)} %select_n.22, bf16[2,128,64,1,288]{4,2,1,0,3:T(8,128)(2,1)} %get-tuple-element.197, s32[]{:T(128)S(6)} %select_n.23), kind=kLoop, calls=%fused_computation.1.clone.1 | loop fusion | flops 16744448 | bytes 16908296 | tf_op jit(solution)/shard_map/while/body/eval_jaxpr/stczx,stczx->szcx/dot_general | solution.py:27
  555.0 11.7 %fusion.13 = f32[2,64,256]{2,1,0:T(8,128)S(1)} fusion(bf16[2,128,64,1,288]{4,2,1,0,3:T(8,128)(2,1)} %get-tuple-element.198, s32[]{:T(128)S(6)} %select_n.22, bf16[2,128,64,1,288]{4,2,1,0,3:T(8,128)(2,1)} %get-tuple-element.197, s32[]{:T(128)S(6)} %select_n.23), kind=kLoop, calls=%fused_computation.1.clone.1 | loop fusion | flops 16744448 | bytes 16908296 | tf_op jit(solution)/shard_map/while/body/eval_jaxpr/stczx,stczx->szcx/dot_general | solution.py:27
  570.5 11.7 %fusion.13 = f32[2,64,256]{2,1,0:T(8,128)S(1)} fusion(bf16[2,128,64,1,288]{4,2,1,0,3:T(8,128)(2,1)} %get-tuple-element.198, s32[]{:T(128)S(6)} %select_n.22, bf16[2,128,64,1,288]{4,2,1,0,3:T(8,128)(2,1)} %get-tuple-element.197, s32[]{:T(128)S(6)} %select_n.23), kind=kLoop, calls=%fused_computation.1.clone.1 | loop fusion | flops 16744448 | bytes 16908296 | tf_op jit(solution)/shard_map/while/body/eval_jaxpr/stczx,stczx->szcx/dot_general | solution.py:27
  586.0 11.7 %fusion.13 = f32[2,64,256]{2,1,0:T(8,128)S(1)} fusion(bf16[2,128,64,1,288]{4,2,1,0,3:T(8,128)(2,1)} %get-tuple-element.198, s32[]{:T(128)S(6)} %select_n.22, bf16[2,128,64,1,288]{4,2,1,0,3:T(8,128)(2,1)} %get-tuple-element.197, s32[]{:T(128)S(6)} %select_n.23), kind=kLoop, calls=%fused_computation.1.clone.1 | loop fusion | flops 16744448 | bytes 16908296 | tf_op jit(solution)/shard_map/while/body/eval_jaxpr/stczx,stczx->szcx/dot_general | solution.py:27
  601.6 11.7 %fusion.13 = f32[2,64,256]{2,1,0:T(8,128)S(1)} fusion(bf16[2,128,64,1,288]{4,2,1,0,3:T(8,128)(2,1)} %get-tuple-element.198, s32[]{:T(128)S(6)} %select_n.22, bf16[2,128,64,1,288]{4,2,1,0,3:T(8,128)(2,1)} %get-tuple-element.197, s32[]{:T(128)S(6)} %select_n.23), kind=kLoop, calls=%fused_computation.1.clone.1 | loop fusion | flops 16744448 | bytes 16908296 | tf_op jit(solution)/shard_map/while/body/eval_jaxpr/stczx,stczx->szcx/dot_general | solution.py:27
  617.1 11.7 %fusion.13 = f32[2,64,256]{2,1,0:T(8,128)S(1)} fusion(bf16[2,128,64,1,288]{4,2,1,0,3:T(8,128)(2,1)} %get-tuple-element.198, s32[]{:T(128)S(6)} %select_n.22, bf16[2,128,64,1,288]{4,2,1,0,3:T(8,128)(2,1)} %get-tuple-element.197, s32[]{:T(128)S(6)} %select_n.23), kind=kLoop, calls=%fused_computation.1.clone.1 | loop fusion | flops 16744448 | bytes 16908296 | tf_op jit(solution)/shard_map/while/body/eval_jaxpr/stczx,stczx->szcx/dot_general | solution.py:27
  632.6 11.7 %fusion.13 = f32[2,64,256]{2,1,0:T(8,128)S(1)} fusion(bf16[2,128,64,1,288]{4,2,1,0,3:T(8,128)(2,1)} %get-tuple-element.198, s32[]{:T(128)S(6)} %select_n.22, bf16[2,128,64,1,288]{4,2,1,0,3:T(8,128)(2,1)} %get-tuple-element.197, s32[]{:T(128)S(6)} %select_n.23), kind=kLoop, calls=%fused_computation.1.clone.1 | loop fusion | flops 16744448 | bytes 16908296 | tf_op jit(solution)/shard_map/while/body/eval_jaxpr/stczx,stczx->szcx/dot_general | solution.py:27
  648.1 11.7 %fusion.13 = f32[2,64,256]{2,1,0:T(8,128)S(1)} fusion(bf16[2,128,64,1,288]{4,2,1,0,3:T(8,128)(2,1)} %get-tuple-element.198, s32[]{:T(128)S(6)} %select_n.22, bf16[2,128,64,1,288]{4,2,1,0,3:T(8,128)(2,1)} %get-tuple-element.197, s32[]{:T(128)S(6)} %select_n.23), kind=kLoop, calls=%fused_computation.1.clone.1 | loop fusion | flops 16744448 | bytes 16908296 | tf_op jit(solution)/shard_map/while/body/eval_jaxpr/stczx,stczx->szcx/dot_general | solution.py:27
  663.7 11.7 %fusion.13 = f32[2,64,256]{2,1,0:T(8,128)S(1)} fusion(bf16[2,128,64,1,288]{4,2,1,0,3:T(8,128)(2,1)} %get-tuple-element.198, s32[]{:T(128)S(6)} %select_n.22, bf16[2,128,64,1,288]{4,2,1,0,3:T(8,128)(2,1)} %get-tuple-element.197, s32[]{:T(128)S(6)} %select_n.23), kind=kLoop, calls=%fused_computation.1.clone.1 | loop fusion | flops 16744448 | bytes 16908296 | tf_op jit(solution)/shard_map/while/body/eval_jaxpr/stczx,stczx->szcx/dot_general | solution.py:27
  679.2 11.7 %fusion.13 = f32[2,64,256]{2,1,0:T(8,128)S(1)} fusion(bf16[2,128,64,1,288]{4,2,1,0,3:T(8,128)(2,1)} %get-tuple-element.198, s32[]{:T(128)S(6)} %select_n.22, bf16[2,128,64,1,288]{4,2,1,0,3:T(8,128)(2,1)} %get-tuple-element.197, s32[]{:T(128)S(6)} %select_n.23), kind=kLoop, calls=%fused_computation.1.clone.1 | loop fusion | flops 16744448 | bytes 16908296 | tf_op jit(solution)/shard_map/while/body/eval_jaxpr/stczx,stczx->szcx/dot_general | solution.py:27
  694.7 11.7 %fusion.13 = f32[2,64,256]{2,1,0:T(8,128)S(1)} fusion(bf16[2,128,64,1,288]{4,2,1,0,3:T(8,128)(2,1)} %get-tuple-element.198, s32[]{:T(128)S(6)} %select_n.22, bf16[2,128,64,1,288]{4,2,1,0,3:T(8,128)(2,1)} %get-tuple-element.197, s32[]{:T(128)S(6)} %select_n.23), kind=kLoop, calls=%fused_computation.1.clone.1 | loop fusion | flops 16744448 | bytes 16908296 | tf_op jit(solution)/shard_map/while/body/eval_jaxpr/stczx,stczx->szcx/dot_general | solution.py:27
  710.2 11.7 %fusion.13 = f32[2,64,256]{2,1,0:T(8,128)S(1)} fusion(bf16[2,128,64,1,288]{4,2,1,0,3:T(8,128)(2,1)} %get-tuple-element.198, s32[]{:T(128)S(6)} %select_n.22, bf16[2,128,64,1,288]{4,2,1,0,3:T(8,128)(2,1)} %get-tuple-element.197, s32[]{:T(128)S(6)} %select_n.23), kind=kLoop, calls=%fused_computation.1.clone.1 | loop fusion | flops 16744448 | bytes 16908296 | tf_op jit(solution)/shard_map/while/body/eval_jaxpr/stczx,stczx->szcx/dot_general | solution.py:27
  725.8 11.7 %fusion.13 = f32[2,64,256]{2,1,0:T(8,128)S(1)} fusion(bf16[2,128,64,1,288]{4,2,1,0,3:T(8,128)(2,1)} %get-tuple-element.198, s32[]{:T(128)S(6)} %select_n.22, bf16[2,128,64,1,288]{4,2,1,0,3:T(8,128)(2,1)} %get-tuple-element.197, s32[]{:T(128)S(6)} %select_n.23), kind=kLoop, calls=%fused_computation.1.clone.1 | loop fusion | flops 16744448 | bytes 16908296 | tf_op jit(solution)/shard_map/while/body/eval_jaxpr/stczx,stczx->szcx/dot_general | solution.py:27
  738.1 6.0 reshape.50
  744.2 14.6 %fusion.3 = f32[1,64,33,3,128]{4,3,2,1,0:T(4,128)S(1)} fusion(f32[2,64,33,2,128]{4,3,1,0,2:T(2,128)} %reshape.50, s32[2,2]{0,1:T(2,128)S(1)} %add_subtract_fusion), kind=kOutput, calls=%fused_computation.5 | convolution fusion | flops 38928396 | bytes 7569424 | tf_op jit(solution)/shard_map/szchax,sak->zchkx/dot_general | solution.py:40
  760.4 4.6 collective-permute-start
  769.4 22.5 %collective-permute-done = f32[1,64,33,128]{3,0,2,1:T(1,128)S(1)} collective-permute-done((f32[1,64,33,128]{3,0,2,1:T(1,128)S(1)}, f32[1,64,33,128]{3,0,2,1:T(1,128)S(1)}, u32[]{:S(2)}, u32[]{:S(2)}) %collective-permute-start) | collective-permute-done | bytes 1081376 | tf_op jit(solution)/shard_map/ppermute | solution.py:13
  (76 shorter events, 52.3 us)
Async XLA Ops:
  8.6 99.7 %all-to-all-start = ((bf16[2,16,64,8,256]{4,2,1,0,3:T(8,128)(2,1)}), bf16[2,16,64,8,256]{4,2,1,0,3:T(8,128)(2,1)}, u32[]{:S(2)}, u32[]{:S(2)}) async-start(bf16[2,16,64,8,256]{4,2,1,0,3:T(8,128)(2,1)} %copy.16), calls=%async_computation | async-start | bytes 16777216 | tf_op jit(solution)/shard_map/all_to_all | solution.py:45
  23.4 90.2 %copy-start = (s32[2]{0:T(128)S(1)}, s32[2]{0:T(128)}, u32[]{:S(2)}) copy-start(s32[2]{0:T(128)} %param.7) | copy-start | bytes 28
  108.4 97.7 %all-to-all-start.1 = ((bf16[2,16,64,8,256]{4,2,1,0,3:T(8,128)(2,1)}), bf16[2,16,64,8,256]{4,2,1,0,3:T(8,128)(2,1)}, u32[]{:S(2)}, u32[]{:S(2)}) async-start(bf16[2,16,64,8,256]{4,2,1,0,3:T(8,128)(2,1)} %copy.18), calls=%async_computation.1 | async-start | bytes 16777216 | tf_op jit(solution)/shard_map/all_to_all | solution.py:46
  760.4 31.5 %collective-permute-start = (f32[1,64,33,128]{3,0,2,1:T(1,128)S(1)}, f32[1,64,33,128]{3,0,2,1:T(1,128)S(1)}, u32[]{:S(2)}, u32[]{:S(2)}) collective-permute-start(f32[1,64,33,128]{3,0,2,1:T(1,128)S(1)} %get-tuple-element.139), channel_id=1, source_target_pairs={{8,0},{16,8},{24,16},{32,24},{40,32},{48,40},{56,48},{64,56},{72,6... | collective-permute-start | bytes 3244040 | tf_op jit(solution)/shard_map/ppermute | solution.py:13
  765.0 26.9 %collective-permute-start.1 = (f32[1,64,33,128]{3,0,2,1:T(1,128)S(1)}, f32[1,64,33,128]{3,0,2,1:T(1,128)S(1)}, u32[]{:S(2)}, u32[]{:S(2)}) collective-permute-start(f32[1,64,33,128]{3,0,2,1:T(1,128)S(1)} %get-tuple-element.140), channel_id=1, source_target_pairs={{0,8},{8,16},{16,24},{24,32},{32,40},{40,48},{48,56},{56,64},{64,7... | collective-permute-start | bytes 3244040 | tf_op jit(solution)/shard_map/ppermute | solution.py:13
where the time goes:
time: 797 us; the launch traced here: 795 us
  other arithmetic  389 us (49%)
  waiting for transfers between devices  180 us (23%)
  local copies, waits for them, and re-layouts  109 us (14%)
  loops' own time  82.4 us (10%)
  starting transfers between devices  20.2 us (3%)
  matrix products  14.6 us (2%)
    dot_general x33, other arithmetic, one_lag(): jnp.einsum('stczx,stczx->szcx', left, right, preferred_element_type=jnp.f...  387 us
    all_to_all x1, waiting for transfers between devices, body(): lax.all_to_all(source_snap, 'tm', split_axis=3, concat_axis=1, tiled=True)  85 us
    another operation x1, loops' own time, correlate(): planes = lax.map(one_lag, jnp.arange(LAGS, dtype=jnp.int32))  82.4 us
    all_to_all x1, waiting for transfers between devices, body(): lax.all_to_all(receiver_snap, 'tm', split_axis=3, concat_axis=1, tiled=True)  72.7 us
    ppermute x2, waiting for transfers between devices, passed_along(): return lax.ppermute(block, axis, route)  22.5 us
    dynamic_update_slice x33, local copies, waits for them, and re-layouts, correlate(): planes = lax.map(one_lag, jnp.arange(LAGS, dtype=jnp.int32))  22 us
    dynamic_slice x33, local copies, waits for them, and re-layouts, correlate(): planes = lax.map(one_lag, jnp.arange(LAGS, dtype=jnp.int32))  21 us
    unnamed x4, local copies, waits for them, and re-layouts  17.3 us
  transfers between devices with their start and end apart: 4, of which 3 were waited for; matrix products, arithmetic and copies ran while one was open for 4% of the time, Pallas kernels for 0%

commit v1 on v0

v1 whole, which is shorter than its diff:
```python
import functools

import jax
import jax.numpy as jnp
from jax import lax
from jax.experimental import pallas as pl
from jax.experimental.pallas import tpu as pltpu
from jax.sharding import PartitionSpec as P

LAGS = 33
TILE = 128
CB = 8


def passed_along(block, axis, distance):
    devices = range(lax.axis_size(axis))
    route = [(i - distance, i) for i in devices if i - distance in devices]
    return lax.ppermute(block, axis, route)


def lag_kernel(s_ref, r_ref, o_ref, band_ref):
    src, _, cb, t16, width = s_ref.shape
    half = (LAGS - 1) // 2
    rows = band_ref.shape[0]
    u_i = lax.broadcasted_iota(jnp.int32, (width, width), 0)
    k_i = lax.broadcasted_iota(jnp.int32, (width, width), 1)
    v_ok = (u_i - k_i + 2 * half >= 0) & (u_i - k_i + 2 * half < width)
    x_i = lax.broadcasted_iota(jnp.int32, (1, width), 1)

    def one_channel(c, carry):
        s_t = s_ref[:, 0, c, :, :].reshape(src * t16, width)
        r_t = r_ref[:, 0, c, :, :].reshape(src * t16, width)
        g = lax.dot_general(s_t, r_t, (((0,), (0,)), ((), ())),
                            preferred_element_type=jnp.float32)
        q = pltpu.roll(g, 2 * half + 1, 1, stride=1, stride_axis=0)
        q = jnp.where(v_ok, q, 0.0)
        band_ref[...] = q[:, :TILE].T[:rows, :]
        for j in range(LAGS):
            d = half - j
            w = band_ref[2 * j:2 * j + 1, :]
            out = pltpu.roll(w, d % width, 1)
            out = jnp.where((x_i - d >= 0) & (x_i - d < width), out, 0.0)
            o_ref[0, c, pl.ds(half + d, 1), :] = out
        return carry

    lax.fori_loop(0, cb, one_channel, 0)


def lag_images(src, rec):
    n_src, shots, chans, t16, width = src.shape
    in_spec = pl.BlockSpec((n_src, 1, CB, t16, width), lambda i, j: (0, i, j, 0, 0))
    return pl.pallas_call(
        lag_kernel,
        grid=(shots, chans // CB),
        in_specs=[in_spec, in_spec],
        out_specs=pl.BlockSpec((1, CB, LAGS, width), lambda i, j: (i, j, 0, 0)),
        out_shape=jax.ShapeDtypeStruct((shots, chans, LAGS, width), jnp.float32),
        scratch_shapes=[pltpu.VMEM((72, width), jnp.float32)],
    )(src, rec)


def place_tiles(image, first, base, slots):
    shots, chans, lags, width = image.shape
    blocks = image.reshape(shots, chans, lags, 2, TILE)
    target = first[:, None] + jnp.arange(2, dtype=jnp.int32)[None, :] - base
    out = []
    for k in range(slots):
        acc = None
        for s in range(shots):
            for a in range(2):
                term = jnp.where(target[s, a] == k, blocks[s, :, :, a, :], 0.0)
                acc = term if acc is None else acc + term
        out.append(acc)
    return out


def body(source_snap, receiver_snap, start_tile):
    def moved(x, flip=False):
        if flip:
            x = jnp.flip(x, axis=4)
        x = jnp.transpose(x, (3, 0, 2, 1, 4))
        return lax.all_to_all(x, "tm", split_axis=0, concat_axis=0, tiled=True)

    image = lag_images(moved(source_snap), moved(receiver_snap, True))
    owner = lax.axis_index("space")
    placed = place_tiles(image, start_tile, owner - 1, 3)
    own_part = placed[1]
    right_part = passed_along(placed[0], "space", -1)
    left_part = passed_along(placed[2], "space", 1)
    return (own_part + right_part + left_part)[None]


def solution(mesh):
    in_specs = (P("space", "tm", None, None, None), P("space", "tm", None, None, None), P("space"))
    out_specs = P("tm", None, None, "space")
    return jax.shard_map(body, mesh=mesh, in_specs=in_specs, out_specs=out_specs, check_vma=False)
```

time: 797 us -> 349 us (0.44)
  other arithmetic: 389 us -> 4.27 us
  loops' own time: 82.4 us -> 0 us
  Pallas kernels: 0 us -> 66.5 us
  local copies, waits for them, and re-layouts: 109 us -> 59.6 us
  matrix products: 14.6 us -> 0 us
  waiting for transfers between devices: 180 us -> 190 us
    dot_general x33 -> x0, other arithmetic: 387 us -> none  [one_lag(): jnp.einsum('stczx,stczx->szcx', left, right, preferred_element_type=jnp.f...]
    another operation x1 -> x0, loops' own time: 82.4 us -> none  [correlate(): planes = lax.map(one_lag, jnp.arange(LAGS, dtype=jnp.int32))]
    pallas_call x0 -> x1, Pallas kernels: none -> 66.5 us  [lag_images(): pl.pallas_call(lag_kernel, grid=(shots, chans // CB), in_specs=[in_spec,...]
    pad x2 -> x0, local copies, waits for them, and re-layouts: 22.8 us -> none  [the longest x1 11.4 us: correlate(): rec_pad = jnp.pad(rec, pad_spec)]
    dynamic_update_slice x33 -> x0, local copies, waits for them, and re-layouts: 22 us -> none  [correlate(): planes = lax.map(one_lag, jnp.arange(LAGS, dtype=jnp.int32))]
    dynamic_slice x33 -> x0, local copies, waits for them, and re-layouts: 21 us -> none  [correlate(): planes = lax.map(one_lag, jnp.arange(LAGS, dtype=jnp.int32))]
    rev x0 -> x1, local copies, waits for them, and re-layouts: none -> 20.8 us  [moved(): x = jnp.flip(x, axis=4)]
    all_to_all x2 -> x0, local copies, waits for them, and re-layouts: 16.6 us -> none  [the longest x1 8.38 us: body(): lax.all_to_all(source_snap, 'tm', split_axis=3, concat_axis=1, tiled=True)]
  transfers between devices with their start and end apart: 4 -> 4, of which waited for: 3 -> 4; matrix products, arithmetic and copies ran while one was open for 4% -> 3% of each run, Pallas kernels for 0% -> 0%
where the time goes in v1:
time: 349 us; the launch traced here: 348 us
  waiting for transfers between devices  190 us (54%)
  Pallas kernels  66.5 us (19%)
  local copies, waits for them, and re-layouts  59.6 us (17%)
  starting transfers between devices  20.4 us (6%)
  between operations  8.03 us (2%)
  other arithmetic  4.27 us (1%)
    all_to_all x2, waiting for transfers between devices, moved(): return lax.all_to_all(x, 'tm', split_axis=0, concat_axis=0, tiled=True)  169 us
    pallas_call x1, Pallas kernels, lag_images(): pl.pallas_call(lag_kernel, grid=(shots, chans // CB), in_specs=[in_spec,...  66.5 us
    unnamed x5, local copies, waits for them, and re-layouts  24 us
    ppermute x2, waiting for transfers between devices, passed_along(): return lax.ppermute(block, axis, route)  20.8 us
    rev x1, local copies, waits for them, and re-layouts, moved(): x = jnp.flip(x, axis=4)  20.8 us
    all_to_all x2, starting transfers between devices, moved(): return lax.all_to_all(x, 'tm', split_axis=0, concat_axis=0, tiled=True)  11.4 us
    ppermute x2, starting transfers between devices, passed_along(): return lax.ppermute(block, axis, route)  8.99 us
    slice x2, local copies, waits for them, and re-layouts, place_tiles(): term = jnp.where(target[s, a] == k, blocks[s, :, :, a, :], 0.0)  8.04 us
  transfers between devices with their start and end apart: 4, of which 4 were waited for; matrix products, arithmetic and copies ran while one was open for 3% of the time, Pallas kernels for 0%

profile of v1, /device:TPU:3, one launch (start us, length us, event | category | flops | bytes accessed | tf_op | source)
XLA Modules:
  0.0 348.3 jit_solution(8719745980114677380)
XLA Ops:
  0.0 11.4 %copy.11 = bf16[2,16,64,8,256]{4,1,2,0,3:T(8,128)(2,1)} copy(bf16[2,16,64,8,256]{4,3,2,1,0:T(8,128)(2,1)} %param.4) | data formatting | bytes 16777216 | tf_op args[1]
  11.4 20.8 %rev.4 = bf16[2,16,64,8,256]{4,1,2,0,3:T(8,128)(2,1)} reverse(bf16[2,16,64,8,256]{4,1,2,0,3:T(8,128)(2,1)} %copy.11), dimensions={4} | reverse | bytes 16777216 | tf_op jit(solution)/shard_map/jit(_flip)/rev | solution.py:80
  32.1 6.0 %all-to-all-start.1 = ((bf16[8,2,64,16,256]{4,3,2,1,0:T(8,128)(2,1)}), bf16[8,2,64,16,256]{4,3,2,1,0:T(8,128)(2,1)}, u32[]{:S(2)}, u32[]{:S(2)}) async-start(bf16[8,2,64,16,256]{4,3,2,1,0:T(8,128)(2,1)} %bitcast.31), calls=%async_computation.1 | async-start | bytes 16777216 | tf_op jit(solution)/shard_map/all_to_all | solution.py:82
  38.2 11.4 %copy.37 = bf16[2,16,64,8,256]{4,1,2,0,3:T(8,128)(2,1)} copy(bf16[2,16,64,8,256]{4,3,2,1,0:T(8,128)(2,1)} %param.3) | data formatting | bytes 16777216 | tf_op args[0]
  49.6 82.3 %all-to-all-done.1.r_ref = bf16[8,2,64,16,256]{4,3,2,1,0:T(8,128)(2,1)} async-done(((bf16[8,2,64,16,256]{4,3,2,1,0:T(8,128)(2,1)}), bf16[8,2,64,16,256]{4,3,2,1,0:T(8,128)(2,1)}, u32[]{:S(2)}, u32[]{:S(2)}) %all-to-all-start.1) | async-done | bytes 8388640 | tf_op jit(solution)/shard_map/all_to_all | solution.py:82
  131.9 0.0 copy-start
  131.9 5.3 %all-to-all-start = ((bf16[8,2,64,16,256]{4,3,2,1,0:T(8,128)(2,1)}), bf16[8,2,64,16,256]{4,3,2,1,0:T(8,128)(2,1)}, u32[]{:S(2)}, u32[]{:S(2)}) async-start(bf16[8,2,64,16,256]{4,3,2,1,0:T(8,128)(2,1)} %bitcast.30), calls=%async_computation | async-start | bytes 16777216 | tf_op jit(solution)/shard_map/all_to_all | solution.py:82
  137.2 0.0 copy-done
  137.2 0.1 add_subtract_fusion
  137.3 0.7 fusion.4
  143.3 86.5 %all-to-all-done.s_ref = bf16[8,2,64,16,256]{4,3,2,1,0:T(8,128)(2,1)} async-done(((bf16[8,2,64,16,256]{4,3,2,1,0:T(8,128)(2,1)}), bf16[8,2,64,16,256]{4,3,2,1,0:T(8,128)(2,1)}, u32[]{:S(2)}, u32[]{:S(2)}) %all-to-all-start) | async-done | bytes 8388640 | tf_op jit(solution)/shard_map/all_to_all | solution.py:82
  229.7 66.5 %shard_map.37 = f32[2,64,33,256]{3,2,1,0:T(8,128)} custom-call(bf16[8,2,64,16,256]{4,3,2,1,0:T(8,128)(2,1)} %all-to-all-done.s_ref, bf16[8,2,64,16,256]{4,3,2,1,0:T(8,128)(2,1)} %all-to-all-done.1.r_ref), custom_call_target="tpu_custom_call" | custom-call | tf_op jit(solution)/shard_map/pallas_call | solution.py:52
  296.3 6.7 %reshape.74 = f32[2,64,33,2,128]{4,3,2,1,0:T(2,128)} reshape(f32[2,64,33,256]{3,2,1,0:T(8,128)} %shard_map.37) | data formatting | bytes 8650752 | tf_op jit(solution)/shard_map/reshape | solution.py:64
  303.0 7.4 %fusion.3 = (f32[1,64,33,1,128]{4,3,2,1,0:T(1,128)S(1)}, f32[1,64,33,1,128]{4,3,2,1,0:T(1,128)S(1)}, f32[1,64,33,1,128]{4,3,2,1,0:T(1,128)S(1)}, f32[1,64,33,1,128]{4,3,2,1,0:T(1,128)S(1)}) fusion(f32[2,64,33,2,128]{4,3,2,1,0:T(2,128)} %reshape.74), kind=kLoop, calls=%fused_computation.9 | loop fusion | bytes 8650752 | tf_op jit(solution)/shard_map/slice | solution.py:71
  310.4 1.2 copy.25
  311.6 0.5 add_bitcast_fusion
  312.1 0.1 broadcast_in_dim.20
  312.2 2.2 fusion
  314.4 7.1 %collective-permute-start.1 = (f32[64,33,128]{2,0,1:T(8,128)S(1)}, f32[64,33,128]{2,0,1:T(8,128)S(1)}, u32[]{:S(2)}, u32[]{:S(2)}) collective-permute-start(f32[64,33,128]{2,0,1:T(8,128)S(1)} %bitcast.36), channel_id=1, source_target_pairs={{0,8},{8,16},{16,24},{24,32},{32,40},{40,48},{48,56},{56,64},{64,7... | collective-permute-start | bytes 3244040 | tf_op jit(solution)/shard_map/ppermute | solution.py:18
  321.4 1.9 collective-permute-start
  326.0 19.1 %collective-permute-done.1 = f32[64,33,128]{2,0,1:T(8,128)S(1)} collective-permute-done((f32[64,33,128]{2,0,1:T(8,128)S(1)}, f32[64,33,128]{2,0,1:T(8,128)S(1)}, u32[]{:S(2)}, u32[]{:S(2)}) %collective-permute-start.1) | collective-permute-done | bytes 1081376 | tf_op jit(solution)/shard_map/ppermute | solution.py:18
  345.1 1.7 collective-permute-done
  346.8 1.6 fusion.2
Async XLA Ops:
  32.1 99.7 %all-to-all-start.1 = ((bf16[8,2,64,16,256]{4,3,2,1,0:T(8,128)(2,1)}), bf16[8,2,64,16,256]{4,3,2,1,0:T(8,128)(2,1)}, u32[]{:S(2)}, u32[]{:S(2)}) async-start(bf16[8,2,64,16,256]{4,3,2,1,0:T(8,128)(2,1)} %bitcast.31), calls=%async_computation.1 | async-start | bytes 16777216 | tf_op jit(solution)/shard_map/all_to_all | solution.py:82
  131.9 5.4 %copy-start = (s32[2]{0:T(128)S(1)}, s32[2]{0:T(128)}, u32[]{:S(2)}) copy-start(s32[2]{0:T(128)} %param.5) | copy-start | bytes 28
  131.9 97.9 %all-to-all-start = ((bf16[8,2,64,16,256]{4,3,2,1,0:T(8,128)(2,1)}), bf16[8,2,64,16,256]{4,3,2,1,0:T(8,128)(2,1)}, u32[]{:S(2)}, u32[]{:S(2)}) async-start(bf16[8,2,64,16,256]{4,3,2,1,0:T(8,128)(2,1)} %bitcast.30), calls=%async_computation | async-start | bytes 16777216 | tf_op jit(solution)/shard_map/all_to_all | solution.py:82
  314.4 30.7 %collective-permute-start.1 = (f32[64,33,128]{2,0,1:T(8,128)S(1)}, f32[64,33,128]{2,0,1:T(8,128)S(1)}, u32[]{:S(2)}, u32[]{:S(2)}) collective-permute-start(f32[64,33,128]{2,0,1:T(8,128)S(1)} %bitcast.36), channel_id=1, source_target_pairs={{0,8},{8,16},{16,24},{24,32},{32,40},{40,48},{48,56},{56,64},{64,7... | collective-permute-start | bytes 3244040 | tf_op jit(solution)/shard_map/ppermute | solution.py:18
  321.4 25.3 %collective-permute-start = (f32[64,33,128]{2,0,1:T(8,128)S(1)}, f32[64,33,128]{2,0,1:T(8,128)S(1)}, u32[]{:S(2)}, u32[]{:S(2)}) collective-permute-start(f32[64,33,128]{2,0,1:T(8,128)S(1)} %get-tuple-element.9), channel_id=1, source_target_pairs={{8,0},{16,8},{24,16},{32,24},{40,32},{48,40},{56,48},{64,56},{72,6... | collective-permute-start | bytes 3244040 | tf_op jit(solution)/shard_map/ppermute | solution.py:18

commit v2 on v1

v2 whole, which is shorter than its diff:
```python
import functools

import jax
import jax.numpy as jnp
from jax import lax
from jax.experimental import pallas as pl
from jax.experimental.pallas import tpu as pltpu
from jax.sharding import PartitionSpec as P

LAGS = 33
TILE = 128
CB = 8
NCH = 4


def passed_along(block, axis, distance):
    devices = range(lax.axis_size(axis))
    route = [(i - distance, i) for i in devices if i - distance in devices]
    return lax.ppermute(block, axis, route)


def lag_kernel(x_ref, o_ref, band_ref):
    src, _, _, cb, t16, width = x_ref.shape
    half = (LAGS - 1) // 2
    rows = band_ref.shape[0]
    u_i = lax.broadcasted_iota(jnp.int32, (width, width), 0)
    k_i = lax.broadcasted_iota(jnp.int32, (width, width), 1)
    v_ok = (u_i - k_i + 2 * half >= 0) & (u_i - k_i + 2 * half < width)
    flip = jnp.where(u_i + k_i == width - 1, 1.0, 0.0).astype(jnp.bfloat16)
    x_i = lax.broadcasted_iota(jnp.int32, (1, width), 1)

    def one_channel(c, carry):
        s_t = x_ref[:, 0, 0, c, :, :].reshape(src * t16, width)
        r_t = x_ref[:, 1, 0, c, :, :].reshape(src * t16, width)
        r_f = jnp.dot(r_t, flip, preferred_element_type=jnp.float32).astype(jnp.bfloat16)
        g = lax.dot_general(s_t, r_f, (((0,), (0,)), ((), ())),
                            preferred_element_type=jnp.float32)
        q = pltpu.roll(g, 2 * half + 1, 1, stride=1, stride_axis=0)
        q = jnp.where(v_ok, q, 0.0)
        band_ref[...] = q[:, :TILE].T[:rows, :]
        for j in range(LAGS):
            d = half - j
            w = band_ref[2 * j:2 * j + 1, :]
            out = pltpu.roll(w, d % width, 1)
            out = jnp.where((x_i - d >= 0) & (x_i - d < width), out, 0.0)
            o_ref[0, 0, c, pl.ds(half + d, 1), :] = out[:, :TILE]
            o_ref[0, 1, c, pl.ds(half + d, 1), :] = out[:, TILE:]
        return carry

    lax.fori_loop(0, cb, one_channel, 0)


def lag_images(pair):
    n_src, _, shots, chans, t16, width = pair.shape
    cb = min(CB, chans)
    return pl.pallas_call(
        lag_kernel,
        grid=(shots, chans // cb),
        in_specs=[pl.BlockSpec((n_src, 2, 1, cb, t16, width), lambda i, j: (0, 0, i, j, 0, 0))],
        out_specs=pl.BlockSpec((1, 2, cb, LAGS, TILE), lambda i, j: (i, 0, j, 0, 0)),
        out_shape=jax.ShapeDtypeStruct((shots, 2, chans, LAGS, TILE), jnp.float32),
        scratch_shapes=[pltpu.VMEM((72, width), jnp.float32)],
    )(pair)


def place_tiles(image, first, base, slots):
    shots = image.shape[0]
    target = first[:, None] + jnp.arange(2, dtype=jnp.int32)[None, :] - base
    out = []
    for k in range(slots):
        acc = None
        for s in range(shots):
            for a in range(2):
                term = jnp.where(target[s, a] == k, image[s, a], 0.0)
                acc = term if acc is None else acc + term
        out.append(acc)
    return out


def body(source_snap, receiver_snap, start_tile):
    chans = source_snap.shape[2]
    owner = lax.axis_index("space")
    parts = []
    images = []
    for g in range(NCH):
        cs = slice(g * chans // NCH, (g + 1) * chans // NCH)
        pair = jnp.stack([source_snap[:, :, cs], receiver_snap[:, :, cs]])
        pair = jnp.transpose(pair, (4, 0, 1, 3, 2, 5))
        if g >= 2:
            pair, images[g - 2] = lax.optimization_barrier((pair, images[g - 2]))
        pair = lax.all_to_all(pair, "tm", split_axis=0, concat_axis=0, tiled=True)
        images.append(lag_images(pair))
    for image in images:
        placed = place_tiles(image, start_tile, owner - 1, 3)
        right_part = passed_along(placed[0], "space", -1)
        left_part = passed_along(placed[2], "space", 1)
        parts.append(placed[1] + right_part + left_part)
    return jnp.concatenate(parts, axis=0)[None]


def solution(mesh):
    in_specs = (P("space", "tm", None, None, None), P("space", "tm", None, None, None), P("space"))
    out_specs = P("tm", None, None, "space")
    return jax.shard_map(body, mesh=mesh, in_specs=in_specs, out_specs=out_specs, check_vma=False)
```

time: 349 us -> 312 us (0.89)
  waiting for transfers between devices: 190 us -> 117 us
  local copies, waits for them, and re-layouts: 59.6 us -> 26.8 us
  starting transfers between devices: 20.4 us -> 51.1 us
  Pallas kernels: 66.5 us -> 89 us
  other arithmetic: 4.27 us -> 17.4 us
    all_to_all x2 -> x4, waiting for transfers between devices: 169 us -> 77.6 us  [body(): pair = lax.all_to_all(pair, 'tm', split_axis=0, concat_axis=0, tiled=True)]
    pallas_call x1 -> x4, Pallas kernels: 66.5 us -> 89 us  [lag_images(): pl.pallas_call(lag_kernel, grid=(shots, chans // cb), in_specs=[pl.BlockS...]
    unnamed x5 -> x16, local copies, waits for them, and re-layouts: 24 us -> 2.06 us
    ppermute x2 -> x8, starting transfers between devices: 8.99 us -> 30.3 us  [passed_along(): return lax.ppermute(block, axis, route)]
    rev x1 -> x0, local copies, waits for them, and re-layouts: 20.8 us -> none  [moved(): x = jnp.flip(x, axis=4)]
    ppermute x2 -> x8, waiting for transfers between devices: 20.8 us -> 39.1 us  [passed_along(): return lax.ppermute(block, axis, route)]
    another operation x0 -> x4, local copies, waits for them, and re-layouts: none -> 14.9 us  [body(): pair = jnp.stack([source_snap[:, :, cs], receiver_snap[:, :, cs]])]
    transpose x0 -> x4, other arithmetic: none -> 11 us  [body(): pair = jnp.transpose(pair, (4, 0, 1, 3, 2, 5))]
  transfers between devices with their start and end apart: 4 -> 12, of which waited for: 4 -> 5; matrix products, arithmetic and copies ran while one was open for 3% -> 9% of each run, Pallas kernels for 0% -> 29%
where the time goes in v2:
time: 312 us; the launch traced here: 309 us
  waiting for transfers between devices  117 us (38%)
  Pallas kernels  89 us (29%)
  starting transfers between devices  51.1 us (16%)
  local copies, waits for them, and re-layouts  26.8 us (9%)
  other arithmetic  17.4 us (6%)
  between operations  7.95 us (3%)
    pallas_call x4, Pallas kernels, lag_images(): pl.pallas_call(lag_kernel, grid=(shots, chans // cb), in_specs=[pl.BlockS...  89 us
    all_to_all x4, waiting for transfers between devices, body(): pair = lax.all_to_all(pair, 'tm', split_axis=0, concat_axis=0, tiled=True)  77.6 us
    ppermute x8, waiting for transfers between devices, passed_along(): return lax.ppermute(block, axis, route)  39.1 us
    ppermute x8, starting transfers between devices, passed_along(): return lax.ppermute(block, axis, route)  30.3 us
    all_to_all x4, starting transfers between devices, body(): pair = lax.all_to_all(pair, 'tm', split_axis=0, concat_axis=0, tiled=True)  20.7 us
    another operation x4, local copies, waits for them, and re-layouts, body(): pair = jnp.stack([source_snap[:, :, cs], receiver_snap[:, :, cs]])  14.9 us
    transpose x4, other arithmetic, body(): pair = jnp.transpose(pair, (4, 0, 1, 3, 2, 5))  11 us
    slice x2, local copies, waits for them, and re-layouts, body(): pair = jnp.stack([source_snap[:, :, cs], receiver_snap[:, :, cs]])  8 us
  transfers between devices with their start and end apart: 12, of which 5 were waited for; matrix products, arithmetic and copies ran while one was open for 9% of the time, Pallas kernels for 29%

profile of v2, /device:TPU:3, one launch (start us, length us, event | category | flops | bytes accessed | tf_op | source)
XLA Modules:
  0.0 309.0 jit_solution(3261373542484286509)
XLA Ops:
  0.0 5.3 %fusion.4 = (bf16[2,16,16,8,256]{4,3,2,1,0:T(8,128)(2,1)S(1)}, bf16[2,16,16,8,256]{4,3,2,1,0:T(8,128)(2,1)}, bf16[2,16,16,8,256]{4,3,2,1,0:T(8,128)(2,1)}, bf16[2,16,16,8,256]{4,3,2,1,0:T(8,128)(2,1)S(1)}) fusion(bf16[2,16,64,8,256]{4,3,2,1,0:T(8,128)(2,1)} %param.3), kind=kLoop, calls=%fused_computation.30 | loop fusion | bytes 16777216 | tf_op jit(solution)/shard_map/slice | solution.py:87
  5.3 2.0 copy-done.4
  7.4 2.7 fusion.5
  10.0 2.4 copy_bitcast_fusion.4
  12.5 2.4 maximum_bitcast_fusion.1
  14.8 6.0 %all-to-all-start = ((bf16[8,2,2,16,16,256]{5,4,3,2,1,0:T(8,128)(2,1)}), bf16[8,2,2,16,16,256]{5,4,3,2,1,0:T(8,128)(2,1)}, u32[]{:S(2)}, u32[]{:S(2)}) async-start(bf16[8,2,2,16,16,256]{5,4,3,2,1,0:T(8,128)(2,1)} %maximum_bitcast_fusion.1), calls=%async_computation | async-start | bytes 8388608 | tf_op jit(solution)/shard_map/all_to_all | solution.py:91
  20.9 4.0 %copy_bitcast_fusion = (bf16[1,2,16,16,8,256]{5,2,3,1,0,4:T(8,128)(2,1)S(1)}, bf16[1,2,16,16,8,256]{5,2,3,1,0,4:T(8,128)(2,1)S(1)}) fusion(bf16[2,16,16,8,256]{4,3,2,1,0:T(8,128)(2,1)} %get-tuple-element.20, bf16[2,16,16,8,256]{4,3,2,1,0:T(8,128)(2,1)S(1)} %get-tuple-element.16), kind=kLoop, calls=%fused_computation.4 | loop fusion | bytes 8388608 | tf_op jit(solution)/shard_map/stack | solution.py:87
  24.8 2.4 maximum_bitcast_fusion.3
  27.2 42.3 %all-to-all-done.x_ref = bf16[8,2,2,16,16,256]{5,4,3,2,1,0:T(8,128)(2,1)} async-done(((bf16[8,2,2,16,16,256]{5,4,3,2,1,0:T(8,128)(2,1)}), bf16[8,2,2,16,16,256]{5,4,3,2,1,0:T(8,128)(2,1)}, u32[]{:S(2)}, u32[]{:S(2)}) %all-to-all-start) | async-done | bytes 4194336 | tf_op jit(solution)/shard_map/all_to_all | solution.py:91
  69.6 4.8 %all-to-all-start.1 = ((bf16[8,2,2,16,16,256]{5,4,3,2,1,0:T(8,128)(2,1)}), bf16[8,2,2,16,16,256]{5,4,3,2,1,0:T(8,128)(2,1)}, u32[]{:S(2)}, u32[]{:S(2)}) async-start(bf16[8,2,2,16,16,256]{5,4,3,2,1,0:T(8,128)(2,1)} %maximum_bitcast_fusion.3), calls=%async_computation.1 | async-start | bytes 8388608 | tf_op jit(solution)/shard_map/all_to_all | solution.py:91
  74.4 4.8 %copy_bitcast_fusion.3 = (bf16[1,2,16,16,8,256]{5,2,3,1,0,4:T(8,128)(2,1)S(1)}, bf16[1,2,16,16,8,256]{5,2,3,1,0,4:T(8,128)(2,1)S(1)}) fusion(bf16[2,16,16,8,256]{4,3,2,1,0:T(8,128)(2,1)} %get-tuple-element.14, bf16[2,16,16,8,256]{4,3,2,1,0:T(8,128)(2,1)} %get-tuple-element.15), kind=kLoop, calls=%fused_computation.7 | loop fusion | bytes 8388608 | tf_op jit(solution)/shard_map/stack | solution.py:87
  79.2 3.8 %copy_bitcast_fusion.2 = (bf16[1,2,16,16,8,256]{5,2,3,1,0,4:T(8,128)(2,1)}, bf16[1,2,16,16,8,256]{5,2,3,1,0,4:T(8,128)(2,1)S(1)}) fusion(bf16[2,16,16,8,256]{4,3,2,1,0:T(8,128)(2,1)S(1)} %copy-done.5, bf16[2,16,16,8,256]{4,3,2,1,0:T(8,128)(2,1)S(1)} %copy-done.6), kind=kLoop, calls=%fused_computation.6 | loop fusion | bytes 8388608 | tf_op jit(solution)/shard_map/stack | solution.py:87
  82.9 2.3 maximum_bitcast_fusion
  85.2 22.2 %shard_map.37 = f32[2,2,16,33,128]{4,3,2,1,0:T(8,128)} custom-call(bf16[8,2,2,16,16,256]{5,4,3,2,1,0:T(8,128)(2,1)} %all-to-all-done.x_ref), custom_call_target="tpu_custom_call" | custom-call | tf_op jit(solution)/shard_map/pallas_call | solution.py:56
  107.5 14.5 %all-to-all-done.1.x_ref = bf16[8,2,2,16,16,256]{5,4,3,2,1,0:T(8,128)(2,1)} async-done(((bf16[8,2,2,16,16,256]{5,4,3,2,1,0:T(8,128)(2,1)}), bf16[8,2,2,16,16,256]{5,4,3,2,1,0:T(8,128)(2,1)}, u32[]{:S(2)}, u32[]{:S(2)}) %all-to-all-start.1) | async-done | bytes 4194336 | tf_op jit(solution)/shard_map/all_to_all | solution.py:91
  121.9 4.6 %all-to-all-start.2 = ((bf16[8,2,2,16,16,256]{5,4,3,2,1,0:T(8,128)(2,1)}), bf16[8,2,2,16,16,256]{5,4,3,2,1,0:T(8,128)(2,1)}, u32[]{:S(2)}, u32[]{:S(2)}) async-start(bf16[8,2,2,16,16,256]{5,4,3,2,1,0:T(8,128)(2,1)} %maximum_bitcast_fusion), calls=%async_computation.2 | async-start | bytes 8388608 | tf_op jit(solution)/shard_map/all_to_all | solution.py:91
  126.5 4.0 %maximum_bitcast_fusion.2 = bf16[8,2,2,16,16,256]{5,4,3,2,1,0:T(8,128)(2,1)} fusion(bf16[1,2,16,16,8,256]{5,2,3,1,0,4:T(8,128)(2,1)} %get-tuple-element.33, bf16[1,2,16,16,8,256]{5,2,3,1,0,4:T(8,128)(2,1)S(1)} %get-tuple-element.35), kind=kLoop, calls=%fused_computation.2 | loop fusion | flops 2097152 | bytes 8388608 | tf_op jit(solution)/shard_map/transpose | solution.py:88
  130.5 22.3 %shard_map.38 = f32[2,2,16,33,128]{4,3,2,1,0:T(8,128)} custom-call(bf16[8,2,2,16,16,256]{5,4,3,2,1,0:T(8,128)(2,1)} %all-to-all-done.1.x_ref), custom_call_target="tpu_custom_call" | custom-call | tf_op jit(solution)/shard_map/pallas_call | solution.py:56
  152.8 20.8 %all-to-all-done.2.x_ref = bf16[8,2,2,16,16,256]{5,4,3,2,1,0:T(8,128)(2,1)} async-done(((bf16[8,2,2,16,16,256]{5,4,3,2,1,0:T(8,128)(2,1)}), bf16[8,2,2,16,16,256]{5,4,3,2,1,0:T(8,128)(2,1)}, u32[]{:S(2)}, u32[]{:S(2)}) %all-to-all-start.2) | async-done | bytes 4194336 | tf_op jit(solution)/shard_map/all_to_all | solution.py:91
  173.6 5.4 %all-to-all-start.3 = ((bf16[8,2,2,16,16,256]{5,4,3,2,1,0:T(8,128)(2,1)}), bf16[8,2,2,16,16,256]{5,4,3,2,1,0:T(8,128)(2,1)}, u32[]{:S(2)}, u32[]{:S(2)}) async-start(bf16[8,2,2,16,16,256]{5,4,3,2,1,0:T(8,128)(2,1)} %maximum_bitcast_fusion.2), calls=%async_computation.3 | async-start | bytes 8388608 | tf_op jit(solution)/shard_map/all_to_all | solution.py:91
  178.9 0.1 add_subtract_fusion
  179.0 0.7 fusion.6
  184.8 0.2 add_bitcast_fusion.7
  185.0 4.6 %collective-permute-start = (f32[16,33,128]{2,1,0:T(8,128)S(1)}, f32[16,33,128]{2,1,0:T(8,128)S(1)}, u32[]{:S(2)}, u32[]{:S(2)}) collective-permute-start(f32[16,33,128]{2,1,0:T(8,128)S(1)} %get-tuple-element.21), channel_id=1, source_target_pairs={{8,0},{16,8},{24,16},{32,24},{40,32},{48,40},{56,48},{64,56},{72,6... | collective-permute-start | bytes 811016 | tf_op jit(solution)/shard_map/ppermute | solution.py:19
  189.6 4.4 %collective-permute-start.1 = (f32[16,33,128]{2,1,0:T(8,128)S(1)}, f32[16,33,128]{2,1,0:T(8,128)S(1)}, u32[]{:S(2)}, u32[]{:S(2)}) collective-permute-start(f32[16,33,128]{2,1,0:T(8,128)S(1)} %get-tuple-element.22), channel_id=1, source_target_pairs={{0,8},{8,16},{16,24},{24,32},{32,40},{40,48},{48,56},{56,64},{64,7... | collective-permute-start | bytes 811016 | tf_op jit(solution)/shard_map/ppermute | solution.py:19
  196.6 1.0 add_bitcast_fusion.5
  197.6 1.9 collective-permute-start.2
  199.5 5.1 %collective-permute-start.3 = (f32[16,33,128]{2,1,0:T(8,128)}, f32[16,33,128]{2,1,0:T(8,128)}, u32[]{:S(2)}, u32[]{:S(2)}) collective-permute-start(f32[16,33,128]{2,1,0:T(8,128)} %get-tuple-element.24), channel_id=1, source_target_pairs={{0,8},{8,16},{16,24},{24,32},{32,40},{40,48},{48,56},{56,64},{64,7... | collective-permute-start | bytes 811016 | tf_op jit(solution)/shard_map/ppermute | solution.py:19
  204.7 34.1 %collective-permute-done = f32[16,33,128]{2,1,0:T(8,128)S(1)} collective-permute-done((f32[16,33,128]{2,1,0:T(8,128)S(1)}, f32[16,33,128]{2,1,0:T(8,128)S(1)}, u32[]{:S(2)}, u32[]{:S(2)}) %collective-permute-start) | collective-permute-done | bytes 270368 | tf_op jit(solution)/shard_map/ppermute | solution.py:19
  238.8 0.1 fusion.3
  238.9 22.2 %shard_map.39 = f32[2,2,16,33,128]{4,3,2,1,0:T(8,128)} custom-call(bf16[8,2,2,16,16,256]{5,4,3,2,1,0:T(8,128)(2,1)} %all-to-all-done.2.x_ref), custom_call_target="tpu_custom_call" | custom-call | tf_op jit(solution)/shard_map/pallas_call | solution.py:56
  261.2 2.1 add_bitcast_fusion.3
  263.3 1.9 collective-permute-start.4
  265.3 5.1 %collective-permute-start.5 = (f32[16,33,128]{2,1,0:T(8,128)S(1)}, f32[16,33,128]{2,1,0:T(8,128)S(1)}, u32[]{:S(2)}, u32[]{:S(2)}) collective-permute-start(f32[16,33,128]{2,1,0:T(8,128)S(1)} %get-tuple-element.26), channel_id=1, source_target_pairs={{0,8},{8,16},{16,24},{24,32},{32,40},{40,48},{48,56},{56,64},{64,7... | collective-permute-start | bytes 811016 | tf_op jit(solution)/shard_map/ppermute | solution.py:19
  270.4 22.3 %shard_map.40 = f32[2,2,16,33,128]{4,3,2,1,0:T(8,128)} custom-call(bf16[8,2,2,16,16,256]{5,4,3,2,1,0:T(8,128)(2,1)} %all-to-all-done.3.x_ref), custom_call_target="tpu_custom_call" | custom-call | tf_op jit(solution)/shard_map/pallas_call | solution.py:56
  292.7 1.5 add_bitcast_fusion.1
  294.2 1.9 collective-permute-start.6
  296.2 0.0 collective-permute-done.2
  296.2 5.3 %collective-permute-start.7 = (f32[16,33,128]{2,1,0:T(8,128)S(1)}, f32[16,33,128]{2,1,0:T(8,128)S(1)}, u32[]{:S(2)}, u32[]{:S(2)}) collective-permute-start(f32[16,33,128]{2,1,0:T(8,128)S(1)} %get-tuple-element.28), channel_id=1, source_target_pairs={{0,8},{8,16},{16,24},{24,32},{32,40},{40,48},{48,56},{56,64},{64,7... | collective-permute-start | bytes 811016 | tf_op jit(solution)/shard_map/ppermute | solution.py:19
  301.5 0.0 collective-permute-done.3
  301.5 1.1 fusion.2
  302.6 0.0 collective-permute-done.5
  302.6 0.1 fusion.1
  302.7 4.9 %collective-permute-done.6 = f32[16,33,128]{2,1,0:T(8,128)S(1)} collective-permute-done((f32[16,33,128]{2,1,0:T(8,128)S(1)}, f32[16,33,128]{2,1,0:T(8,128)S(1)}, u32[]{:S(2)}, u32[]{:S(2)}) %collective-permute-start.6) | collective-permute-done | bytes 270368 | tf_op jit(solution)/shard_map/ppermute | solution.py:19
  307.6 0.0 collective-permute-done.7
  307.6 0.1 fusion
  307.8 0.1 maximum_bitcast_fusion.4
  307.8 1.2 copy.12
  (18 shorter events, 0.0 us)
Async XLA Ops:
  0.0 7.4 %copy-start.4 = (bf16[2,16,64,8,256]{4,3,2,1,0:T(8,128)(2,1)S(1)}, bf16[2,16,64,8,256]{4,3,2,1,0:T(8,128)(2,1)}, u32[]{:S(2)}) copy-start(bf16[2,16,64,8,256]{4,3,2,1,0:T(8,128)(2,1)} %param.4) | copy-start | bytes 25165828
  14.8 54.7 %all-to-all-start = ((bf16[8,2,2,16,16,256]{5,4,3,2,1,0:T(8,128)(2,1)}), bf16[8,2,2,16,16,256]{5,4,3,2,1,0:T(8,128)(2,1)}, u32[]{:S(2)}, u32[]{:S(2)}) async-start(bf16[8,2,2,16,16,256]{5,4,3,2,1,0:T(8,128)(2,1)} %maximum_bitcast_fusion.1), calls=%async_computation | async-start | bytes 8388608 | tf_op jit(solution)/shard_map/all_to_all | solution.py:91
  69.6 52.4 %all-to-all-start.1 = ((bf16[8,2,2,16,16,256]{5,4,3,2,1,0:T(8,128)(2,1)}), bf16[8,2,2,16,16,256]{5,4,3,2,1,0:T(8,128)(2,1)}, u32[]{:S(2)}, u32[]{:S(2)}) async-start(bf16[8,2,2,16,16,256]{5,4,3,2,1,0:T(8,128)(2,1)} %maximum_bitcast_fusion.3), calls=%async_computation.1 | async-start | bytes 8388608 | tf_op jit(solution)/shard_map/all_to_all | solution.py:91
  74.4 4.8 %copy-start.5 = (bf16[2,16,16,8,256]{4,3,2,1,0:T(8,128)(2,1)S(1)}, bf16[2,16,16,8,256]{4,3,2,1,0:T(8,128)(2,1)}, u32[]{:S(2)}) copy-start(bf16[2,16,16,8,256]{4,3,2,1,0:T(8,128)(2,1)} %get-tuple-element.18) | copy-start | bytes 6291460
  74.4 4.8 %copy-start.6 = (bf16[2,16,16,8,256]{4,3,2,1,0:T(8,128)(2,1)S(1)}, bf16[2,16,16,8,256]{4,3,2,1,0:T(8,128)(2,1)}, u32[]{:S(2)}) copy-start(bf16[2,16,16,8,256]{4,3,2,1,0:T(8,128)(2,1)} %get-tuple-element.19) | copy-start | bytes 6291460
  121.9 51.6 %all-to-all-start.2 = ((bf16[8,2,2,16,16,256]{5,4,3,2,1,0:T(8,128)(2,1)}), bf16[8,2,2,16,16,256]{5,4,3,2,1,0:T(8,128)(2,1)}, u32[]{:S(2)}, u32[]{:S(2)}) async-start(bf16[8,2,2,16,16,256]{5,4,3,2,1,0:T(8,128)(2,1)} %maximum_bitcast_fusion), calls=%async_computation.2 | async-start | bytes 8388608 | tf_op jit(solution)/shard_map/all_to_all | solution.py:91
  152.7 26.2 %copy-start.7 = (s32[2]{0:T(128)S(1)}, s32[2]{0:T(128)}, u32[]{:S(2)}) copy-start(s32[2]{0:T(128)} %param.5) | copy-start | bytes 28
  152.7 32.1 %copy-start.1 = (f32[2,2,16,33,128]{4,3,2,1,0:T(8,128)S(1)}, f32[2,2,16,33,128]{4,3,2,1,0:T(8,128)}, u32[]{:S(2)}) copy-start(f32[2,2,16,33,128]{4,3,2,1,0:T(8,128)} %shard_map.37) | copy-start | bytes 3244036
  173.6 96.8 %all-to-all-start.3 = ((bf16[8,2,2,16,16,256]{5,4,3,2,1,0:T(8,128)(2,1)}), bf16[8,2,2,16,16,256]{5,4,3,2,1,0:T(8,128)(2,1)}, u32[]{:S(2)}, u32[]{:S(2)}) async-start(bf16[8,2,2,16,16,256]{5,4,3,2,1,0:T(8,128)(2,1)} %maximum_bitcast_fusion.2), calls=%async_computation.3 | async-start | bytes 8388608 | tf_op jit(solution)/shard_map/all_to_all | solution.py:91
  178.9 17.7 %copy-start = (f32[2,2,16,33,128]{4,3,2,1,0:T(8,128)S(1)}, f32[2,2,16,33,128]{4,3,2,1,0:T(8,128)}, u32[]{:S(2)}) copy-start(f32[2,2,16,33,128]{4,3,2,1,0:T(8,128)} %shard_map.38) | copy-start | bytes 3244036
  185.0 53.9 %collective-permute-start = (f32[16,33,128]{2,1,0:T(8,128)S(1)}, f32[16,33,128]{2,1,0:T(8,128)S(1)}, u32[]{:S(2)}, u32[]{:S(2)}) collective-permute-start(f32[16,33,128]{2,1,0:T(8,128)S(1)} %get-tuple-element.21), channel_id=1, source_target_pairs={{8,0},{16,8},{24,16},{32,24},{40,32},{48,40},{56,48},{64,56},{72,6... | collective-permute-start | bytes 811016 | tf_op jit(solution)/shard_map/ppermute | solution.py:19
  189.6 49.2 %collective-permute-start.1 = (f32[16,33,128]{2,1,0:T(8,128)S(1)}, f32[16,33,128]{2,1,0:T(8,128)S(1)}, u32[]{:S(2)}, u32[]{:S(2)}) collective-permute-start(f32[16,33,128]{2,1,0:T(8,128)S(1)} %get-tuple-element.22), channel_id=1, source_target_pairs={{0,8},{8,16},{16,24},{24,32},{32,40},{40,48},{48,56},{56,64},{64,7... | collective-permute-start | bytes 811016 | tf_op jit(solution)/shard_map/ppermute | solution.py:19
  197.6 98.5 %collective-permute-start.2 = (f32[16,33,128]{2,1,0:T(8,128)}, f32[16,33,128]{2,1,0:T(8,128)S(1)}, u32[]{:S(2)}, u32[]{:S(2)}) collective-permute-start(f32[16,33,128]{2,1,0:T(8,128)} %get-tuple-element.23), channel_id=1, source_target_pairs={{8,0},{16,8},{24,16},{32,24},{40,32},{48,40},{56,48},{64,56},{72,6... | collective-permute-start | bytes 811016 | tf_op jit(solution)/shard_map/ppermute | solution.py:19
  199.5 101.9 %collective-permute-start.3 = (f32[16,33,128]{2,1,0:T(8,128)}, f32[16,33,128]{2,1,0:T(8,128)}, u32[]{:S(2)}, u32[]{:S(2)}) collective-permute-start(f32[16,33,128]{2,1,0:T(8,128)} %get-tuple-element.24), channel_id=1, source_target_pairs={{0,8},{8,16},{16,24},{24,32},{32,40},{40,48},{48,56},{56,64},{64,7... | collective-permute-start | bytes 811016 | tf_op jit(solution)/shard_map/ppermute | solution.py:19
  263.3 39.2 %collective-permute-start.4 = (f32[16,33,128]{2,1,0:T(8,128)}, f32[16,33,128]{2,1,0:T(8,128)S(1)}, u32[]{:S(2)}, u32[]{:S(2)}) collective-permute-start(f32[16,33,128]{2,1,0:T(8,128)} %get-tuple-element.25), channel_id=1, source_target_pairs={{8,0},{16,8},{24,16},{32,24},{40,32},{48,40},{56,48},{64,56},{72,6... | collective-permute-start | bytes 811016 | tf_op jit(solution)/shard_map/ppermute | solution.py:19
  265.3 37.3 %collective-permute-start.5 = (f32[16,33,128]{2,1,0:T(8,128)S(1)}, f32[16,33,128]{2,1,0:T(8,128)S(1)}, u32[]{:S(2)}, u32[]{:S(2)}) collective-permute-start(f32[16,33,128]{2,1,0:T(8,128)S(1)} %get-tuple-element.26), channel_id=1, source_target_pairs={{0,8},{8,16},{16,24},{24,32},{32,40},{40,48},{48,56},{56,64},{64,7... | collective-permute-start | bytes 811016 | tf_op jit(solution)/shard_map/ppermute | solution.py:19
  292.7 9.9 %copy-start.2 = (f32[2,2,16,33,128]{4,3,2,1,0:T(8,128)S(1)}, f32[2,2,16,33,128]{4,3,2,1,0:T(8,128)}, u32[]{:S(2)}) copy-start(f32[2,2,16,33,128]{4,3,2,1,0:T(8,128)} %shard_map.39) | copy-start | bytes 3244036
  294.2 13.4 %collective-permute-start.6 = (f32[16,33,128]{2,1,0:T(8,128)S(1)}, f32[16,33,128]{2,1,0:T(8,128)S(1)}, u32[]{:S(2)}, u32[]{:S(2)}) collective-permute-start(f32[16,33,128]{2,1,0:T(8,128)S(1)} %get-tuple-element.27), channel_id=1, source_target_pairs={{8,0},{16,8},{24,16},{32,24},{40,32},{48,40},{56,48},{64,56},{72,6... | collective-permute-start | bytes 811016 | tf_op jit(solution)/shard_map/ppermute | solution.py:19
  296.2 11.5 %copy-start.3 = (f32[2,2,16,33,128]{4,3,2,1,0:T(8,128)S(1)}, f32[2,2,16,33,128]{4,3,2,1,0:T(8,128)}, u32[]{:S(2)}) copy-start(f32[2,2,16,33,128]{4,3,2,1,0:T(8,128)} %shard_map.40) | copy-start | bytes 3244036
  296.2 11.5 %collective-permute-start.7 = (f32[16,33,128]{2,1,0:T(8,128)S(1)}, f32[16,33,128]{2,1,0:T(8,128)S(1)}, u32[]{:S(2)}, u32[]{:S(2)}) collective-permute-start(f32[16,33,128]{2,1,0:T(8,128)S(1)} %get-tuple-element.28), channel_id=1, source_target_pairs={{0,8},{8,16},{16,24},{24,32},{32,40},{40,48},{48,56},{56,64},{64,7... | collective-permute-start | bytes 811016 | tf_op jit(solution)/shard_map/ppermute | solution.py:19

commit v3 on v2

--- a/solution.py
+++ b/solution.py
@@ -10,7 +10,7 @@
 LAGS = 33
 TILE = 128
 CB = 8
-NCH = 4
+CHUNKS = (48, 16)
 
 
 def passed_along(block, axis, distance):
@@ -26,14 +26,12 @@
     u_i = lax.broadcasted_iota(jnp.int32, (width, width), 0)
     k_i = lax.broadcasted_iota(jnp.int32, (width, width), 1)
     v_ok = (u_i - k_i + 2 * half >= 0) & (u_i - k_i + 2 * half < width)
-    flip = jnp.where(u_i + k_i == width - 1, 1.0, 0.0).astype(jnp.bfloat16)
     x_i = lax.broadcasted_iota(jnp.int32, (1, width), 1)
 
     def one_channel(c, carry):
         s_t = x_ref[:, 0, 0, c, :, :].reshape(src * t16, width)
         r_t = x_ref[:, 1, 0, c, :, :].reshape(src * t16, width)
-        r_f = jnp.dot(r_t, flip, preferred_element_type=jnp.float32).astype(jnp.bfloat16)
-        g = lax.dot_general(s_t, r_f, (((0,), (0,)), ((), ())),
+        g = lax.dot_general(s_t, r_t, (((0,), (0,)), ((), ())),
                             preferred_element_type=jnp.float32)
         q = pltpu.roll(g, 2 * half + 1, 1, stride=1, stride_axis=0)
         q = jnp.where(v_ok, q, 0.0)
@@ -77,25 +75,37 @@
     return out
 
 
+def flipped(x):
+    width = x.shape[-1]
+    i = jnp.arange(width, dtype=jnp.int32)
+    anti = (i[:, None] + i[None, :] == width - 1).astype(x.dtype)
+    return jnp.dot(x, anti, preferred_element_type=jnp.float32).astype(x.dtype)
+
+
 def body(source_snap, receiver_snap, start_tile):
-    chans = source_snap.shape[2]
     owner = lax.axis_index("space")
-    parts = []
+    receiver_snap = flipped(receiver_snap)
     images = []
-    for g in range(NCH):
-        cs = slice(g * chans // NCH, (g + 1) * chans // NCH)
+    received = []
+    first = 0
+    for g, size in enumerate(CHUNKS):
+        cs = slice(first, first + size)
+        first += size
         pair = jnp.stack([source_snap[:, :, cs], receiver_snap[:, :, cs]])
         pair = jnp.transpose(pair, (4, 0, 1, 3, 2, 5))
+        if g >= 1:
+            pair, received[g - 1] = lax.optimization_barrier((pair, received[g - 1]))
         if g >= 2:
             pair, images[g - 2] = lax.optimization_barrier((pair, images[g - 2]))
-        pair = lax.all_to_all(pair, "tm", split_axis=0, concat_axis=0, tiled=True)
-        images.append(lag_images(pair))
-    for image in images:
-        placed = place_tiles(image, start_tile, owner - 1, 3)
-        right_part = passed_along(placed[0], "space", -1)
-        left_part = passed_along(placed[2], "space", 1)
-        parts.append(placed[1] + right_part + left_part)
-    return jnp.concatenate(parts, axis=0)[None]
+        received.append(lax.all_to_all(pair, "tm", split_axis=0, concat_axis=0, tiled=True))
+        if g >= 1:
+            images.append(lag_images(received[g - 1]))
+    images.append(lag_images(received[-1]))
+    placed = [place_tiles(image, start_tile, owner - 1, 3) for image in images]
+    slots = [jnp.concatenate([p[k] for p in placed], axis=0) for k in range(3)]
+    right_part = passed_along(slots[0], "space", -1)
+    left_part = passed_along(slots[2], "space", 1)
+    return (slots[1] + right_part + left_part)[None]
 
 
 def solution(mesh):

time: 312 us -> 295 us (0.946)
  waiting for transfers between devices: 117 us -> 152 us
  starting transfers between devices: 51.1 us -> 18.5 us
  Pallas kernels: 89 us -> 68.1 us
  matrix products: 0 us -> 15.9 us
  other arithmetic: 17.4 us -> 9.34 us
  local copies, waits for them, and re-layouts: 26.8 us -> 22 us
    all_to_all x4 -> x2, waiting for transfers between devices: 77.6 us -> 133 us  [body(): lax.all_to_all(pair, 'tm', split_axis=0, concat_axis=0, tiled=True)]
    ppermute x8 -> x2, starting transfers between devices: 30.3 us -> 7.84 us  [passed_along(): return lax.ppermute(block, axis, route)]
    pallas_call x4 -> x2, Pallas kernels: 89 us -> 68.1 us  [lag_images(): pl.pallas_call(lag_kernel, grid=(shots, chans // cb), in_specs=[pl.BlockS...]
    ppermute x8 -> x2, waiting for transfers between devices: 39.1 us -> 18.9 us  [passed_along(): return lax.ppermute(block, axis, route)]
    dot_general x0 -> x1, matrix products: none -> 15.9 us  [flipped(): return jnp.dot(x, anti, preferred_element_type=jnp.float32).astype(x.dtype)]
    all_to_all x4 -> x2, starting transfers between devices: 20.7 us -> 10.6 us  [body(): lax.all_to_all(pair, 'tm', split_axis=0, concat_axis=0, tiled=True)]
    transpose x4 -> x2, other arithmetic: 11 us -> 3.6 us  [body(): pair = jnp.transpose(pair, (4, 0, 1, 3, 2, 5))]
    another operation x4 -> x2, local copies, waits for them, and re-layouts: 14.9 us -> 8.91 us  [body(): pair = jnp.stack([source_snap[:, :, cs], receiver_snap[:, :, cs]])]
  transfers between devices with their start and end apart: 12 -> 4, of which waited for: 5 -> 3; matrix products, arithmetic and copies ran while one was open for 9% -> 3% of each run, Pallas kernels for 29% -> 17%
where the time goes in v3:
time: 295 us; the launch traced here: 294 us
  waiting for transfers between devices  152 us (52%)
  Pallas kernels  68.1 us (23%)
  local copies, waits for them, and re-layouts  22 us (7%)
  starting transfers between devices  18.5 us (6%)
  matrix products  15.9 us (5%)
  other arithmetic  9.34 us (3%)
  between operations  7.87 us (3%)
    all_to_all x2, waiting for transfers between devices, body(): lax.all_to_all(pair, 'tm', split_axis=0, concat_axis=0, tiled=True)  133 us
    pallas_call x2, Pallas kernels, lag_images(): pl.pallas_call(lag_kernel, grid=(shots, chans // cb), in_specs=[pl.BlockS...  68.1 us
    ppermute x2, waiting for transfers between devices, passed_along(): return lax.ppermute(block, axis, route)  18.9 us
    dot_general x1, matrix products, flipped(): return jnp.dot(x, anti, preferred_element_type=jnp.float32).astype(x.dtype)  15.9 us
    all_to_all x2, starting transfers between devices, body(): lax.all_to_all(pair, 'tm', split_axis=0, concat_axis=0, tiled=True)  10.6 us
    another operation x2, local copies, waits for them, and re-layouts, body(): pair = jnp.stack([source_snap[:, :, cs], receiver_snap[:, :, cs]])  8.91 us
    ppermute x2, starting transfers between devices, passed_along(): return lax.ppermute(block, axis, route)  7.84 us
  transfers between devices with their start and end apart: 4, of which 3 were waited for; matrix products, arithmetic and copies ran while one was open for 3% of the time, Pallas kernels for 17%

profile of v3, /device:TPU:3, one launch (start us, length us, event | category | flops | bytes accessed | tf_op | source)
XLA Modules:
  0.0 293.6 jit_solution(9900462288509803811)
XLA Ops:
  0.0 15.9 %convert_bitcast_fusion = bf16[2,16,64,8,256]{4,1,2,0,3:T(8,128)(2,1)} fusion(bf16[2,16,64,8,256]{4,3,2,1,0:T(8,128)(2,1)} %param.4), kind=kOutput, calls=%fused_computation.3 | convolution fusion | flops 2151809024 | bytes 16777216 | tf_op jit(solution)/shard_map/dot_general | solution.py:82
  15.9 0.0 slice-start
  15.9 2.8 slice-done
  18.7 6.0 %slice_bitcast_fusion = (bf16[1,2,16,48,8,256]{5,2,3,1,4,0:T(8,128)(2,1)S(1)}, bf16[1,2,16,48,8,256]{5,2,3,1,4,0:T(8,128)(2,1)S(1)}) fusion(bf16[2,16,64,8,256]{4,1,2,0,3:T(8,128)(2,1)} %convert_bitcast_fusion, bf16[2,16,48,8,256]{4,3,2,1,0:T(8,128)(2,1)S(1)} %slice-done), kind=kLoop, calls=%fused_computation.4 | loop fusion | bytes 25165824 | tf_op jit(solution)/shard_map/stack | solution.py:94
  24.6 1.3 maximum_bitcast_fusion
  25.9 5.4 %copy.14 = bf16[8,2,2,48,16,256]{5,4,3,2,1,0:T(8,128)(2,1)} copy(bf16[8,2,2,48,16,256]{5,4,3,2,0,1:T(8,128)(2,1)S(1)} %maximum_bitcast_fusion) | data formatting | bytes 25165824 | tf_op jit(solution)/shard_map/transpose | solution.py:95
  31.3 6.0 %all-to-all-start = ((bf16[8,2,2,48,16,256]{5,4,3,2,1,0:T(8,128)(2,1)}), bf16[8,2,2,48,16,256]{5,4,3,2,1,0:T(8,128)(2,1)}, u32[]{:S(2)}, u32[]{:S(2)}) async-start(bf16[8,2,2,48,16,256]{5,4,3,2,1,0:T(8,128)(2,1)} %copy.14), calls=%async_computation | async-start | bytes 25165824 | tf_op jit(solution)/shard_map/all_to_all | solution.py:100
  37.3 0.0 slice-start.1
  37.3 1.6 slice-done.1
  38.9 2.9 %slice_bitcast_fusion.1 = (bf16[1,2,16,16,8,256]{5,2,3,1,0,4:T(8,128)(2,1)S(1)}, bf16[1,2,16,16,8,256]{5,2,3,1,0,4:T(8,128)(2,1)S(1)}) fusion(bf16[2,16,64,8,256]{4,1,2,0,3:T(8,128)(2,1)} %convert_bitcast_fusion, bf16[2,16,16,8,256]{4,3,2,1,0:T(8,128)(2,1)S(1)} %slice-done.1), kind=kLoop, calls=%fused_computation.7 | loop fusion | bytes 8388608 | tf_op jit(solution)/shard_map/stack | solution.py:94
  41.9 2.3 maximum_bitcast_fusion.1
  44.2 0.0 copy-start.2
  44.2 133.0 %all-to-all-done.x_ref = bf16[8,2,2,48,16,256]{5,4,3,2,1,0:T(8,128)(2,1)} async-done(((bf16[8,2,2,48,16,256]{5,4,3,2,1,0:T(8,128)(2,1)}), bf16[8,2,2,48,16,256]{5,4,3,2,1,0:T(8,128)(2,1)}, u32[]{:S(2)}, u32[]{:S(2)}) %all-to-all-start) | async-done | bytes 12582944 | tf_op jit(solution)/shard_map/all_to_all | solution.py:100
  177.2 4.6 %all-to-all-start.1 = ((bf16[8,2,2,16,16,256]{5,4,3,2,1,0:T(8,128)(2,1)}), bf16[8,2,2,16,16,256]{5,4,3,2,1,0:T(8,128)(2,1)}, u32[]{:S(2)}, u32[]{:S(2)}) async-start(bf16[8,2,2,16,16,256]{5,4,3,2,1,0:T(8,128)(2,1)} %maximum_bitcast_fusion.1), calls=%async_computation.1 | async-start | bytes 8388608 | tf_op jit(solution)/shard_map/all_to_all | solution.py:100
  181.8 0.0 copy-done.2
  181.8 0.1 add_subtract_fusion
  181.9 0.7 fusion.10
  187.7 50.1 %shard_map.37 = f32[2,2,48,33,128]{4,3,2,1,0:T(8,128)} custom-call(bf16[8,2,2,48,16,256]{5,4,3,2,1,0:T(8,128)(2,1)} %all-to-all-done.x_ref), custom_call_target="tpu_custom_call" | custom-call | tf_op jit(solution)/shard_map/pallas_call | solution.py:54
  237.9 2.5 add_bitcast_fusion.1
  240.4 0.0 all-to-all-done.1.x_ref
  240.4 18.0 %shard_map.38 = f32[2,2,16,33,128]{4,3,2,1,0:T(8,128)} custom-call(bf16[8,2,2,16,16,256]{5,4,3,2,1,0:T(8,128)(2,1)} %all-to-all-done.1.x_ref), custom_call_target="tpu_custom_call" | custom-call | tf_op jit(solution)/shard_map/pallas_call | solution.py:54
  258.4 1.4 add_bitcast_fusion.4
  259.8 0.1 pad_maximum_fusion.1
  259.9 0.2 copy.17
  260.2 5.7 %collective-permute-start.1 = (f32[64,33,128]{2,0,1:T(8,128)S(1)}, f32[64,33,128]{2,0,1:T(8,128)S(1)}, u32[]{:S(2)}, u32[]{:S(2)}) collective-permute-start(f32[64,33,128]{2,0,1:T(8,128)S(1)} %copy.17), channel_id=1, source_target_pairs={{0,8},{8,16},{16,24},{24,32},{32,40},{40,48},{48,56},{56,64},{64,7... | collective-permute-start | bytes 3244040 | tf_op jit(solution)/shard_map/ppermute | solution.py:19
  265.8 0.0 copy-start
  265.8 0.1 pad_maximum_fusion
  265.9 0.2 copy.15
  266.1 2.2 collective-permute-start
  270.9 0.0 copy-done
  270.9 0.0 copy-start.1
  270.9 0.2 add_bitcast_fusion.2
  271.2 1.1 copy-done.1
  272.2 0.1 add_bitcast_fusion.5
  272.3 17.2 %collective-permute-done.1 = f32[64,33,128]{2,0,1:T(8,128)S(1)} collective-permute-done((f32[64,33,128]{2,0,1:T(8,128)S(1)}, f32[64,33,128]{2,0,1:T(8,128)S(1)}, u32[]{:S(2)}, u32[]{:S(2)}) %collective-permute-start.1) | collective-permute-done | bytes 1081376 | tf_op jit(solution)/shard_map/ppermute | solution.py:19
  289.5 1.7 collective-permute-done
  291.2 1.2 fusion.5
  292.4 1.2 copy.19
Async XLA Ops:
  15.9 2.8 slice-start
  31.3 145.9 %all-to-all-start = ((bf16[8,2,2,48,16,256]{5,4,3,2,1,0:T(8,128)(2,1)}), bf16[8,2,2,48,16,256]{5,4,3,2,1,0:T(8,128)(2,1)}, u32[]{:S(2)}, u32[]{:S(2)}) async-start(bf16[8,2,2,48,16,256]{5,4,3,2,1,0:T(8,128)(2,1)} %copy.14), calls=%async_computation | async-start | bytes 25165824 | tf_op jit(solution)/shard_map/all_to_all | solution.py:100
  37.3 1.6 slice-start.1
  44.2 137.6 %copy-start.2 = (s32[2]{0:T(128)S(1)}, s32[2]{0:T(128)}, u32[]{:S(2)}) copy-start(s32[2]{0:T(128)} %param.5) | copy-start | bytes 28
  177.2 63.2 %all-to-all-start.1 = ((bf16[8,2,2,16,16,256]{5,4,3,2,1,0:T(8,128)(2,1)}), bf16[8,2,2,16,16,256]{5,4,3,2,1,0:T(8,128)(2,1)}, u32[]{:S(2)}, u32[]{:S(2)}) async-start(bf16[8,2,2,16,16,256]{5,4,3,2,1,0:T(8,128)(2,1)} %maximum_bitcast_fusion.1), calls=%async_computation.1 | async-start | bytes 8388608 | tf_op jit(solution)/shard_map/all_to_all | solution.py:100
  260.2 29.3 %collective-permute-start.1 = (f32[64,33,128]{2,0,1:T(8,128)S(1)}, f32[64,33,128]{2,0,1:T(8,128)S(1)}, u32[]{:S(2)}, u32[]{:S(2)}) collective-permute-start(f32[64,33,128]{2,0,1:T(8,128)S(1)} %copy.17), channel_id=1, source_target_pairs={{0,8},{8,16},{16,24},{24,32},{32,40},{40,48},{48,56},{56,64},{64,7... | collective-permute-start | bytes 3244040 | tf_op jit(solution)/shard_map/ppermute | solution.py:19
  265.8 5.1 %copy-start = (f32[2,2,48,33,128]{4,3,2,1,0:T(8,128)S(1)}, f32[2,2,48,33,128]{4,3,2,1,0:T(8,128)}, u32[]{:S(2)}) copy-start(f32[2,2,48,33,128]{4,3,2,1,0:T(8,128)} %shard_map.37) | copy-start | bytes 9732100
  266.1 25.0 %collective-permute-start = (f32[64,33,128]{2,0,1:T(8,128)S(1)}, f32[64,33,128]{2,0,1:T(8,128)S(1)}, u32[]{:S(2)}, u32[]{:S(2)}) collective-permute-start(f32[64,33,128]{2,0,1:T(8,128)S(1)} %copy.15), channel_id=1, source_target_pairs={{8,0},{16,8},{24,16},{32,24},{40,32},{48,40},{56,48},{64,56},{72,6... | collective-permute-start | bytes 3244040 | tf_op jit(solution)/shard_map/ppermute | solution.py:19
  270.9 1.3 copy-start.1

commit v4 on v3

--- a/solution.py
+++ b/solution.py
@@ -27,10 +27,16 @@
     k_i = lax.broadcasted_iota(jnp.int32, (width, width), 1)
     v_ok = (u_i - k_i + 2 * half >= 0) & (u_i - k_i + 2 * half < width)
     x_i = lax.broadcasted_iota(jnp.int32, (1, width), 1)
+    a_i = lax.broadcasted_iota(jnp.int32, (TILE, TILE), 0)
+    b_i = lax.broadcasted_iota(jnp.int32, (TILE, TILE), 1)
+    anti = jnp.where(a_i + b_i == TILE - 1, 1.0, 0.0).astype(jnp.bfloat16)
 
     def one_channel(c, carry):
         s_t = x_ref[:, 0, 0, c, :, :].reshape(src * t16, width)
         r_t = x_ref[:, 1, 0, c, :, :].reshape(src * t16, width)
+        swapped = jnp.concatenate([r_t[:, TILE:], r_t[:, :TILE]], axis=0)
+        rev = jnp.dot(swapped, anti, preferred_element_type=jnp.float32).astype(jnp.bfloat16)
+        r_t = jnp.concatenate([rev[:src * t16], rev[src * t16:]], axis=1)
         g = lax.dot_general(s_t, r_t, (((0,), (0,)), ((), ())),
                             preferred_element_type=jnp.float32)
         q = pltpu.roll(g, 2 * half + 1, 1, stride=1, stride_axis=0)
@@ -84,7 +90,6 @@
 
 def body(source_snap, receiver_snap, start_tile):
     owner = lax.axis_index("space")
-    receiver_snap = flipped(receiver_snap)
     images = []
     received = []
     first = 0

time: 295 us -> 294 us (level)
  matrix products: 15.9 us -> 0 us
  Pallas kernels: 68.1 us -> 83.3 us
  other arithmetic: 9.34 us -> 13.3 us
    dot_general x1 -> x0, matrix products: 15.9 us -> none  [flipped(): return jnp.dot(x, anti, preferred_element_type=jnp.float32).astype(x.dtype)]
    pallas_call x2, Pallas kernels: 68.1 us -> 83.3 us  [lag_images(): pl.pallas_call(lag_kernel, grid=(shots, chans // cb), in_specs=[pl.BlockS...]
    transpose x1 -> x0, local copies, waits for them, and re-layouts: 5.37 us -> none  [body(): pair = jnp.transpose(pair, (4, 0, 1, 3, 2, 5))]
    transpose x2, other arithmetic: 3.6 us -> 7.59 us  [body(): pair = jnp.transpose(pair, (4, 0, 1, 3, 2, 5))]
    slice x4 -> x8, local copies, waits for them, and re-layouts: 4.37 us -> 6.82 us  [body(): pair = jnp.stack([source_snap[:, :, cs], receiver_snap[:, :, cs]])]
  transfers between devices with their start and end apart: 4 -> 4, of which waited for: 3 -> 2; matrix products, arithmetic and copies ran while one was open for 3% -> 3% of each run, Pallas kernels for 17% -> 21%
where the time goes in v4:
time: 294 us; the launch traced here: 293 us
  waiting for transfers between devices  150 us (51%)
  Pallas kernels  83.3 us (28%)
  local copies, waits for them, and re-layouts  19.7 us (7%)
  starting transfers between devices  18.7 us (6%)
  other arithmetic  13.3 us (5%)
  between operations  7.64 us (3%)
    all_to_all x2, waiting for transfers between devices, body(): lax.all_to_all(pair, 'tm', split_axis=0, concat_axis=0, tiled=True)  133 us
    pallas_call x2, Pallas kernels, lag_images(): pl.pallas_call(lag_kernel, grid=(shots, chans // cb), in_specs=[pl.BlockS...  83.3 us
    ppermute x2, waiting for transfers between devices, passed_along(): return lax.ppermute(block, axis, route)  18 us
    all_to_all x2, starting transfers between devices, body(): lax.all_to_all(pair, 'tm', split_axis=0, concat_axis=0, tiled=True)  10.7 us
    another operation x2, local copies, waits for them, and re-layouts, body(): pair = jnp.stack([source_snap[:, :, cs], receiver_snap[:, :, cs]])  9.62 us
    ppermute x2, starting transfers between devices, passed_along(): return lax.ppermute(block, axis, route)  8.03 us
    transpose x2, other arithmetic, body(): pair = jnp.transpose(pair, (4, 0, 1, 3, 2, 5))  7.59 us
    slice x8, local copies, waits for them, and re-layouts, body(): pair = jnp.stack([source_snap[:, :, cs], receiver_snap[:, :, cs]])  6.82 us
  transfers between devices with their start and end apart: 4, of which 2 were waited for; matrix products, arithmetic and copies ran while one was open for 3% of the time, Pallas kernels for 21%

profile of v4, /device:TPU:3, one launch (start us, length us, event | category | flops | bytes accessed | tf_op | source)
XLA Modules:
  0.0 293.2 jit_solution(2760021760631443910)
XLA Ops:
  0.0 0.0 slice-start
  0.0 0.0 slice-start.2
  0.0 2.8 slice-done
  2.8 1.8 slice-done.2
  4.6 7.2 %copy_bitcast_fusion = (bf16[1,2,16,48,8,256]{5,2,3,1,0,4:T(8,128)(2,1)S(1)}, bf16[1,2,16,48,8,256]{5,2,3,1,0,4:T(8,128)(2,1)S(1)}) fusion(bf16[2,16,48,8,256]{4,3,2,1,0:T(8,128)(2,1)S(1)} %slice-done.2, bf16[2,16,48,8,256]{4,3,2,1,0:T(8,128)(2,1)S(1)} %slice-done), kind=kLoop, calls=%fused_computation.1 | loop fusion | bytes 25165824 | tf_op jit(solution)/shard_map/stack | solution.py:99
  11.8 5.3 %maximum_bitcast_fusion = bf16[8,2,2,48,16,256]{5,4,3,2,1,0:T(8,128)(2,1)} fusion(bf16[1,2,16,48,8,256]{5,2,3,1,0,4:T(8,128)(2,1)S(1)} %get-tuple-element.19, bf16[1,2,16,48,8,256]{5,2,3,1,0,4:T(8,128)(2,1)S(1)} %get-tuple-element.20), kind=kLoop, calls=%fused_computation | loop fusion | flops 6291456 | bytes 25165824 | tf_op jit(solution)/shard_map/transpose | solution.py:100
  17.1 6.0 %all-to-all-start = ((bf16[8,2,2,48,16,256]{5,4,3,2,1,0:T(8,128)(2,1)}), bf16[8,2,2,48,16,256]{5,4,3,2,1,0:T(8,128)(2,1)}, u32[]{:S(2)}, u32[]{:S(2)}) async-start(bf16[8,2,2,48,16,256]{5,4,3,2,1,0:T(8,128)(2,1)} %maximum_bitcast_fusion), calls=%async_computation | async-start | bytes 25165824 | tf_op jit(solution)/shard_map/all_to_all | solution.py:105
  23.1 0.0 slice-start.1
  23.1 0.0 slice-start.3
  23.1 1.6 slice-done.1
  24.7 0.6 slice-done.3
  25.3 2.4 copy_bitcast_fusion.2
  27.8 2.3 maximum_bitcast_fusion.1
  30.1 0.0 copy-start.2
  30.1 132.5 %all-to-all-done.x_ref = bf16[8,2,2,48,16,256]{5,4,3,2,1,0:T(8,128)(2,1)} async-done(((bf16[8,2,2,48,16,256]{5,4,3,2,1,0:T(8,128)(2,1)}), bf16[8,2,2,48,16,256]{5,4,3,2,1,0:T(8,128)(2,1)}, u32[]{:S(2)}, u32[]{:S(2)}) %all-to-all-start) | async-done | bytes 12582944 | tf_op jit(solution)/shard_map/all_to_all | solution.py:105
  162.6 4.6 %all-to-all-start.1 = ((bf16[8,2,2,16,16,256]{5,4,3,2,1,0:T(8,128)(2,1)}), bf16[8,2,2,16,16,256]{5,4,3,2,1,0:T(8,128)(2,1)}, u32[]{:S(2)}, u32[]{:S(2)}) async-start(bf16[8,2,2,16,16,256]{5,4,3,2,1,0:T(8,128)(2,1)} %maximum_bitcast_fusion.1), calls=%async_computation.1 | async-start | bytes 8388608 | tf_op jit(solution)/shard_map/all_to_all | solution.py:105
  167.2 0.0 copy-done.2
  167.2 0.1 add_subtract_fusion
  167.3 0.6 fusion.2
  172.9 61.6 %shard_map.37 = f32[2,2,48,33,128]{4,3,2,1,0:T(8,128)} custom-call(bf16[8,2,2,48,16,256]{5,4,3,2,1,0:T(8,128)(2,1)} %all-to-all-done.x_ref), custom_call_target="tpu_custom_call" | custom-call | tf_op jit(solution)/shard_map/pallas_call | solution.py:60
  234.5 2.5 add_bitcast_fusion.1
  237.0 0.0 all-to-all-done.1.x_ref
  237.0 21.8 %shard_map.38 = f32[2,2,16,33,128]{4,3,2,1,0:T(8,128)} custom-call(bf16[8,2,2,16,16,256]{5,4,3,2,1,0:T(8,128)(2,1)} %all-to-all-done.1.x_ref), custom_call_target="tpu_custom_call" | custom-call | tf_op jit(solution)/shard_map/pallas_call | solution.py:60
  258.8 1.4 add_bitcast_fusion.4
  260.2 0.1 pad_maximum_fusion
  260.3 0.2 copy.13
  260.6 3.3 %collective-permute-start = (f32[64,33,128]{2,0,1:T(8,128)S(1)}, f32[64,33,128]{2,0,1:T(8,128)S(1)}, u32[]{:S(2)}, u32[]{:S(2)}) collective-permute-start(f32[64,33,128]{2,0,1:T(8,128)S(1)} %copy.13), channel_id=1, source_target_pairs={{8,0},{16,8},{24,16},{32,24},{40,32},{48,40},{56,48},{64,56},{72,6... | collective-permute-start | bytes 3244040 | tf_op jit(solution)/shard_map/ppermute | solution.py:19
  263.9 0.0 copy-start
  263.9 0.1 pad_maximum_fusion.1
  264.0 0.2 copy.15
  264.2 4.7 %collective-permute-start.1 = (f32[64,33,128]{2,0,1:T(8,128)S(1)}, f32[64,33,128]{2,0,1:T(8,128)S(1)}, u32[]{:S(2)}, u32[]{:S(2)}) collective-permute-start(f32[64,33,128]{2,0,1:T(8,128)S(1)} %copy.15), channel_id=1, source_target_pairs={{0,8},{8,16},{16,24},{24,32},{32,40},{40,48},{48,56},{56,64},{64,7... | collective-permute-start | bytes 3244040 | tf_op jit(solution)/shard_map/ppermute | solution.py:19
  271.4 0.0 copy-done
  271.4 0.0 copy-start.1
  271.4 0.2 add_bitcast_fusion.2
  271.7 1.1 copy-done.1
  272.8 0.1 add_bitcast_fusion.5
  272.8 18.0 %collective-permute-done = f32[64,33,128]{2,0,1:T(8,128)S(1)} collective-permute-done((f32[64,33,128]{2,0,1:T(8,128)S(1)}, f32[64,33,128]{2,0,1:T(8,128)S(1)}, u32[]{:S(2)}, u32[]{:S(2)}) %collective-permute-start) | collective-permute-done | bytes 1081376 | tf_op jit(solution)/shard_map/ppermute | solution.py:19
  290.8 0.0 collective-permute-done.1
  290.8 1.2 fusion.1
  292.1 1.2 copy.17
Async XLA Ops:
  0.0 2.8 slice-start
  0.0 4.6 %slice-start.2 = ((bf16[2,16,64,8,256]{4,3,2,1,0:T(8,128)(2,1)}), bf16[2,16,48,8,256]{4,3,2,1,0:T(8,128)(2,1)S(1)}, s32[]{:S(2)}) async-start(bf16[2,16,64,8,256]{4,3,2,1,0:T(8,128)(2,1)} %param.4), calls=%async_computation.4 | async-start | bytes 12582912 | tf_op jit(solution)/shard_map/slice | solution.py:99
  17.1 145.5 %all-to-all-start = ((bf16[8,2,2,48,16,256]{5,4,3,2,1,0:T(8,128)(2,1)}), bf16[8,2,2,48,16,256]{5,4,3,2,1,0:T(8,128)(2,1)}, u32[]{:S(2)}, u32[]{:S(2)}) async-start(bf16[8,2,2,48,16,256]{5,4,3,2,1,0:T(8,128)(2,1)} %maximum_bitcast_fusion), calls=%async_computation | async-start | bytes 25165824 | tf_op jit(solution)/shard_map/all_to_all | solution.py:105
  23.1 1.6 slice-start.1
  23.1 2.2 slice-start.3
  30.1 137.1 %copy-start.2 = (s32[2]{0:T(128)S(1)}, s32[2]{0:T(128)}, u32[]{:S(2)}) copy-start(s32[2]{0:T(128)} %param.5) | copy-start | bytes 28
  162.6 74.4 %all-to-all-start.1 = ((bf16[8,2,2,16,16,256]{5,4,3,2,1,0:T(8,128)(2,1)}), bf16[8,2,2,16,16,256]{5,4,3,2,1,0:T(8,128)(2,1)}, u32[]{:S(2)}, u32[]{:S(2)}) async-start(bf16[8,2,2,16,16,256]{5,4,3,2,1,0:T(8,128)(2,1)} %maximum_bitcast_fusion.1), calls=%async_computation.1 | async-start | bytes 8388608 | tf_op jit(solution)/shard_map/all_to_all | solution.py:105
  260.6 30.3 %collective-permute-start = (f32[64,33,128]{2,0,1:T(8,128)S(1)}, f32[64,33,128]{2,0,1:T(8,128)S(1)}, u32[]{:S(2)}, u32[]{:S(2)}) collective-permute-start(f32[64,33,128]{2,0,1:T(8,128)S(1)} %copy.13), channel_id=1, source_target_pairs={{8,0},{16,8},{24,16},{32,24},{40,32},{48,40},{56,48},{64,56},{72,6... | collective-permute-start | bytes 3244040 | tf_op jit(solution)/shard_map/ppermute | solution.py:19
  263.9 7.5 %copy-start = (f32[2,2,48,33,128]{4,3,2,1,0:T(8,128)S(1)}, f32[2,2,48,33,128]{4,3,2,1,0:T(8,128)}, u32[]{:S(2)}) copy-start(f32[2,2,48,33,128]{4,3,2,1,0:T(8,128)} %shard_map.37) | copy-start | bytes 9732100
  264.2 26.6 %collective-permute-start.1 = (f32[64,33,128]{2,0,1:T(8,128)S(1)}, f32[64,33,128]{2,0,1:T(8,128)S(1)}, u32[]{:S(2)}, u32[]{:S(2)}) collective-permute-start(f32[64,33,128]{2,0,1:T(8,128)S(1)} %copy.15), channel_id=1, source_target_pairs={{0,8},{8,16},{16,24},{24,32},{32,40},{40,48},{48,56},{56,64},{64,7... | collective-permute-start | bytes 3244040 | tf_op jit(solution)/shard_map/ppermute | solution.py:19
  271.4 1.3 copy-start.1

commit v5 on v4

--- a/solution.py
+++ b/solution.py
@@ -10,7 +10,7 @@
 LAGS = 33
 TILE = 128
 CB = 8
-CHUNKS = (48, 16)
+CHUNKS = (32, 24, 8)
 
 
 def passed_along(block, axis, distance):

time: 294 us -> 291 us (0.990)
  waiting for transfers between devices: 150 us -> 127 us
  local copies, waits for them, and re-layouts: 19.7 us -> 26.6 us
  other arithmetic: 13.3 us -> 19.1 us
  starting transfers between devices: 18.7 us -> 24.5 us
    all_to_all x2 -> x3, waiting for transfers between devices: 133 us -> 108 us  [body(): lax.all_to_all(pair, 'tm', split_axis=0, concat_axis=0, tiled=True)]
    another operation x2 -> x3, local copies, waits for them, and re-layouts: 9.62 us -> 15.6 us  [body(): pair = jnp.stack([source_snap[:, :, cs], receiver_snap[:, :, cs]])]
    all_to_all x2 -> x3, starting transfers between devices: 10.7 us -> 15.5 us  [body(): lax.all_to_all(pair, 'tm', split_axis=0, concat_axis=0, tiled=True)]
    transpose x2 -> x3, other arithmetic: 7.59 us -> 10.9 us  [body(): pair = jnp.transpose(pair, (4, 0, 1, 3, 2, 5))]
    pallas_call x2 -> x3, Pallas kernels: 83.3 us -> 85.3 us  [lag_images(): pl.pallas_call(lag_kernel, grid=(shots, chans // cb), in_specs=[pl.BlockS...]
    slice x8 -> x12, local copies, waits for them, and re-layouts: 6.82 us -> 7.83 us  [body(): pair = jnp.stack([source_snap[:, :, cs], receiver_snap[:, :, cs]])]
  transfers between devices with their start and end apart: 4 -> 5, of which waited for: 2 -> 3; matrix products, arithmetic and copies ran while one was open for 3% -> 5% of each run, Pallas kernels for 21% -> 25%
where the time goes in v5:
time: 291 us; the launch traced here: 290 us
  waiting for transfers between devices  127 us (44%)
  Pallas kernels  85.3 us (29%)
  local copies, waits for them, and re-layouts  26.6 us (9%)
  starting transfers between devices  24.5 us (8%)
  other arithmetic  19.1 us (7%)
  between operations  7.72 us (3%)
    all_to_all x3, waiting for transfers between devices, body(): lax.all_to_all(pair, 'tm', split_axis=0, concat_axis=0, tiled=True)  108 us
    pallas_call x3, Pallas kernels, lag_images(): pl.pallas_call(lag_kernel, grid=(shots, chans // cb), in_specs=[pl.BlockS...  85.3 us
    ppermute x2, waiting for transfers between devices, passed_along(): return lax.ppermute(block, axis, route)  18.2 us
    another operation x3, local copies, waits for them, and re-layouts, body(): pair = jnp.stack([source_snap[:, :, cs], receiver_snap[:, :, cs]])  15.6 us
    all_to_all x3, starting transfers between devices, body(): lax.all_to_all(pair, 'tm', split_axis=0, concat_axis=0, tiled=True)  15.5 us
    transpose x3, other arithmetic, body(): pair = jnp.transpose(pair, (4, 0, 1, 3, 2, 5))  10.9 us
    ppermute x2, starting transfers between devices, passed_along(): return lax.ppermute(block, axis, route)  8.95 us
    slice x12, local copies, waits for them, and re-layouts, body(): pair = jnp.stack([source_snap[:, :, cs], receiver_snap[:, :, cs]])  7.83 us
  transfers between devices with their start and end apart: 5, of which 3 were waited for; matrix products, arithmetic and copies ran while one was open for 5% of the time, Pallas kernels for 25%

profile of v5, /device:TPU:3, one launch (start us, length us, event | category | flops | bytes accessed | tf_op | source)
XLA Modules:
  0.0 289.8 jit_solution(16702802361027743749)
XLA Ops:
  0.0 2.2 slice-done
  2.2 1.3 slice-done.3
  3.5 10.8 %copy_bitcast_fusion = (bf16[1,2,16,32,8,256]{5,2,3,1,0,4:T(8,128)(2,1)S(1)}, bf16[1,2,16,32,8,256]{5,2,3,1,0,4:T(8,128)(2,1)}) fusion(bf16[2,16,32,8,256]{4,3,2,1,0:T(8,128)(2,1)S(1)} %slice-done.3, bf16[2,16,32,8,256]{4,3,2,1,0:T(8,128)(2,1)S(1)} %slice-done), kind=kLoop, calls=%fused_computation.2 | loop fusion | bytes 16777216 | tf_op jit(solution)/shard_map/stack | solution.py:99
  14.3 6.2 %maximum_bitcast_fusion = bf16[8,2,2,32,16,256]{5,4,3,2,1,0:T(8,128)(2,1)} fusion(bf16[1,2,16,32,8,256]{5,2,3,1,0,4:T(8,128)(2,1)S(1)} %get-tuple-element.31, bf16[1,2,16,32,8,256]{5,2,3,1,0,4:T(8,128)(2,1)} %get-tuple-element.32), kind=kLoop, calls=%fused_computation | loop fusion | flops 4194304 | bytes 16777216 | tf_op jit(solution)/shard_map/transpose | solution.py:100
  20.5 6.0 %all-to-all-start = ((bf16[8,2,2,32,16,256]{5,4,3,2,1,0:T(8,128)(2,1)}), bf16[8,2,2,32,16,256]{5,4,3,2,1,0:T(8,128)(2,1)}, u32[]{:S(2)}, u32[]{:S(2)}) async-start(bf16[8,2,2,32,16,256]{5,4,3,2,1,0:T(8,128)(2,1)} %maximum_bitcast_fusion), calls=%async_computation | async-start | bytes 16777216 | tf_op jit(solution)/shard_map/all_to_all | solution.py:105
  26.5 0.0 slice-start.4
  26.5 1.9 slice-done.1
  28.4 1.0 slice-done.4
  29.4 3.6 %copy_bitcast_fusion.2 = (bf16[1,2,16,24,8,256]{5,2,3,1,0,4:T(8,128)(2,1)S(1)}, bf16[1,2,16,24,8,256]{5,2,3,1,0,4:T(8,128)(2,1)S(1)}) fusion(bf16[2,16,24,8,256]{4,3,2,1,0:T(8,128)(2,1)S(1)} %slice-done.4, bf16[2,16,24,8,256]{4,3,2,1,0:T(8,128)(2,1)S(1)} %slice-done.1), kind=kLoop, calls=%fused_computation.4 | loop fusion | bytes 12582912 | tf_op jit(solution)/shard_map/stack | solution.py:99
  32.9 3.2 %maximum_bitcast_fusion.1 = bf16[8,2,2,24,16,256]{5,4,3,2,1,0:T(8,128)(2,1)} fusion(bf16[1,2,16,24,8,256]{5,2,3,1,0,4:T(8,128)(2,1)S(1)} %get-tuple-element.29, bf16[1,2,16,24,8,256]{5,2,3,1,0,4:T(8,128)(2,1)S(1)} %get-tuple-element.30), kind=kLoop, calls=%fused_computation.1 | loop fusion | flops 3145728 | bytes 12582912 | tf_op jit(solution)/shard_map/transpose | solution.py:100
  36.1 84.2 %all-to-all-done.x_ref = bf16[8,2,2,32,16,256]{5,4,3,2,1,0:T(8,128)(2,1)} async-done(((bf16[8,2,2,32,16,256]{5,4,3,2,1,0:T(8,128)(2,1)}), bf16[8,2,2,32,16,256]{5,4,3,2,1,0:T(8,128)(2,1)}, u32[]{:S(2)}, u32[]{:S(2)}) %all-to-all-start) | async-done | bytes 8388640 | tf_op jit(solution)/shard_map/all_to_all | solution.py:105
  120.3 5.0 %all-to-all-start.1 = ((bf16[8,2,2,24,16,256]{5,4,3,2,1,0:T(8,128)(2,1)}), bf16[8,2,2,24,16,256]{5,4,3,2,1,0:T(8,128)(2,1)}, u32[]{:S(2)}, u32[]{:S(2)}) async-start(bf16[8,2,2,24,16,256]{5,4,3,2,1,0:T(8,128)(2,1)} %maximum_bitcast_fusion.1), calls=%async_computation.1 | async-start | bytes 12582912 | tf_op jit(solution)/shard_map/all_to_all | solution.py:105
  125.3 0.0 slice-start.2
  125.3 0.0 slice-start.5
  125.3 1.2 slice-done.2
  126.5 0.3 slice-done.5
  126.9 1.2 copy_bitcast_fusion.4
  128.1 1.5 maximum_bitcast_fusion.2
  129.6 41.7 %shard_map.37 = f32[2,2,32,33,128]{4,3,2,1,0:T(8,128)} custom-call(bf16[8,2,2,32,16,256]{5,4,3,2,1,0:T(8,128)(2,1)} %all-to-all-done.x_ref), custom_call_target="tpu_custom_call" | custom-call | tf_op jit(solution)/shard_map/pallas_call | solution.py:60
  171.2 24.2 %all-to-all-done.1.x_ref = bf16[8,2,2,24,16,256]{5,4,3,2,1,0:T(8,128)(2,1)} async-done(((bf16[8,2,2,24,16,256]{5,4,3,2,1,0:T(8,128)(2,1)}), bf16[8,2,2,24,16,256]{5,4,3,2,1,0:T(8,128)(2,1)}, u32[]{:S(2)}, u32[]{:S(2)}) %all-to-all-start.1) | async-done | bytes 6291488 | tf_op jit(solution)/shard_map/all_to_all | solution.py:105
  195.4 4.5 %all-to-all-start.2 = ((bf16[8,2,2,8,16,256]{5,4,3,2,1,0:T(8,128)(2,1)}), bf16[8,2,2,8,16,256]{5,4,3,2,1,0:T(8,128)(2,1)}, u32[]{:S(2)}, u32[]{:S(2)}) async-start(bf16[8,2,2,8,16,256]{5,4,3,2,1,0:T(8,128)(2,1)} %maximum_bitcast_fusion.2), calls=%async_computation.2 | async-start | bytes 4194304 | tf_op jit(solution)/shard_map/all_to_all | solution.py:105
  199.9 0.0 copy-done.4
  199.9 0.1 add_subtract_fusion
  200.0 0.7 fusion.2
  205.7 31.7 %shard_map.38 = f32[2,2,24,33,128]{4,3,2,1,0:T(8,128)} custom-call(bf16[8,2,2,24,16,256]{5,4,3,2,1,0:T(8,128)(2,1)} %all-to-all-done.1.x_ref), custom_call_target="tpu_custom_call" | custom-call | tf_op jit(solution)/shard_map/pallas_call | solution.py:60
  237.4 2.8 add_bitcast_fusion.4
  240.2 0.0 copy-done
  240.2 1.1 add_bitcast_fusion.1
  241.4 0.0 all-to-all-done.2.x_ref
  241.4 11.8 %shard_map.39 = f32[2,2,8,33,128]{4,3,2,1,0:T(8,128)} custom-call(bf16[8,2,2,8,16,256]{5,4,3,2,1,0:T(8,128)(2,1)} %all-to-all-done.2.x_ref), custom_call_target="tpu_custom_call" | custom-call | tf_op jit(solution)/shard_map/pallas_call | solution.py:60
  253.2 1.2 add_bitcast_fusion.7
  254.5 0.0 copy-start.3
  254.5 1.4 pad_maximum_fusion
  255.9 0.2 copy.17
  256.1 4.4 %collective-permute-start = (f32[64,33,128]{2,0,1:T(8,128)S(1)}, f32[64,33,128]{2,0,1:T(8,128)S(1)}, u32[]{:S(2)}, u32[]{:S(2)}) collective-permute-start(f32[64,33,128]{2,0,1:T(8,128)S(1)} %copy.17), channel_id=1, source_target_pairs={{8,0},{16,8},{24,16},{32,24},{40,32},{48,40},{56,48},{64,56},{72,6... | collective-permute-start | bytes 3244040 | tf_op jit(solution)/shard_map/ppermute | solution.py:19
  260.5 0.0 copy-done.3
  260.5 0.0 copy-start.1
  260.5 0.1 pad_maximum_fusion.1
  260.6 0.2 copy.19
  260.8 4.6 %collective-permute-start.1 = (f32[64,33,128]{2,0,1:T(8,128)S(1)}, f32[64,33,128]{2,0,1:T(8,128)S(1)}, u32[]{:S(2)}, u32[]{:S(2)}) collective-permute-start(f32[64,33,128]{2,0,1:T(8,128)S(1)} %copy.19), channel_id=1, source_target_pairs={{0,8},{8,16},{16,24},{24,32},{32,40},{40,48},{48,56},{56,64},{64,7... | collective-permute-start | bytes 3244040 | tf_op jit(solution)/shard_map/ppermute | solution.py:19
  267.9 0.1 add_bitcast_fusion.5
  268.0 0.0 copy-start.2
  268.0 0.2 add_bitcast_fusion.2
  268.2 0.9 copy-done.2
  269.2 18.2 %collective-permute-done = f32[64,33,128]{2,0,1:T(8,128)S(1)} collective-permute-done((f32[64,33,128]{2,0,1:T(8,128)S(1)}, f32[64,33,128]{2,0,1:T(8,128)S(1)}, u32[]{:S(2)}, u32[]{:S(2)}) %collective-permute-start) | collective-permute-done | bytes 1081376 | tf_op jit(solution)/shard_map/ppermute | solution.py:19
  287.4 0.0 collective-permute-done.1
  287.4 1.2 fusion.1
  288.6 1.2 copy.21
  (7 shorter events, 0.1 us)
Async XLA Ops:
  0.0 2.2 slice-start
  0.0 3.5 %slice-start.3 = ((bf16[2,16,64,8,256]{4,3,2,1,0:T(8,128)(2,1)}), bf16[2,16,32,8,256]{4,3,2,1,0:T(8,128)(2,1)S(1)}, s32[]{:S(2)}) async-start(bf16[2,16,64,8,256]{4,3,2,1,0:T(8,128)(2,1)} %param.4), calls=%async_computation.6 | async-start | bytes 8388608 | tf_op jit(solution)/shard_map/slice | solution.py:99
  20.5 99.8 %all-to-all-start = ((bf16[8,2,2,32,16,256]{5,4,3,2,1,0:T(8,128)(2,1)}), bf16[8,2,2,32,16,256]{5,4,3,2,1,0:T(8,128)(2,1)}, u32[]{:S(2)}, u32[]{:S(2)}) async-start(bf16[8,2,2,32,16,256]{5,4,3,2,1,0:T(8,128)(2,1)} %maximum_bitcast_fusion), calls=%async_computation | async-start | bytes 16777216 | tf_op jit(solution)/shard_map/all_to_all | solution.py:105
  26.5 1.9 slice-start.1
  26.5 2.8 slice-start.4
  120.3 75.1 %all-to-all-start.1 = ((bf16[8,2,2,24,16,256]{5,4,3,2,1,0:T(8,128)(2,1)}), bf16[8,2,2,24,16,256]{5,4,3,2,1,0:T(8,128)(2,1)}, u32[]{:S(2)}, u32[]{:S(2)}) async-start(bf16[8,2,2,24,16,256]{5,4,3,2,1,0:T(8,128)(2,1)} %maximum_bitcast_fusion.1), calls=%async_computation.1 | async-start | bytes 12582912 | tf_op jit(solution)/shard_map/all_to_all | solution.py:105
  125.3 1.2 slice-start.2
  125.3 1.5 slice-start.5
  171.2 28.7 %copy-start.4 = (s32[2]{0:T(128)S(1)}, s32[2]{0:T(128)}, u32[]{:S(2)}) copy-start(s32[2]{0:T(128)} %param.5) | copy-start | bytes 28
  195.4 46.0 %all-to-all-start.2 = ((bf16[8,2,2,8,16,256]{5,4,3,2,1,0:T(8,128)(2,1)}), bf16[8,2,2,8,16,256]{5,4,3,2,1,0:T(8,128)(2,1)}, u32[]{:S(2)}, u32[]{:S(2)}) async-start(bf16[8,2,2,8,16,256]{5,4,3,2,1,0:T(8,128)(2,1)} %maximum_bitcast_fusion.2), calls=%async_computation.2 | async-start | bytes 4194304 | tf_op jit(solution)/shard_map/all_to_all | solution.py:105
  237.4 2.8 copy-start
  254.5 6.0 %copy-start.3 = (f32[24,33,128]{2,1,0:T(8,128)S(1)}, f32[24,33,128]{2,1,0:T(8,128)}, u32[]{:S(2)}) copy-start(f32[24,33,128]{2,1,0:T(8,128)} %get-tuple-element.20) | copy-start | bytes 1216516
  256.1 31.3 %collective-permute-start = (f32[64,33,128]{2,0,1:T(8,128)S(1)}, f32[64,33,128]{2,0,1:T(8,128)S(1)}, u32[]{:S(2)}, u32[]{:S(2)}) collective-permute-start(f32[64,33,128]{2,0,1:T(8,128)S(1)} %copy.17), channel_id=1, source_target_pairs={{8,0},{16,8},{24,16},{32,24},{40,32},{48,40},{56,48},{64,56},{72,6... | collective-permute-start | bytes 3244040 | tf_op jit(solution)/shard_map/ppermute | solution.py:19
  260.5 7.4 %copy-start.1 = (f32[2,2,24,33,128]{4,3,2,1,0:T(8,128)S(1)}, f32[2,2,24,33,128]{4,3,2,1,0:T(8,128)}, u32[]{:S(2)}) copy-start(f32[2,2,24,33,128]{4,3,2,1,0:T(8,128)} %shard_map.38) | copy-start | bytes 4866052
  260.8 26.6 %collective-permute-start.1 = (f32[64,33,128]{2,0,1:T(8,128)S(1)}, f32[64,33,128]{2,0,1:T(8,128)S(1)}, u32[]{:S(2)}, u32[]{:S(2)}) collective-permute-start(f32[64,33,128]{2,0,1:T(8,128)S(1)} %copy.19), channel_id=1, source_target_pairs={{0,8},{8,16},{16,24},{24,32},{32,40},{40,48},{48,56},{56,64},{64,7... | collective-permute-start | bytes 3244040 | tf_op jit(solution)/shard_map/ppermute | solution.py:19
  268.0 1.1 copy-start.2

commit v6 on v5

--- a/solution.py
+++ b/solution.py
@@ -51,7 +51,7 @@
             o_ref[0, 1, c, pl.ds(half + d, 1), :] = out[:, TILE:]
         return carry
 
-    lax.fori_loop(0, cb, one_channel, 0)
+    lax.fori_loop(0, cb, one_channel, 0, unroll=2)
 
 
 def lag_images(pair):

time: 291 us -> 276 us (0.948)
  Pallas kernels: 85.3 us -> 56.4 us
  waiting for transfers between devices: 127 us -> 141 us
    pallas_call x3, Pallas kernels: 85.3 us -> 56.4 us  [lag_images(): pl.pallas_call(lag_kernel, grid=(shots, chans // cb), in_specs=[pl.BlockS...]
    all_to_all x3, waiting for transfers between devices: 108 us -> 123 us  [body(): lax.all_to_all(pair, 'tm', split_axis=0, concat_axis=0, tiled=True)]
  transfers between devices with their start and end apart: 5 -> 5, of which waited for: 3 -> 3; matrix products, arithmetic and copies ran while one was open for 5% -> 5% of each run, Pallas kernels for 25% -> 17%
where the time goes in v6:
time: 276 us; the launch traced here: 275 us
  waiting for transfers between devices  141 us (51%)
  Pallas kernels  56.4 us (20%)
  local copies, waits for them, and re-layouts  26.6 us (10%)
  starting transfers between devices  24.5 us (9%)
  other arithmetic  19.1 us (7%)
  between operations  7.72 us (3%)
    all_to_all x3, waiting for transfers between devices, body(): lax.all_to_all(pair, 'tm', split_axis=0, concat_axis=0, tiled=True)  123 us
    pallas_call x3, Pallas kernels, lag_images(): pl.pallas_call(lag_kernel, grid=(shots, chans // cb), in_specs=[pl.BlockS...  56.4 us
    ppermute x2, waiting for transfers between devices, passed_along(): return lax.ppermute(block, axis, route)  18.2 us
    another operation x3, local copies, waits for them, and re-layouts, body(): pair = jnp.stack([source_snap[:, :, cs], receiver_snap[:, :, cs]])  15.6 us
    all_to_all x3, starting transfers between devices, body(): lax.all_to_all(pair, 'tm', split_axis=0, concat_axis=0, tiled=True)  15.5 us
    transpose x3, other arithmetic, body(): pair = jnp.transpose(pair, (4, 0, 1, 3, 2, 5))  10.9 us
    ppermute x2, starting transfers between devices, passed_along(): return lax.ppermute(block, axis, route)  8.99 us
    slice x12, local copies, waits for them, and re-layouts, body(): pair = jnp.stack([source_snap[:, :, cs], receiver_snap[:, :, cs]])  7.83 us
  transfers between devices with their start and end apart: 5, of which 3 were waited for; matrix products, arithmetic and copies ran while one was open for 5% of the time, Pallas kernels for 17%

profile of v6, /device:TPU:3, one launch (start us, length us, event | category | flops | bytes accessed | tf_op | source)
XLA Modules:
  0.0 275.4 jit_solution(18013868900157683823)
XLA Ops:
  0.0 2.2 slice-done
  2.2 1.3 slice-done.3
  3.5 10.8 %copy_bitcast_fusion = (bf16[1,2,16,32,8,256]{5,2,3,1,0,4:T(8,128)(2,1)S(1)}, bf16[1,2,16,32,8,256]{5,2,3,1,0,4:T(8,128)(2,1)}) fusion(bf16[2,16,32,8,256]{4,3,2,1,0:T(8,128)(2,1)S(1)} %slice-done.3, bf16[2,16,32,8,256]{4,3,2,1,0:T(8,128)(2,1)S(1)} %slice-done), kind=kLoop, calls=%fused_computation.2 | loop fusion | bytes 16777216 | tf_op jit(solution)/shard_map/stack | solution.py:99
  14.3 6.2 %maximum_bitcast_fusion = bf16[8,2,2,32,16,256]{5,4,3,2,1,0:T(8,128)(2,1)} fusion(bf16[1,2,16,32,8,256]{5,2,3,1,0,4:T(8,128)(2,1)S(1)} %get-tuple-element.31, bf16[1,2,16,32,8,256]{5,2,3,1,0,4:T(8,128)(2,1)} %get-tuple-element.32), kind=kLoop, calls=%fused_computation | loop fusion | flops 4194304 | bytes 16777216 | tf_op jit(solution)/shard_map/transpose | solution.py:100
  20.5 6.0 %all-to-all-start = ((bf16[8,2,2,32,16,256]{5,4,3,2,1,0:T(8,128)(2,1)}), bf16[8,2,2,32,16,256]{5,4,3,2,1,0:T(8,128)(2,1)}, u32[]{:S(2)}, u32[]{:S(2)}) async-start(bf16[8,2,2,32,16,256]{5,4,3,2,1,0:T(8,128)(2,1)} %maximum_bitcast_fusion), calls=%async_computation | async-start | bytes 16777216 | tf_op jit(solution)/shard_map/all_to_all | solution.py:105
  26.5 0.0 slice-start.4
  26.5 1.9 slice-done.1
  28.4 1.0 slice-done.4
  29.4 3.6 %copy_bitcast_fusion.2 = (bf16[1,2,16,24,8,256]{5,2,3,1,0,4:T(8,128)(2,1)S(1)}, bf16[1,2,16,24,8,256]{5,2,3,1,0,4:T(8,128)(2,1)S(1)}) fusion(bf16[2,16,24,8,256]{4,3,2,1,0:T(8,128)(2,1)S(1)} %slice-done.4, bf16[2,16,24,8,256]{4,3,2,1,0:T(8,128)(2,1)S(1)} %slice-done.1), kind=kLoop, calls=%fused_computation.4 | loop fusion | bytes 12582912 | tf_op jit(solution)/shard_map/stack | solution.py:99
  32.9 3.2 %maximum_bitcast_fusion.1 = bf16[8,2,2,24,16,256]{5,4,3,2,1,0:T(8,128)(2,1)} fusion(bf16[1,2,16,24,8,256]{5,2,3,1,0,4:T(8,128)(2,1)S(1)} %get-tuple-element.29, bf16[1,2,16,24,8,256]{5,2,3,1,0,4:T(8,128)(2,1)S(1)} %get-tuple-element.30), kind=kLoop, calls=%fused_computation.1 | loop fusion | flops 3145728 | bytes 12582912 | tf_op jit(solution)/shard_map/transpose | solution.py:100
  36.1 84.2 %all-to-all-done.x_ref = bf16[8,2,2,32,16,256]{5,4,3,2,1,0:T(8,128)(2,1)} async-done(((bf16[8,2,2,32,16,256]{5,4,3,2,1,0:T(8,128)(2,1)}), bf16[8,2,2,32,16,256]{5,4,3,2,1,0:T(8,128)(2,1)}, u32[]{:S(2)}, u32[]{:S(2)}) %all-to-all-start) | async-done | bytes 8388640 | tf_op jit(solution)/shard_map/all_to_all | solution.py:105
  120.3 5.0 %all-to-all-start.1 = ((bf16[8,2,2,24,16,256]{5,4,3,2,1,0:T(8,128)(2,1)}), bf16[8,2,2,24,16,256]{5,4,3,2,1,0:T(8,128)(2,1)}, u32[]{:S(2)}, u32[]{:S(2)}) async-start(bf16[8,2,2,24,16,256]{5,4,3,2,1,0:T(8,128)(2,1)} %maximum_bitcast_fusion.1), calls=%async_computation.1 | async-start | bytes 12582912 | tf_op jit(solution)/shard_map/all_to_all | solution.py:105
  125.3 0.0 slice-start.2
  125.3 0.0 slice-start.5
  125.3 1.2 slice-done.2
  126.5 0.3 slice-done.5
  126.9 1.2 copy_bitcast_fusion.4
  128.1 1.5 maximum_bitcast_fusion.2
  129.6 27.3 %shard_map.37 = f32[2,2,32,33,128]{4,3,2,1,0:T(8,128)} custom-call(bf16[8,2,2,32,16,256]{5,4,3,2,1,0:T(8,128)(2,1)} %all-to-all-done.x_ref), custom_call_target="tpu_custom_call" | custom-call | tf_op jit(solution)/shard_map/pallas_call | solution.py:60
  156.8 38.6 %all-to-all-done.1.x_ref = bf16[8,2,2,24,16,256]{5,4,3,2,1,0:T(8,128)(2,1)} async-done(((bf16[8,2,2,24,16,256]{5,4,3,2,1,0:T(8,128)(2,1)}), bf16[8,2,2,24,16,256]{5,4,3,2,1,0:T(8,128)(2,1)}, u32[]{:S(2)}, u32[]{:S(2)}) %all-to-all-start.1) | async-done | bytes 6291488 | tf_op jit(solution)/shard_map/all_to_all | solution.py:105
  195.4 4.5 %all-to-all-start.2 = ((bf16[8,2,2,8,16,256]{5,4,3,2,1,0:T(8,128)(2,1)}), bf16[8,2,2,8,16,256]{5,4,3,2,1,0:T(8,128)(2,1)}, u32[]{:S(2)}, u32[]{:S(2)}) async-start(bf16[8,2,2,8,16,256]{5,4,3,2,1,0:T(8,128)(2,1)} %maximum_bitcast_fusion.2), calls=%async_computation.2 | async-start | bytes 4194304 | tf_op jit(solution)/shard_map/all_to_all | solution.py:105
  199.9 0.0 copy-done.4
  199.9 0.1 add_subtract_fusion
  200.0 0.7 fusion.2
  205.7 20.9 %shard_map.38 = f32[2,2,24,33,128]{4,3,2,1,0:T(8,128)} custom-call(bf16[8,2,2,24,16,256]{5,4,3,2,1,0:T(8,128)(2,1)} %all-to-all-done.1.x_ref), custom_call_target="tpu_custom_call" | custom-call | tf_op jit(solution)/shard_map/pallas_call | solution.py:60
  226.6 2.8 %add_bitcast_fusion.4 = (f32[24,33,128]{2,1,0:T(8,128)}, f32[24,33,128]{2,1,0:T(8,128)}) fusion(f32[2,2,24,33,128]{4,3,2,1,0:T(8,128)} %shard_map.38, pred[]{:T(512)} %bitcast.19, pred[]{:T(512)} %bitcast.18, pred[]{:T(512)} %bitcast.17, pred[]{:T(512)} %bitcast.16, pred[]{:T(512)} %bitcast.26, pred[]{:T(512)} %bitcast.25, pred[]{:T(512)} %bitcast.24, ...), kind=kLoop, calls=%fused_computation.18 | loop fusion | flops 1419264 | bytes 2433032 | tf_op jit(solution)/shard_map/add | solution.py:79
  229.4 0.0 copy-done
  229.4 1.1 add_bitcast_fusion.1
  230.6 0.0 all-to-all-done.2.x_ref
  230.6 8.2 %shard_map.39 = f32[2,2,8,33,128]{4,3,2,1,0:T(8,128)} custom-call(bf16[8,2,2,8,16,256]{5,4,3,2,1,0:T(8,128)(2,1)} %all-to-all-done.2.x_ref), custom_call_target="tpu_custom_call" | custom-call | tf_op jit(solution)/shard_map/pallas_call | solution.py:60
  238.8 1.2 add_bitcast_fusion.7
  240.0 0.0 copy-start.3
  240.0 1.4 pad_maximum_fusion
  241.4 0.2 copy.17
  241.6 4.4 %collective-permute-start = (f32[64,33,128]{2,0,1:T(8,128)S(1)}, f32[64,33,128]{2,0,1:T(8,128)S(1)}, u32[]{:S(2)}, u32[]{:S(2)}) collective-permute-start(f32[64,33,128]{2,0,1:T(8,128)S(1)} %copy.17), channel_id=1, source_target_pairs={{8,0},{16,8},{24,16},{32,24},{40,32},{48,40},{56,48},{64,56},{72,6... | collective-permute-start | bytes 3244040 | tf_op jit(solution)/shard_map/ppermute | solution.py:19
  246.0 0.0 copy-done.3
  246.0 0.0 copy-start.1
  246.0 0.1 pad_maximum_fusion.1
  246.1 0.2 copy.19
  246.4 4.6 %collective-permute-start.1 = (f32[64,33,128]{2,0,1:T(8,128)S(1)}, f32[64,33,128]{2,0,1:T(8,128)S(1)}, u32[]{:S(2)}, u32[]{:S(2)}) collective-permute-start(f32[64,33,128]{2,0,1:T(8,128)S(1)} %copy.19), channel_id=1, source_target_pairs={{0,8},{8,16},{16,24},{24,32},{32,40},{40,48},{48,56},{56,64},{64,7... | collective-permute-start | bytes 3244040 | tf_op jit(solution)/shard_map/ppermute | solution.py:19
  253.5 0.1 add_bitcast_fusion.5
  253.6 0.0 copy-start.2
  253.6 0.2 add_bitcast_fusion.2
  253.8 0.9 copy-done.2
  254.7 18.2 %collective-permute-done = f32[64,33,128]{2,0,1:T(8,128)S(1)} collective-permute-done((f32[64,33,128]{2,0,1:T(8,128)S(1)}, f32[64,33,128]{2,0,1:T(8,128)S(1)}, u32[]{:S(2)}, u32[]{:S(2)}) %collective-permute-start) | collective-permute-done | bytes 1081376 | tf_op jit(solution)/shard_map/ppermute | solution.py:19
  273.0 0.0 collective-permute-done.1
  273.0 1.2 fusion.1
  274.2 1.2 copy.21
  (7 shorter events, 0.1 us)
Async XLA Ops:
  0.0 2.2 slice-start
  0.0 3.5 %slice-start.3 = ((bf16[2,16,64,8,256]{4,3,2,1,0:T(8,128)(2,1)}), bf16[2,16,32,8,256]{4,3,2,1,0:T(8,128)(2,1)S(1)}, s32[]{:S(2)}) async-start(bf16[2,16,64,8,256]{4,3,2,1,0:T(8,128)(2,1)} %param.4), calls=%async_computation.6 | async-start | bytes 8388608 | tf_op jit(solution)/shard_map/slice | solution.py:99
  20.5 99.8 %all-to-all-start = ((bf16[8,2,2,32,16,256]{5,4,3,2,1,0:T(8,128)(2,1)}), bf16[8,2,2,32,16,256]{5,4,3,2,1,0:T(8,128)(2,1)}, u32[]{:S(2)}, u32[]{:S(2)}) async-start(bf16[8,2,2,32,16,256]{5,4,3,2,1,0:T(8,128)(2,1)} %maximum_bitcast_fusion), calls=%async_computation | async-start | bytes 16777216 | tf_op jit(solution)/shard_map/all_to_all | solution.py:105
  26.5 1.9 slice-start.1
  26.5 2.8 %slice-start.4 = ((bf16[2,16,64,8,256]{4,3,2,1,0:T(8,128)(2,1)}), bf16[2,16,24,8,256]{4,3,2,1,0:T(8,128)(2,1)S(1)}, s32[]{:S(2)}) async-start(bf16[2,16,64,8,256]{4,3,2,1,0:T(8,128)(2,1)} %param.4), calls=%async_computation.7 | async-start | bytes 6291456 | tf_op jit(solution)/shard_map/slice | solution.py:99
  120.3 75.1 %all-to-all-start.1 = ((bf16[8,2,2,24,16,256]{5,4,3,2,1,0:T(8,128)(2,1)}), bf16[8,2,2,24,16,256]{5,4,3,2,1,0:T(8,128)(2,1)}, u32[]{:S(2)}, u32[]{:S(2)}) async-start(bf16[8,2,2,24,16,256]{5,4,3,2,1,0:T(8,128)(2,1)} %maximum_bitcast_fusion.1), calls=%async_computation.1 | async-start | bytes 12582912 | tf_op jit(solution)/shard_map/all_to_all | solution.py:105
  125.3 1.2 slice-start.2
  125.3 1.5 slice-start.5
  156.8 43.1 %copy-start.4 = (s32[2]{0:T(128)S(1)}, s32[2]{0:T(128)}, u32[]{:S(2)}) copy-start(s32[2]{0:T(128)} %param.5) | copy-start | bytes 28
  195.4 35.1 %all-to-all-start.2 = ((bf16[8,2,2,8,16,256]{5,4,3,2,1,0:T(8,128)(2,1)}), bf16[8,2,2,8,16,256]{5,4,3,2,1,0:T(8,128)(2,1)}, u32[]{:S(2)}, u32[]{:S(2)}) async-start(bf16[8,2,2,8,16,256]{5,4,3,2,1,0:T(8,128)(2,1)} %maximum_bitcast_fusion.2), calls=%async_computation.2 | async-start | bytes 4194304 | tf_op jit(solution)/shard_map/all_to_all | solution.py:105
  226.6 2.8 %copy-start = (f32[2,2,32,33,128]{4,3,2,1,0:T(8,128)S(1)}, f32[2,2,32,33,128]{4,3,2,1,0:T(8,128)}, u32[]{:S(2)}) copy-start(f32[2,2,32,33,128]{4,3,2,1,0:T(8,128)} %shard_map.37) | copy-start | bytes 6488068
  240.0 6.0 %copy-start.3 = (f32[24,33,128]{2,1,0:T(8,128)S(1)}, f32[24,33,128]{2,1,0:T(8,128)}, u32[]{:S(2)}) copy-start(f32[24,33,128]{2,1,0:T(8,128)} %get-tuple-element.20) | copy-start | bytes 1216516
  241.6 31.3 %collective-permute-start = (f32[64,33,128]{2,0,1:T(8,128)S(1)}, f32[64,33,128]{2,0,1:T(8,128)S(1)}, u32[]{:S(2)}, u32[]{:S(2)}) collective-permute-start(f32[64,33,128]{2,0,1:T(8,128)S(1)} %copy.17), channel_id=1, source_target_pairs={{8,0},{16,8},{24,16},{32,24},{40,32},{48,40},{56,48},{64,56},{72,6... | collective-permute-start | bytes 3244040 | tf_op jit(solution)/shard_map/ppermute | solution.py:19
  246.0 7.4 %copy-start.1 = (f32[2,2,24,33,128]{4,3,2,1,0:T(8,128)S(1)}, f32[2,2,24,33,128]{4,3,2,1,0:T(8,128)}, u32[]{:S(2)}) copy-start(f32[2,2,24,33,128]{4,3,2,1,0:T(8,128)} %shard_map.38) | copy-start | bytes 4866052
  246.4 26.6 %collective-permute-start.1 = (f32[64,33,128]{2,0,1:T(8,128)S(1)}, f32[64,33,128]{2,0,1:T(8,128)S(1)}, u32[]{:S(2)}, u32[]{:S(2)}) collective-permute-start(f32[64,33,128]{2,0,1:T(8,128)S(1)} %copy.19), channel_id=1, source_target_pairs={{0,8},{8,16},{16,24},{24,32},{32,40},{40,48},{48,56},{56,64},{64,7... | collective-permute-start | bytes 3244040 | tf_op jit(solution)/shard_map/ppermute | solution.py:19
  253.6 1.1 copy-start.2

commit v7 on v6

--- a/solution.py
+++ b/solution.py
@@ -51,7 +51,7 @@
             o_ref[0, 1, c, pl.ds(half + d, 1), :] = out[:, TILE:]
         return carry
 
-    lax.fori_loop(0, cb, one_channel, 0, unroll=2)
+    lax.fori_loop(0, cb, one_channel, 0, unroll=4)
 
 
 def lag_images(pair):

time: 276 us -> 276 us (level)
  no operation moved by 1% of the time
where the time goes in v7:
time: 276 us; the launch traced here: 275 us
  waiting for transfers between devices  141 us (51%)
  Pallas kernels  55.5 us (20%)
  local copies, waits for them, and re-layouts  26.6 us (10%)
  starting transfers between devices  24.5 us (9%)
  other arithmetic  19.1 us (7%)
  between operations  7.72 us (3%)
    all_to_all x3, waiting for transfers between devices, body(): lax.all_to_all(pair, 'tm', split_axis=0, concat_axis=0, tiled=True)  123 us
    pallas_call x3, Pallas kernels, lag_images(): pl.pallas_call(lag_kernel, grid=(shots, chans // cb), in_specs=[pl.BlockS...  55.5 us
    ppermute x2, waiting for transfers between devices, passed_along(): return lax.ppermute(block, axis, route)  18.2 us
    another operation x3, local copies, waits for them, and re-layouts, body(): pair = jnp.stack([source_snap[:, :, cs], receiver_snap[:, :, cs]])  15.6 us
    all_to_all x3, starting transfers between devices, body(): lax.all_to_all(pair, 'tm', split_axis=0, concat_axis=0, tiled=True)  15.5 us
    transpose x3, other arithmetic, body(): pair = jnp.transpose(pair, (4, 0, 1, 3, 2, 5))  10.9 us
    ppermute x2, starting transfers between devices, passed_along(): return lax.ppermute(block, axis, route)  8.95 us
    slice x12, local copies, waits for them, and re-layouts, body(): pair = jnp.stack([source_snap[:, :, cs], receiver_snap[:, :, cs]])  7.83 us
  transfers between devices with their start and end apart: 5, of which 3 were waited for; matrix products, arithmetic and copies ran while one was open for 5% of the time, Pallas kernels for 17%

profile of v7, /device:TPU:3, one launch (start us, length us, event | category | flops | bytes accessed | tf_op | source)
XLA Modules:
  0.0 274.9 jit_solution(2417221147480926537)
XLA Ops:
  0.0 2.2 slice-done
  2.2 1.3 slice-done.3
  3.5 10.8 %copy_bitcast_fusion = (bf16[1,2,16,32,8,256]{5,2,3,1,0,4:T(8,128)(2,1)S(1)}, bf16[1,2,16,32,8,256]{5,2,3,1,0,4:T(8,128)(2,1)}) fusion(bf16[2,16,32,8,256]{4,3,2,1,0:T(8,128)(2,1)S(1)} %slice-done.3, bf16[2,16,32,8,256]{4,3,2,1,0:T(8,128)(2,1)S(1)} %slice-done), kind=kLoop, calls=%fused_computation.2 | loop fusion | bytes 16777216 | tf_op jit(solution)/shard_map/stack | solution.py:99
  14.3 6.2 %maximum_bitcast_fusion = bf16[8,2,2,32,16,256]{5,4,3,2,1,0:T(8,128)(2,1)} fusion(bf16[1,2,16,32,8,256]{5,2,3,1,0,4:T(8,128)(2,1)S(1)} %get-tuple-element.31, bf16[1,2,16,32,8,256]{5,2,3,1,0,4:T(8,128)(2,1)} %get-tuple-element.32), kind=kLoop, calls=%fused_computation | loop fusion | flops 4194304 | bytes 16777216 | tf_op jit(solution)/shard_map/transpose | solution.py:100
  20.5 6.0 %all-to-all-start = ((bf16[8,2,2,32,16,256]{5,4,3,2,1,0:T(8,128)(2,1)}), bf16[8,2,2,32,16,256]{5,4,3,2,1,0:T(8,128)(2,1)}, u32[]{:S(2)}, u32[]{:S(2)}) async-start(bf16[8,2,2,32,16,256]{5,4,3,2,1,0:T(8,128)(2,1)} %maximum_bitcast_fusion), calls=%async_computation | async-start | bytes 16777216 | tf_op jit(solution)/shard_map/all_to_all | solution.py:105
  26.5 0.0 slice-start.4
  26.5 1.9 slice-done.1
  28.4 1.0 slice-done.4
  29.4 3.6 %copy_bitcast_fusion.2 = (bf16[1,2,16,24,8,256]{5,2,3,1,0,4:T(8,128)(2,1)S(1)}, bf16[1,2,16,24,8,256]{5,2,3,1,0,4:T(8,128)(2,1)S(1)}) fusion(bf16[2,16,24,8,256]{4,3,2,1,0:T(8,128)(2,1)S(1)} %slice-done.4, bf16[2,16,24,8,256]{4,3,2,1,0:T(8,128)(2,1)S(1)} %slice-done.1), kind=kLoop, calls=%fused_computation.4 | loop fusion | bytes 12582912 | tf_op jit(solution)/shard_map/stack | solution.py:99
  32.9 3.2 %maximum_bitcast_fusion.1 = bf16[8,2,2,24,16,256]{5,4,3,2,1,0:T(8,128)(2,1)} fusion(bf16[1,2,16,24,8,256]{5,2,3,1,0,4:T(8,128)(2,1)S(1)} %get-tuple-element.29, bf16[1,2,16,24,8,256]{5,2,3,1,0,4:T(8,128)(2,1)S(1)} %get-tuple-element.30), kind=kLoop, calls=%fused_computation.1 | loop fusion | flops 3145728 | bytes 12582912 | tf_op jit(solution)/shard_map/transpose | solution.py:100
  36.1 84.2 %all-to-all-done.x_ref = bf16[8,2,2,32,16,256]{5,4,3,2,1,0:T(8,128)(2,1)} async-done(((bf16[8,2,2,32,16,256]{5,4,3,2,1,0:T(8,128)(2,1)}), bf16[8,2,2,32,16,256]{5,4,3,2,1,0:T(8,128)(2,1)}, u32[]{:S(2)}, u32[]{:S(2)}) %all-to-all-start) | async-done | bytes 8388640 | tf_op jit(solution)/shard_map/all_to_all | solution.py:105
  120.3 5.0 %all-to-all-start.1 = ((bf16[8,2,2,24,16,256]{5,4,3,2,1,0:T(8,128)(2,1)}), bf16[8,2,2,24,16,256]{5,4,3,2,1,0:T(8,128)(2,1)}, u32[]{:S(2)}, u32[]{:S(2)}) async-start(bf16[8,2,2,24,16,256]{5,4,3,2,1,0:T(8,128)(2,1)} %maximum_bitcast_fusion.1), calls=%async_computation.1 | async-start | bytes 12582912 | tf_op jit(solution)/shard_map/all_to_all | solution.py:105
  125.3 0.0 slice-start.2
  125.3 0.0 slice-start.5
  125.3 1.2 slice-done.2
  126.5 0.3 slice-done.5
  126.9 1.2 copy_bitcast_fusion.4
  128.1 1.5 maximum_bitcast_fusion.2
  129.6 26.8 %shard_map.37 = f32[2,2,32,33,128]{4,3,2,1,0:T(8,128)} custom-call(bf16[8,2,2,32,16,256]{5,4,3,2,1,0:T(8,128)(2,1)} %all-to-all-done.x_ref), custom_call_target="tpu_custom_call" | custom-call | tf_op jit(solution)/shard_map/pallas_call | solution.py:60
  156.3 39.1 %all-to-all-done.1.x_ref = bf16[8,2,2,24,16,256]{5,4,3,2,1,0:T(8,128)(2,1)} async-done(((bf16[8,2,2,24,16,256]{5,4,3,2,1,0:T(8,128)(2,1)}), bf16[8,2,2,24,16,256]{5,4,3,2,1,0:T(8,128)(2,1)}, u32[]{:S(2)}, u32[]{:S(2)}) %all-to-all-start.1) | async-done | bytes 6291488 | tf_op jit(solution)/shard_map/all_to_all | solution.py:105
  195.4 4.5 %all-to-all-start.2 = ((bf16[8,2,2,8,16,256]{5,4,3,2,1,0:T(8,128)(2,1)}), bf16[8,2,2,8,16,256]{5,4,3,2,1,0:T(8,128)(2,1)}, u32[]{:S(2)}, u32[]{:S(2)}) async-start(bf16[8,2,2,8,16,256]{5,4,3,2,1,0:T(8,128)(2,1)} %maximum_bitcast_fusion.2), calls=%async_computation.2 | async-start | bytes 4194304 | tf_op jit(solution)/shard_map/all_to_all | solution.py:105
  199.9 0.0 copy-done.4
  199.9 0.1 add_subtract_fusion
  200.0 0.7 fusion.2
  205.7 20.6 %shard_map.38 = f32[2,2,24,33,128]{4,3,2,1,0:T(8,128)} custom-call(bf16[8,2,2,24,16,256]{5,4,3,2,1,0:T(8,128)(2,1)} %all-to-all-done.1.x_ref), custom_call_target="tpu_custom_call" | custom-call | tf_op jit(solution)/shard_map/pallas_call | solution.py:60
  226.3 2.8 %add_bitcast_fusion.4 = (f32[24,33,128]{2,1,0:T(8,128)}, f32[24,33,128]{2,1,0:T(8,128)}) fusion(f32[2,2,24,33,128]{4,3,2,1,0:T(8,128)} %shard_map.38, pred[]{:T(512)} %bitcast.19, pred[]{:T(512)} %bitcast.18, pred[]{:T(512)} %bitcast.17, pred[]{:T(512)} %bitcast.16, pred[]{:T(512)} %bitcast.26, pred[]{:T(512)} %bitcast.25, pred[]{:T(512)} %bitcast.24, ...), kind=kLoop, calls=%fused_computation.18 | loop fusion | flops 1419264 | bytes 2433032 | tf_op jit(solution)/shard_map/add | solution.py:79
  229.1 0.0 copy-done
  229.1 1.1 add_bitcast_fusion.1
  230.2 0.0 all-to-all-done.2.x_ref
  230.2 8.1 %shard_map.39 = f32[2,2,8,33,128]{4,3,2,1,0:T(8,128)} custom-call(bf16[8,2,2,8,16,256]{5,4,3,2,1,0:T(8,128)(2,1)} %all-to-all-done.2.x_ref), custom_call_target="tpu_custom_call" | custom-call | tf_op jit(solution)/shard_map/pallas_call | solution.py:60
  238.3 1.2 add_bitcast_fusion.7
  239.6 0.0 copy-start.3
  239.6 1.4 pad_maximum_fusion
  241.0 0.2 copy.17
  241.2 4.4 %collective-permute-start = (f32[64,33,128]{2,0,1:T(8,128)S(1)}, f32[64,33,128]{2,0,1:T(8,128)S(1)}, u32[]{:S(2)}, u32[]{:S(2)}) collective-permute-start(f32[64,33,128]{2,0,1:T(8,128)S(1)} %copy.17), channel_id=1, source_target_pairs={{8,0},{16,8},{24,16},{32,24},{40,32},{48,40},{56,48},{64,56},{72,6... | collective-permute-start | bytes 3244040 | tf_op jit(solution)/shard_map/ppermute | solution.py:19
  245.6 0.0 copy-done.3
  245.6 0.0 copy-start.1
  245.6 0.1 pad_maximum_fusion.1
  245.7 0.2 copy.19
  245.9 4.6 %collective-permute-start.1 = (f32[64,33,128]{2,0,1:T(8,128)S(1)}, f32[64,33,128]{2,0,1:T(8,128)S(1)}, u32[]{:S(2)}, u32[]{:S(2)}) collective-permute-start(f32[64,33,128]{2,0,1:T(8,128)S(1)} %copy.19), channel_id=1, source_target_pairs={{0,8},{8,16},{16,24},{24,32},{32,40},{40,48},{48,56},{56,64},{64,7... | collective-permute-start | bytes 3244040 | tf_op jit(solution)/shard_map/ppermute | solution.py:19
  253.0 0.1 add_bitcast_fusion.5
  253.1 0.0 copy-start.2
  253.1 0.2 add_bitcast_fusion.2
  253.3 0.9 copy-done.2
  254.3 18.2 %collective-permute-done = f32[64,33,128]{2,0,1:T(8,128)S(1)} collective-permute-done((f32[64,33,128]{2,0,1:T(8,128)S(1)}, f32[64,33,128]{2,0,1:T(8,128)S(1)}, u32[]{:S(2)}, u32[]{:S(2)}) %collective-permute-start) | collective-permute-done | bytes 1081376 | tf_op jit(solution)/shard_map/ppermute | solution.py:19
  272.5 0.0 collective-permute-done.1
  272.5 1.2 fusion.1
  273.7 1.2 copy.21
  (7 shorter events, 0.1 us)
Async XLA Ops:
  0.0 2.2 slice-start
  0.0 3.5 %slice-start.3 = ((bf16[2,16,64,8,256]{4,3,2,1,0:T(8,128)(2,1)}), bf16[2,16,32,8,256]{4,3,2,1,0:T(8,128)(2,1)S(1)}, s32[]{:S(2)}) async-start(bf16[2,16,64,8,256]{4,3,2,1,0:T(8,128)(2,1)} %param.4), calls=%async_computation.6 | async-start | bytes 8388608 | tf_op jit(solution)/shard_map/slice | solution.py:99
  20.5 99.8 %all-to-all-start = ((bf16[8,2,2,32,16,256]{5,4,3,2,1,0:T(8,128)(2,1)}), bf16[8,2,2,32,16,256]{5,4,3,2,1,0:T(8,128)(2,1)}, u32[]{:S(2)}, u32[]{:S(2)}) async-start(bf16[8,2,2,32,16,256]{5,4,3,2,1,0:T(8,128)(2,1)} %maximum_bitcast_fusion), calls=%async_computation | async-start | bytes 16777216 | tf_op jit(solution)/shard_map/all_to_all | solution.py:105
  26.5 1.9 slice-start.1
  26.5 2.8 %slice-start.4 = ((bf16[2,16,64,8,256]{4,3,2,1,0:T(8,128)(2,1)}), bf16[2,16,24,8,256]{4,3,2,1,0:T(8,128)(2,1)S(1)}, s32[]{:S(2)}) async-start(bf16[2,16,64,8,256]{4,3,2,1,0:T(8,128)(2,1)} %param.4), calls=%async_computation.7 | async-start | bytes 6291456 | tf_op jit(solution)/shard_map/slice | solution.py:99
  120.3 75.1 %all-to-all-start.1 = ((bf16[8,2,2,24,16,256]{5,4,3,2,1,0:T(8,128)(2,1)}), bf16[8,2,2,24,16,256]{5,4,3,2,1,0:T(8,128)(2,1)}, u32[]{:S(2)}, u32[]{:S(2)}) async-start(bf16[8,2,2,24,16,256]{5,4,3,2,1,0:T(8,128)(2,1)} %maximum_bitcast_fusion.1), calls=%async_computation.1 | async-start | bytes 12582912 | tf_op jit(solution)/shard_map/all_to_all | solution.py:105
  125.3 1.2 slice-start.2
  125.3 1.5 slice-start.5
  156.3 43.6 %copy-start.4 = (s32[2]{0:T(128)S(1)}, s32[2]{0:T(128)}, u32[]{:S(2)}) copy-start(s32[2]{0:T(128)} %param.5) | copy-start | bytes 28
  195.4 34.8 %all-to-all-start.2 = ((bf16[8,2,2,8,16,256]{5,4,3,2,1,0:T(8,128)(2,1)}), bf16[8,2,2,8,16,256]{5,4,3,2,1,0:T(8,128)(2,1)}, u32[]{:S(2)}, u32[]{:S(2)}) async-start(bf16[8,2,2,8,16,256]{5,4,3,2,1,0:T(8,128)(2,1)} %maximum_bitcast_fusion.2), calls=%async_computation.2 | async-start | bytes 4194304 | tf_op jit(solution)/shard_map/all_to_all | solution.py:105
  226.3 2.8 %copy-start = (f32[2,2,32,33,128]{4,3,2,1,0:T(8,128)S(1)}, f32[2,2,32,33,128]{4,3,2,1,0:T(8,128)}, u32[]{:S(2)}) copy-start(f32[2,2,32,33,128]{4,3,2,1,0:T(8,128)} %shard_map.37) | copy-start | bytes 6488068
  239.6 6.0 %copy-start.3 = (f32[24,33,128]{2,1,0:T(8,128)S(1)}, f32[24,33,128]{2,1,0:T(8,128)}, u32[]{:S(2)}) copy-start(f32[24,33,128]{2,1,0:T(8,128)} %get-tuple-element.20) | copy-start | bytes 1216516
  241.2 31.3 %collective-permute-start = (f32[64,33,128]{2,0,1:T(8,128)S(1)}, f32[64,33,128]{2,0,1:T(8,128)S(1)}, u32[]{:S(2)}, u32[]{:S(2)}) collective-permute-start(f32[64,33,128]{2,0,1:T(8,128)S(1)} %copy.17), channel_id=1, source_target_pairs={{8,0},{16,8},{24,16},{32,24},{40,32},{48,40},{56,48},{64,56},{72,6... | collective-permute-start | bytes 3244040 | tf_op jit(solution)/shard_map/ppermute | solution.py:19
  245.6 7.4 %copy-start.1 = (f32[2,2,24,33,128]{4,3,2,1,0:T(8,128)S(1)}, f32[2,2,24,33,128]{4,3,2,1,0:T(8,128)}, u32[]{:S(2)}) copy-start(f32[2,2,24,33,128]{4,3,2,1,0:T(8,128)} %shard_map.38) | copy-start | bytes 4866052
  245.9 26.6 %collective-permute-start.1 = (f32[64,33,128]{2,0,1:T(8,128)S(1)}, f32[64,33,128]{2,0,1:T(8,128)S(1)}, u32[]{:S(2)}, u32[]{:S(2)}) collective-permute-start(f32[64,33,128]{2,0,1:T(8,128)S(1)} %copy.19), channel_id=1, source_target_pairs={{0,8},{8,16},{16,24},{24,32},{32,40},{40,48},{48,56},{56,64},{64,7... | collective-permute-start | bytes 3244040 | tf_op jit(solution)/shard_map/ppermute | solution.py:19
  253.1 1.1 copy-start.2

commit v8 on v6

--- a/solution.py
+++ b/solution.py
@@ -10,7 +10,7 @@
 LAGS = 33
 TILE = 128
 CB = 8
-CHUNKS = (32, 24, 8)
+CHUNKS = (8, 40, 16)
 
 
 def passed_along(block, axis, distance):

time: 276 us -> 269 us (0.975)
  waiting for transfers between devices: 141 us -> 124 us
  local copies, waits for them, and re-layouts: 26.6 us -> 36.9 us
    all_to_all x3, waiting for transfers between devices: 123 us -> 106 us  [body(): lax.all_to_all(pair, 'tm', split_axis=0, concat_axis=0, tiled=True)]
    slice x12 -> x10, local copies, waits for them, and re-layouts: 7.83 us -> 14.4 us  [body(): pair = jnp.stack([source_snap[:, :, cs], receiver_snap[:, :, cs]])]
  transfers between devices with their start and end apart: 5 -> 5, of which waited for: 3 -> 3; matrix products, arithmetic and copies ran while one was open for 5% -> 16% of each run, Pallas kernels for 17% -> 16%
where the time goes in v8:
time: 269 us
  waiting for transfers between devices  124 us (46%)
  Pallas kernels  56.5 us (21%)
  local copies, waits for them, and re-layouts  36.9 us (14%)
  starting transfers between devices  25.6 us (10%)
  other arithmetic  18.3 us (7%)
  between operations  7.69 us (3%)
    all_to_all x3, waiting for transfers between devices, body(): lax.all_to_all(pair, 'tm', split_axis=0, concat_axis=0, tiled=True)  106 us
    pallas_call x3, Pallas kernels, lag_images(): pl.pallas_call(lag_kernel, grid=(shots, chans // cb), in_specs=[pl.BlockS...  56.5 us
    ppermute x2, waiting for transfers between devices, passed_along(): return lax.ppermute(block, axis, route)  18.1 us
    another operation x3, local copies, waits for them, and re-layouts, body(): pair = jnp.stack([source_snap[:, :, cs], receiver_snap[:, :, cs]])  17.7 us
    all_to_all x3, starting transfers between devices, body(): lax.all_to_all(pair, 'tm', split_axis=0, concat_axis=0, tiled=True)  15.9 us
    slice x10, local copies, waits for them, and re-layouts, body(): pair = jnp.stack([source_snap[:, :, cs], receiver_snap[:, :, cs]])  14.4 us
    transpose x3, other arithmetic, body(): pair = jnp.transpose(pair, (4, 0, 1, 3, 2, 5))  12.8 us
    ppermute x2, starting transfers between devices, passed_along(): return lax.ppermute(block, axis, route)  9.62 us
  transfers between devices with their start and end apart: 5, of which 3 were waited for; matrix products, arithmetic and copies ran while one was open for 16% of the time, Pallas kernels for 16%

profile of v8, /device:TPU:3, one launch (start us, length us, event | category | flops | bytes accessed | tf_op | source)
XLA Modules:
  0.0 268.7 jit_solution(12011317276119612112)
XLA Ops:
  0.0 1.2 slice-done
  1.2 0.3 slice-done.2
  1.5 1.2 copy_bitcast_fusion.4
  2.7 1.5 maximum_bitcast_fusion.2
  4.3 6.0 %all-to-all-start = ((bf16[8,2,2,8,16,256]{5,4,3,2,1,0:T(8,128)(2,1)}), bf16[8,2,2,8,16,256]{5,4,3,2,1,0:T(8,128)(2,1)S(1)}, u32[]{:S(2)}, u32[]{:S(2)}) async-start(bf16[8,2,2,8,16,256]{5,4,3,2,1,0:T(8,128)(2,1)} %maximum_bitcast_fusion.2), calls=%async_computation | async-start | bytes 4194304 | tf_op jit(solution)/shard_map/all_to_all | solution.py:105
  10.3 5.3 %slice.47 = bf16[2,16,40,8,256]{4,3,2,1,0:T(8,128)(2,1)} slice(bf16[2,16,64,8,256]{4,3,2,1,0:T(8,128)(2,1)} %param.3), slice={[0:2], [0:16], [8:48], [0:8], [0:256]} | slice | bytes 10485760 | tf_op jit(solution)/shard_map/slice | solution.py:99
  15.6 5.4 %slice.48 = bf16[2,16,40,8,256]{4,3,2,1,0:T(8,128)(2,1)} slice(bf16[2,16,64,8,256]{4,3,2,1,0:T(8,128)(2,1)} %param.4), slice={[0:2], [0:16], [8:48], [0:8], [0:256]} | slice | bytes 10485760 | tf_op jit(solution)/shard_map/slice | solution.py:99
  21.0 14.1 %copy_bitcast_fusion = (bf16[1,2,16,40,8,256]{5,2,3,1,0,4:T(8,128)(2,1)}, bf16[1,2,16,40,8,256]{5,2,3,1,0,4:T(8,128)(2,1)}) fusion(bf16[2,16,40,8,256]{4,3,2,1,0:T(8,128)(2,1)} %slice.48, bf16[2,16,40,8,256]{4,3,2,1,0:T(8,128)(2,1)} %slice.47), kind=kLoop, calls=%fused_computation.1 | loop fusion | bytes 20971520 | tf_op jit(solution)/shard_map/stack | solution.py:99
  35.1 8.9 %maximum_bitcast_fusion = bf16[8,2,2,40,16,256]{5,4,3,2,1,0:T(8,128)(2,1)} fusion(bf16[1,2,16,40,8,256]{5,2,3,1,0,4:T(8,128)(2,1)} %get-tuple-element.29, bf16[1,2,16,40,8,256]{5,2,3,1,0,4:T(8,128)(2,1)} %get-tuple-element.30), kind=kLoop, calls=%fused_computation | loop fusion | flops 5242880 | bytes 20971520 | tf_op jit(solution)/shard_map/transpose | solution.py:100
  43.9 0.0 all-to-all-done.x_ref
  43.9 1.4 copy-done.2
  45.3 5.3 %all-to-all-start.1 = ((bf16[8,2,2,40,16,256]{5,4,3,2,1,0:T(8,128)(2,1)}), bf16[8,2,2,40,16,256]{5,4,3,2,1,0:T(8,128)(2,1)}, u32[]{:S(2)}, u32[]{:S(2)}) async-start(bf16[8,2,2,40,16,256]{5,4,3,2,1,0:T(8,128)(2,1)} %maximum_bitcast_fusion), calls=%async_computation.1 | async-start | bytes 20971520 | tf_op jit(solution)/shard_map/all_to_all | solution.py:105
  50.7 0.0 slice-start.1
  50.7 0.0 slice-start.3
  50.7 1.6 slice-done.1
  52.3 0.6 slice-done.3
  52.9 2.4 copy_bitcast_fusion.2
  55.3 2.4 maximum_bitcast_fusion.1
  57.7 8.2 %shard_map.37 = f32[2,2,8,33,128]{4,3,2,1,0:T(8,128)} custom-call(bf16[8,2,2,8,16,256]{5,4,3,2,1,0:T(8,128)(2,1)} %copy-done.2), custom_call_target="tpu_custom_call" | custom-call | tf_op jit(solution)/shard_map/pallas_call | solution.py:60
  65.9 100.2 %all-to-all-done.1.x_ref = bf16[8,2,2,40,16,256]{5,4,3,2,1,0:T(8,128)(2,1)} async-done(((bf16[8,2,2,40,16,256]{5,4,3,2,1,0:T(8,128)(2,1)}), bf16[8,2,2,40,16,256]{5,4,3,2,1,0:T(8,128)(2,1)}, u32[]{:S(2)}, u32[]{:S(2)}) %all-to-all-start.1) | async-done | bytes 10485792 | tf_op jit(solution)/shard_map/all_to_all | solution.py:105
  166.2 4.6 %all-to-all-start.2 = ((bf16[8,2,2,16,16,256]{5,4,3,2,1,0:T(8,128)(2,1)}), bf16[8,2,2,16,16,256]{5,4,3,2,1,0:T(8,128)(2,1)}, u32[]{:S(2)}, u32[]{:S(2)}) async-start(bf16[8,2,2,16,16,256]{5,4,3,2,1,0:T(8,128)(2,1)} %maximum_bitcast_fusion.1), calls=%async_computation.2 | async-start | bytes 8388608 | tf_op jit(solution)/shard_map/all_to_all | solution.py:105
  170.7 0.0 copy-done.4
  170.8 0.1 add_subtract_fusion
  170.8 0.7 fusion.2
  176.5 0.0 copy-start.3
  176.5 33.7 %shard_map.38 = f32[2,2,40,33,128]{4,3,2,1,0:T(8,128)} custom-call(bf16[8,2,2,40,16,256]{5,4,3,2,1,0:T(8,128)(2,1)} %all-to-all-done.1.x_ref), custom_call_target="tpu_custom_call" | custom-call | tf_op jit(solution)/shard_map/pallas_call | solution.py:60
  210.2 0.0 copy-done.3
  210.2 0.1 add_bitcast_fusion.7
  210.3 2.3 add_bitcast_fusion.1
  212.6 5.4 %all-to-all-done.2.x_ref = bf16[8,2,2,16,16,256]{5,4,3,2,1,0:T(8,128)(2,1)} async-done(((bf16[8,2,2,16,16,256]{5,4,3,2,1,0:T(8,128)(2,1)}), bf16[8,2,2,16,16,256]{5,4,3,2,1,0:T(8,128)(2,1)}, u32[]{:S(2)}, u32[]{:S(2)}) %all-to-all-start.2) | async-done | bytes 4194336 | tf_op jit(solution)/shard_map/all_to_all | solution.py:105
  218.0 14.6 %shard_map.39 = f32[2,2,16,33,128]{4,3,2,1,0:T(8,128)} custom-call(bf16[8,2,2,16,16,256]{5,4,3,2,1,0:T(8,128)(2,1)} %all-to-all-done.2.x_ref), custom_call_target="tpu_custom_call" | custom-call | tf_op jit(solution)/shard_map/pallas_call | solution.py:60
  232.6 1.4 add_bitcast_fusion.4
  234.0 0.1 pad_maximum_fusion
  234.1 0.2 copy.17
  234.3 5.1 %collective-permute-start = (f32[64,33,128]{2,0,1:T(8,128)S(1)}, f32[64,33,128]{2,0,1:T(8,128)S(1)}, u32[]{:S(2)}, u32[]{:S(2)}) collective-permute-start(f32[64,33,128]{2,0,1:T(8,128)S(1)} %copy.17), channel_id=1, source_target_pairs={{8,0},{16,8},{24,16},{32,24},{40,32},{48,40},{56,48},{64,56},{72,6... | collective-permute-start | bytes 3244040 | tf_op jit(solution)/shard_map/ppermute | solution.py:19
  239.4 0.0 copy-start
  239.4 0.1 pad_maximum_fusion.1
  239.5 0.2 copy.19
  239.7 4.5 %collective-permute-start.1 = (f32[64,33,128]{2,0,1:T(8,128)S(1)}, f32[64,33,128]{2,0,1:T(8,128)S(1)}, u32[]{:S(2)}, u32[]{:S(2)}) collective-permute-start(f32[64,33,128]{2,0,1:T(8,128)S(1)} %copy.19), channel_id=1, source_target_pairs={{0,8},{8,16},{16,24},{24,32},{32,40},{40,48},{48,56},{56,64},{64,7... | collective-permute-start | bytes 3244040 | tf_op jit(solution)/shard_map/ppermute | solution.py:19
  246.8 0.0 copy-done
  246.8 0.0 copy-start.1
  246.9 0.2 add_bitcast_fusion.2
  247.1 1.1 copy-done.1
  248.2 0.1 add_bitcast_fusion.5
  248.2 18.1 %collective-permute-done = f32[64,33,128]{2,0,1:T(8,128)S(1)} collective-permute-done((f32[64,33,128]{2,0,1:T(8,128)S(1)}, f32[64,33,128]{2,0,1:T(8,128)S(1)}, u32[]{:S(2)}, u32[]{:S(2)}) %collective-permute-start) | collective-permute-done | bytes 1081376 | tf_op jit(solution)/shard_map/ppermute | solution.py:19
  266.3 0.0 collective-permute-done.1
  266.3 1.2 fusion.1
  267.5 1.2 copy.21
  (5 shorter events, 0.1 us)
Async XLA Ops:
  0.0 1.2 slice-start
  0.0 1.5 slice-start.2
  4.3 39.7 %all-to-all-start = ((bf16[8,2,2,8,16,256]{5,4,3,2,1,0:T(8,128)(2,1)}), bf16[8,2,2,8,16,256]{5,4,3,2,1,0:T(8,128)(2,1)S(1)}, u32[]{:S(2)}, u32[]{:S(2)}) async-start(bf16[8,2,2,8,16,256]{5,4,3,2,1,0:T(8,128)(2,1)} %maximum_bitcast_fusion.2), calls=%async_computation | async-start | bytes 4194304 | tf_op jit(solution)/shard_map/all_to_all | solution.py:105
  43.9 1.4 copy-start.2
  45.3 120.8 %all-to-all-start.1 = ((bf16[8,2,2,40,16,256]{5,4,3,2,1,0:T(8,128)(2,1)}), bf16[8,2,2,40,16,256]{5,4,3,2,1,0:T(8,128)(2,1)}, u32[]{:S(2)}, u32[]{:S(2)}) async-start(bf16[8,2,2,40,16,256]{5,4,3,2,1,0:T(8,128)(2,1)} %maximum_bitcast_fusion), calls=%async_computation.1 | async-start | bytes 20971520 | tf_op jit(solution)/shard_map/all_to_all | solution.py:105
  50.7 1.6 slice-start.1
  50.7 2.2 slice-start.3
  65.9 104.8 %copy-start.4 = (s32[2]{0:T(128)S(1)}, s32[2]{0:T(128)}, u32[]{:S(2)}) copy-start(s32[2]{0:T(128)} %param.5) | copy-start | bytes 28
  166.2 51.8 %all-to-all-start.2 = ((bf16[8,2,2,16,16,256]{5,4,3,2,1,0:T(8,128)(2,1)}), bf16[8,2,2,16,16,256]{5,4,3,2,1,0:T(8,128)(2,1)}, u32[]{:S(2)}, u32[]{:S(2)}) async-start(bf16[8,2,2,16,16,256]{5,4,3,2,1,0:T(8,128)(2,1)} %maximum_bitcast_fusion.1), calls=%async_computation.2 | async-start | bytes 8388608 | tf_op jit(solution)/shard_map/all_to_all | solution.py:105
  176.5 33.7 %copy-start.3 = (f32[2,2,8,33,128]{4,3,2,1,0:T(8,128)S(1)}, f32[2,2,8,33,128]{4,3,2,1,0:T(8,128)}, u32[]{:S(2)}) copy-start(f32[2,2,8,33,128]{4,3,2,1,0:T(8,128)} %shard_map.37) | copy-start | bytes 1622020
  234.3 32.0 %collective-permute-start = (f32[64,33,128]{2,0,1:T(8,128)S(1)}, f32[64,33,128]{2,0,1:T(8,128)S(1)}, u32[]{:S(2)}, u32[]{:S(2)}) collective-permute-start(f32[64,33,128]{2,0,1:T(8,128)S(1)} %copy.17), channel_id=1, source_target_pairs={{8,0},{16,8},{24,16},{32,24},{40,32},{48,40},{56,48},{64,56},{72,6... | collective-permute-start | bytes 3244040 | tf_op jit(solution)/shard_map/ppermute | solution.py:19
  239.4 7.4 %copy-start = (f32[2,2,40,33,128]{4,3,2,1,0:T(8,128)S(1)}, f32[2,2,40,33,128]{4,3,2,1,0:T(8,128)}, u32[]{:S(2)}) copy-start(f32[2,2,40,33,128]{4,3,2,1,0:T(8,128)} %shard_map.38) | copy-start | bytes 8110084
  239.7 26.6 %collective-permute-start.1 = (f32[64,33,128]{2,0,1:T(8,128)S(1)}, f32[64,33,128]{2,0,1:T(8,128)S(1)}, u32[]{:S(2)}, u32[]{:S(2)}) collective-permute-start(f32[64,33,128]{2,0,1:T(8,128)S(1)} %copy.19), channel_id=1, source_target_pairs={{0,8},{8,16},{16,24},{24,32},{32,40},{40,48},{48,56},{56,64},{64,7... | collective-permute-start | bytes 3244040 | tf_op jit(solution)/shard_map/ppermute | solution.py:19
  246.8 1.3 copy-start.1

commit v9 on v8

--- a/solution.py
+++ b/solution.py
@@ -10,7 +10,7 @@
 LAGS = 33
 TILE = 128
 CB = 8
-CHUNKS = (8, 40, 16)
+CHUNKS = (8, 48, 8)
 
 
 def passed_along(block, axis, distance):

time: 269 us -> 285 us (1.059)
  waiting for transfers between devices: 124 us -> 154 us
  local copies, waits for them, and re-layouts: 36.9 us -> 25.5 us
    all_to_all x3, waiting for transfers between devices: 106 us -> 135 us  [body(): lax.all_to_all(pair, 'tm', split_axis=0, concat_axis=0, tiled=True)]
    another operation x3, local copies, waits for them, and re-layouts: 17.7 us -> 10.8 us  [body(): pair = jnp.stack([source_snap[:, :, cs], receiver_snap[:, :, cs]])]
    slice x10 -> x6, local copies, waits for them, and re-layouts: 14.4 us -> 8.98 us  [body(): pair = jnp.stack([source_snap[:, :, cs], receiver_snap[:, :, cs]])]
    transpose x3, other arithmetic: 12.8 us -> 8.32 us  [body(): pair = jnp.transpose(pair, (4, 0, 1, 3, 2, 5))]
  transfers between devices with their start and end apart: 5 -> 5, of which waited for: 3 -> 4; matrix products, arithmetic and copies ran while one was open for 16% -> 8% of each run, Pallas kernels for 16% -> 17%
where the time goes in v9:
time: 285 us; the launch traced here: 284 us
  waiting for transfers between devices  154 us (54%)
  Pallas kernels  56.5 us (20%)
  local copies, waits for them, and re-layouts  25.5 us (9%)
  starting transfers between devices  24.3 us (9%)
  other arithmetic  16.5 us (6%)
  between operations  7.67 us (3%)
    all_to_all x3, waiting for transfers between devices, body(): lax.all_to_all(pair, 'tm', split_axis=0, concat_axis=0, tiled=True)  135 us
    pallas_call x3, Pallas kernels, lag_images(): pl.pallas_call(lag_kernel, grid=(shots, chans // cb), in_specs=[pl.BlockS...  56.5 us
    ppermute x2, waiting for transfers between devices, passed_along(): return lax.ppermute(block, axis, route)  19.1 us
    all_to_all x3, starting transfers between devices, body(): lax.all_to_all(pair, 'tm', split_axis=0, concat_axis=0, tiled=True)  16 us
    another operation x3, local copies, waits for them, and re-layouts, body(): pair = jnp.stack([source_snap[:, :, cs], receiver_snap[:, :, cs]])  10.8 us
    slice x6, local copies, waits for them, and re-layouts, body(): pair = jnp.stack([source_snap[:, :, cs], receiver_snap[:, :, cs]])  8.98 us
    ppermute x2, starting transfers between devices, passed_along(): return lax.ppermute(block, axis, route)  8.33 us
    transpose x3, other arithmetic, body(): pair = jnp.transpose(pair, (4, 0, 1, 3, 2, 5))  8.32 us
  transfers between devices with their start and end apart: 5, of which 4 were waited for; matrix products, arithmetic and copies ran while one was open for 8% of the time, Pallas kernels for 17%

profile of v9, /device:TPU:3, one launch (start us, length us, event | category | flops | bytes accessed | tf_op | source)
XLA Modules:
  0.0 284.2 jit_solution(7186824618416876377)
XLA Ops:
  0.0 1.7 fusion.3
  1.7 2.7 fusion.2
  4.4 1.2 copy_bitcast_fusion.2
  5.6 1.5 maximum_bitcast_fusion.2
  7.1 6.0 %all-to-all-start = ((bf16[8,2,2,8,16,256]{5,4,3,2,1,0:T(8,128)(2,1)}), bf16[8,2,2,8,16,256]{5,4,3,2,1,0:T(8,128)(2,1)S(1)}, u32[]{:S(2)}, u32[]{:S(2)}) async-start(bf16[8,2,2,8,16,256]{5,4,3,2,1,0:T(8,128)(2,1)} %maximum_bitcast_fusion.2), calls=%async_computation | async-start | bytes 4194304 | tf_op jit(solution)/shard_map/all_to_all | solution.py:105
  13.1 0.0 slice-start
  13.2 0.0 slice-start.1
  13.2 2.8 slice-done
  15.9 1.8 slice-done.1
  17.8 7.2 %copy_bitcast_fusion = (bf16[1,2,16,48,8,256]{5,2,3,1,0,4:T(8,128)(2,1)S(1)}, bf16[1,2,16,48,8,256]{5,2,3,1,0,4:T(8,128)(2,1)S(1)}) fusion(bf16[2,16,48,8,256]{4,3,2,1,0:T(8,128)(2,1)S(1)} %slice-done, bf16[2,16,48,8,256]{4,3,2,1,0:T(8,128)(2,1)S(1)} %slice-done.1), kind=kLoop, calls=%fused_computation.1 | loop fusion | bytes 25165824 | tf_op jit(solution)/shard_map/stack | solution.py:99
  25.0 5.2 %maximum_bitcast_fusion = bf16[8,2,2,48,16,256]{5,4,3,2,1,0:T(8,128)(2,1)} fusion(bf16[1,2,16,48,8,256]{5,2,3,1,0,4:T(8,128)(2,1)S(1)} %get-tuple-element.33, bf16[1,2,16,48,8,256]{5,2,3,1,0,4:T(8,128)(2,1)S(1)} %get-tuple-element.34), kind=kLoop, calls=%fused_computation | loop fusion | flops 6291456 | bytes 25165824 | tf_op jit(solution)/shard_map/transpose | solution.py:100
  30.2 9.1 %all-to-all-done.x_ref = bf16[8,2,2,8,16,256]{5,4,3,2,1,0:T(8,128)(2,1)S(1)} async-done(((bf16[8,2,2,8,16,256]{5,4,3,2,1,0:T(8,128)(2,1)}), bf16[8,2,2,8,16,256]{5,4,3,2,1,0:T(8,128)(2,1)S(1)}, u32[]{:S(2)}, u32[]{:S(2)}) %all-to-all-start) | async-done | bytes 2097184 | tf_op jit(solution)/shard_map/all_to_all | solution.py:105
  39.3 1.3 copy-done.2
  40.6 5.4 %all-to-all-start.1 = ((bf16[8,2,2,48,16,256]{5,4,3,2,1,0:T(8,128)(2,1)}), bf16[8,2,2,48,16,256]{5,4,3,2,1,0:T(8,128)(2,1)}, u32[]{:S(2)}, u32[]{:S(2)}) async-start(bf16[8,2,2,48,16,256]{5,4,3,2,1,0:T(8,128)(2,1)} %maximum_bitcast_fusion), calls=%async_computation.1 | async-start | bytes 25165824 | tf_op jit(solution)/shard_map/all_to_all | solution.py:105
  46.0 2.4 copy_bitcast_fusion.4
  48.4 1.6 maximum_bitcast_fusion.1
  50.0 8.2 %shard_map.37 = f32[2,2,8,33,128]{4,3,2,1,0:T(8,128)} custom-call(bf16[8,2,2,8,16,256]{5,4,3,2,1,0:T(8,128)(2,1)} %copy-done.2), custom_call_target="tpu_custom_call" | custom-call | tf_op jit(solution)/shard_map/pallas_call | solution.py:60
  58.2 125.4 %all-to-all-done.1.x_ref = bf16[8,2,2,48,16,256]{5,4,3,2,1,0:T(8,128)(2,1)} async-done(((bf16[8,2,2,48,16,256]{5,4,3,2,1,0:T(8,128)(2,1)}), bf16[8,2,2,48,16,256]{5,4,3,2,1,0:T(8,128)(2,1)}, u32[]{:S(2)}, u32[]{:S(2)}) %all-to-all-start.1) | async-done | bytes 12582944 | tf_op jit(solution)/shard_map/all_to_all | solution.py:105
  183.6 4.6 %all-to-all-start.2 = ((bf16[8,2,2,8,16,256]{5,4,3,2,1,0:T(8,128)(2,1)}), bf16[8,2,2,8,16,256]{5,4,3,2,1,0:T(8,128)(2,1)S(1)}, u32[]{:S(2)}, u32[]{:S(2)}) async-start(bf16[8,2,2,8,16,256]{5,4,3,2,1,0:T(8,128)(2,1)} %maximum_bitcast_fusion.1), calls=%async_computation.2 | async-start | bytes 4194304 | tf_op jit(solution)/shard_map/all_to_all | solution.py:105
  188.2 0.0 copy-done.6
  188.2 0.1 add_subtract_fusion
  188.3 0.6 fusion.4
  193.9 0.0 copy-start.4
  193.9 40.0 %shard_map.38 = f32[2,2,48,33,128]{4,3,2,1,0:T(8,128)} custom-call(bf16[8,2,2,48,16,256]{5,4,3,2,1,0:T(8,128)(2,1)} %all-to-all-done.1.x_ref), custom_call_target="tpu_custom_call" | custom-call | tf_op jit(solution)/shard_map/pallas_call | solution.py:60
  233.9 0.0 copy-done.4
  233.9 0.1 add_bitcast_fusion.6
  234.0 3.8 %add_bitcast_fusion.1 = (f32[48,33,128]{2,1,0:T(8,128)}, f32[48,33,128]{2,1,0:T(8,128)}) fusion(f32[2,2,48,33,128]{4,3,2,1,0:T(8,128)} %shard_map.38, pred[]{:T(512)} %bitcast.19, pred[]{:T(512)} %bitcast.18, pred[]{:T(512)} %bitcast.17, pred[]{:T(512)} %bitcast.16, pred[]{:T(512)} %bitcast.26, pred[]{:T(512)} %bitcast.25, pred[]{:T(512)} %bitcast.24, ...), kind=kLoop, calls=%fused_computation.15 | loop fusion | flops 2838528 | bytes 4866056 | tf_op jit(solution)/shard_map/add | solution.py:79
  237.8 0.0 all-to-all-done.2.x_ref
  237.8 1.3 copy-done.1
  239.2 8.2 %shard_map.39 = f32[2,2,8,33,128]{4,3,2,1,0:T(8,128)} custom-call(bf16[8,2,2,8,16,256]{5,4,3,2,1,0:T(8,128)(2,1)} %copy-done.1), custom_call_target="tpu_custom_call" | custom-call | tf_op jit(solution)/shard_map/pallas_call | solution.py:60
  247.4 1.2 add_bitcast_fusion.5
  248.6 0.0 copy-start.5
  248.7 1.4 pad_maximum_fusion.1
  250.0 0.2 copy.19
  250.3 6.2 %collective-permute-start.1 = (f32[64,33,128]{2,0,1:T(8,128)S(1)}, f32[64,33,128]{2,0,1:T(8,128)S(1)}, u32[]{:S(2)}, u32[]{:S(2)}) collective-permute-start(f32[64,33,128]{2,0,1:T(8,128)S(1)} %copy.19), channel_id=1, source_target_pairs={{0,8},{8,16},{16,24},{24,32},{32,40},{40,48},{48,56},{56,64},{64,7... | collective-permute-start | bytes 3244040 | tf_op jit(solution)/shard_map/ppermute | solution.py:19
  256.4 0.0 copy-done.5
  256.4 0.0 copy-start
  256.4 0.1 pad_maximum_fusion
  256.5 0.2 copy.17
  256.7 2.2 collective-permute-start
  261.5 0.0 copy-done
  261.5 0.0 copy-start.3
  261.5 0.2 add_bitcast_fusion.2
  261.7 0.8 copy-done.3
  262.6 17.4 %collective-permute-done.1 = f32[64,33,128]{2,0,1:T(8,128)S(1)} collective-permute-done((f32[64,33,128]{2,0,1:T(8,128)S(1)}, f32[64,33,128]{2,0,1:T(8,128)S(1)}, u32[]{:S(2)}, u32[]{:S(2)}) %collective-permute-start.1) | collective-permute-done | bytes 1081376 | tf_op jit(solution)/shard_map/ppermute | solution.py:19
  280.1 1.7 collective-permute-done
  281.8 1.2 fusion.1
  283.0 1.2 copy.21
  (5 shorter events, 0.1 us)
Async XLA Ops:
  7.1 32.2 %all-to-all-start = ((bf16[8,2,2,8,16,256]{5,4,3,2,1,0:T(8,128)(2,1)}), bf16[8,2,2,8,16,256]{5,4,3,2,1,0:T(8,128)(2,1)S(1)}, u32[]{:S(2)}, u32[]{:S(2)}) async-start(bf16[8,2,2,8,16,256]{5,4,3,2,1,0:T(8,128)(2,1)} %maximum_bitcast_fusion.2), calls=%async_computation | async-start | bytes 4194304 | tf_op jit(solution)/shard_map/all_to_all | solution.py:105
  13.1 2.8 slice-start
  13.2 4.6 %slice-start.1 = ((bf16[2,16,64,8,256]{4,3,2,1,0:T(8,128)(2,1)}), bf16[2,16,48,8,256]{4,3,2,1,0:T(8,128)(2,1)S(1)}, s32[]{:S(2)}) async-start(bf16[2,16,64,8,256]{4,3,2,1,0:T(8,128)(2,1)} %param.3), calls=%async_computation.4 | async-start | bytes 12582912 | tf_op jit(solution)/shard_map/slice | solution.py:99
  39.3 1.3 copy-start.2
  40.6 143.0 %all-to-all-start.1 = ((bf16[8,2,2,48,16,256]{5,4,3,2,1,0:T(8,128)(2,1)}), bf16[8,2,2,48,16,256]{5,4,3,2,1,0:T(8,128)(2,1)}, u32[]{:S(2)}, u32[]{:S(2)}) async-start(bf16[8,2,2,48,16,256]{5,4,3,2,1,0:T(8,128)(2,1)} %maximum_bitcast_fusion), calls=%async_computation.1 | async-start | bytes 25165824 | tf_op jit(solution)/shard_map/all_to_all | solution.py:105
  58.2 130.0 %copy-start.6 = (s32[2]{0:T(128)S(1)}, s32[2]{0:T(128)}, u32[]{:S(2)}) copy-start(s32[2]{0:T(128)} %param.5) | copy-start | bytes 28
  183.6 54.2 %all-to-all-start.2 = ((bf16[8,2,2,8,16,256]{5,4,3,2,1,0:T(8,128)(2,1)}), bf16[8,2,2,8,16,256]{5,4,3,2,1,0:T(8,128)(2,1)S(1)}, u32[]{:S(2)}, u32[]{:S(2)}) async-start(bf16[8,2,2,8,16,256]{5,4,3,2,1,0:T(8,128)(2,1)} %maximum_bitcast_fusion.1), calls=%async_computation.2 | async-start | bytes 4194304 | tf_op jit(solution)/shard_map/all_to_all | solution.py:105
  193.9 40.0 %copy-start.4 = (f32[2,2,8,33,128]{4,3,2,1,0:T(8,128)S(1)}, f32[2,2,8,33,128]{4,3,2,1,0:T(8,128)}, u32[]{:S(2)}) copy-start(f32[2,2,8,33,128]{4,3,2,1,0:T(8,128)} %shard_map.37) | copy-start | bytes 1622020
  237.8 1.3 copy-start.1
  248.6 7.8 %copy-start.5 = (f32[48,33,128]{2,1,0:T(8,128)S(1)}, f32[48,33,128]{2,1,0:T(8,128)}, u32[]{:S(2)}) copy-start(f32[48,33,128]{2,1,0:T(8,128)} %get-tuple-element.21) | copy-start | bytes 2433028
  250.3 29.8 %collective-permute-start.1 = (f32[64,33,128]{2,0,1:T(8,128)S(1)}, f32[64,33,128]{2,0,1:T(8,128)S(1)}, u32[]{:S(2)}, u32[]{:S(2)}) collective-permute-start(f32[64,33,128]{2,0,1:T(8,128)S(1)} %copy.19), channel_id=1, source_target_pairs={{0,8},{8,16},{16,24},{24,32},{32,40},{40,48},{48,56},{56,64},{64,7... | collective-permute-start | bytes 3244040 | tf_op jit(solution)/shard_map/ppermute | solution.py:19
  256.4 5.1 %copy-start = (f32[2,2,48,33,128]{4,3,2,1,0:T(8,128)S(1)}, f32[2,2,48,33,128]{4,3,2,1,0:T(8,128)}, u32[]{:S(2)}) copy-start(f32[2,2,48,33,128]{4,3,2,1,0:T(8,128)} %shard_map.38) | copy-start | bytes 9732100
  256.7 25.0 %collective-permute-start = (f32[64,33,128]{2,0,1:T(8,128)S(1)}, f32[64,33,128]{2,0,1:T(8,128)S(1)}, u32[]{:S(2)}, u32[]{:S(2)}) collective-permute-start(f32[64,33,128]{2,0,1:T(8,128)S(1)} %copy.17), channel_id=1, source_target_pairs={{8,0},{16,8},{24,16},{32,24},{40,32},{48,40},{56,48},{64,56},{72,6... | collective-permute-start | bytes 3244040 | tf_op jit(solution)/shard_map/ppermute | solution.py:19
  261.5 1.1 copy-start.3

commit v10 on v8

--- a/solution.py
+++ b/solution.py
@@ -81,13 +81,6 @@
     return out
 
 
-def flipped(x):
-    width = x.shape[-1]
-    i = jnp.arange(width, dtype=jnp.int32)
-    anti = (i[:, None] + i[None, :] == width - 1).astype(x.dtype)
-    return jnp.dot(x, anti, preferred_element_type=jnp.float32).astype(x.dtype)
-
-
 def body(source_snap, receiver_snap, start_tile):
     owner = lax.axis_index("space")
     images = []
@@ -105,12 +98,16 @@
         received.append(lax.all_to_all(pair, "tm", split_axis=0, concat_axis=0, tiled=True))
         if g >= 1:
             images.append(lag_images(received[g - 1]))
-    images.append(lag_images(received[-1]))
-    placed = [place_tiles(image, start_tile, owner - 1, 3) for image in images]
-    slots = [jnp.concatenate([p[k] for p in placed], axis=0) for k in range(3)]
-    right_part = passed_along(slots[0], "space", -1)
-    left_part = passed_along(slots[2], "space", 1)
-    return (slots[1] + right_part + left_part)[None]
+    early = [place_tiles(image, start_tile, owner - 1, 3) for image in images]
+    early = [jnp.concatenate([p[k] for p in early], axis=0) for k in range(3)]
+    early, received[-1] = lax.optimization_barrier((early, received[-1]))
+    parts = [early, place_tiles(lag_images(received[-1]), start_tile, owner - 1, 3)]
+    out = []
+    for slots in parts:
+        right_part = passed_along(slots[0], "space", -1)
+        left_part = passed_along(slots[2], "space", 1)
+        out.append(slots[1] + right_part + left_part)
+    return jnp.concatenate(out, axis=0)[None]
 
 
 def solution(mesh):

time: 269 us -> 263 us (0.978)
  waiting for transfers between devices: 124 us -> 105 us
  starting transfers between devices: 25.6 us -> 32.5 us
    ppermute x2 -> x4, waiting for transfers between devices: 18.1 us -> 5.07 us  [passed_along(): return lax.ppermute(block, axis, route)]
    ppermute x2 -> x4, starting transfers between devices: 9.62 us -> 16.5 us  [passed_along(): return lax.ppermute(block, axis, route)]
    all_to_all x3, waiting for transfers between devices: 106 us -> 100 us  [body(): lax.all_to_all(pair, 'tm', split_axis=0, concat_axis=0, tiled=True)]
  transfers between devices with their start and end apart: 5 -> 7, of which waited for: 3 -> 4; matrix products, arithmetic and copies ran while one was open for 16% -> 18% of each run, Pallas kernels for 16% -> 22%
where the time goes in v10:
time: 263 us; the launch traced here: 260 us
  waiting for transfers between devices  105 us (40%)
  Pallas kernels  56.5 us (21%)
  local copies, waits for them, and re-layouts  37.7 us (14%)
  starting transfers between devices  32.5 us (12%)
  other arithmetic  20.2 us (8%)
  between operations  7.96 us (3%)
    all_to_all x3, waiting for transfers between devices, body(): lax.all_to_all(pair, 'tm', split_axis=0, concat_axis=0, tiled=True)  100 us
    pallas_call x3, Pallas kernels, lag_images(): pl.pallas_call(lag_kernel, grid=(shots, chans // cb), in_specs=[pl.BlockS...  56.5 us
    another operation x3, local copies, waits for them, and re-layouts, body(): pair = jnp.stack([source_snap[:, :, cs], receiver_snap[:, :, cs]])  17.7 us
    ppermute x4, starting transfers between devices, passed_along(): return lax.ppermute(block, axis, route)  16.5 us
    all_to_all x3, starting transfers between devices, body(): lax.all_to_all(pair, 'tm', split_axis=0, concat_axis=0, tiled=True)  16 us
    slice x10, local copies, waits for them, and re-layouts, body(): pair = jnp.stack([source_snap[:, :, cs], receiver_snap[:, :, cs]])  14.4 us
    transpose x3, other arithmetic, body(): pair = jnp.transpose(pair, (4, 0, 1, 3, 2, 5))  12.8 us
  transfers between devices with their start and end apart: 7, of which 4 were waited for; matrix products, arithmetic and copies ran while one was open for 18% of the time, Pallas kernels for 22%

profile of v10, /device:TPU:3, one launch (start us, length us, event | category | flops | bytes accessed | tf_op | source)
XLA Modules:
  0.0 260.3 jit_solution(13470427298492838375)
XLA Ops:
  0.0 1.2 slice-done
  1.2 0.3 slice-done.2
  1.5 1.2 copy_bitcast_fusion.4
  2.7 1.5 maximum_bitcast_fusion.2
  4.3 6.0 %all-to-all-start = ((bf16[8,2,2,8,16,256]{5,4,3,2,1,0:T(8,128)(2,1)}), bf16[8,2,2,8,16,256]{5,4,3,2,1,0:T(8,128)(2,1)S(1)}, u32[]{:S(2)}, u32[]{:S(2)}) async-start(bf16[8,2,2,8,16,256]{5,4,3,2,1,0:T(8,128)(2,1)} %maximum_bitcast_fusion.2), calls=%async_computation | async-start | bytes 4194304 | tf_op jit(solution)/shard_map/all_to_all | solution.py:98
  10.3 5.3 %slice.47 = bf16[2,16,40,8,256]{4,3,2,1,0:T(8,128)(2,1)} slice(bf16[2,16,64,8,256]{4,3,2,1,0:T(8,128)(2,1)} %param.3), slice={[0:2], [0:16], [8:48], [0:8], [0:256]} | slice | bytes 10485760 | tf_op jit(solution)/shard_map/slice | solution.py:92
  15.6 5.4 %slice.48 = bf16[2,16,40,8,256]{4,3,2,1,0:T(8,128)(2,1)} slice(bf16[2,16,64,8,256]{4,3,2,1,0:T(8,128)(2,1)} %param.4), slice={[0:2], [0:16], [8:48], [0:8], [0:256]} | slice | bytes 10485760 | tf_op jit(solution)/shard_map/slice | solution.py:92
  21.0 14.1 %copy_bitcast_fusion = (bf16[1,2,16,40,8,256]{5,2,3,1,0,4:T(8,128)(2,1)}, bf16[1,2,16,40,8,256]{5,2,3,1,0,4:T(8,128)(2,1)}) fusion(bf16[2,16,40,8,256]{4,3,2,1,0:T(8,128)(2,1)} %slice.48, bf16[2,16,40,8,256]{4,3,2,1,0:T(8,128)(2,1)} %slice.47), kind=kLoop, calls=%fused_computation.1 | loop fusion | bytes 20971520 | tf_op jit(solution)/shard_map/stack | solution.py:92
  35.1 8.9 %maximum_bitcast_fusion = bf16[8,2,2,40,16,256]{5,4,3,2,1,0:T(8,128)(2,1)} fusion(bf16[1,2,16,40,8,256]{5,2,3,1,0,4:T(8,128)(2,1)} %get-tuple-element.37, bf16[1,2,16,40,8,256]{5,2,3,1,0,4:T(8,128)(2,1)} %get-tuple-element.38), kind=kLoop, calls=%fused_computation | loop fusion | flops 5242880 | bytes 20971520 | tf_op jit(solution)/shard_map/transpose | solution.py:93
  43.9 0.0 all-to-all-done.x_ref
  43.9 1.4 copy-done.1
  45.3 5.3 %all-to-all-start.1 = ((bf16[8,2,2,40,16,256]{5,4,3,2,1,0:T(8,128)(2,1)}), bf16[8,2,2,40,16,256]{5,4,3,2,1,0:T(8,128)(2,1)}, u32[]{:S(2)}, u32[]{:S(2)}) async-start(bf16[8,2,2,40,16,256]{5,4,3,2,1,0:T(8,128)(2,1)} %maximum_bitcast_fusion), calls=%async_computation.1 | async-start | bytes 20971520 | tf_op jit(solution)/shard_map/all_to_all | solution.py:98
  50.6 0.0 slice-start.1
  50.7 0.0 slice-start.3
  50.7 1.6 slice-done.1
  52.2 0.6 slice-done.3
  52.9 2.4 copy_bitcast_fusion.2
  55.3 2.4 maximum_bitcast_fusion.1
  57.7 8.2 %shard_map.37 = f32[2,2,8,33,128]{4,3,2,1,0:T(8,128)} custom-call(bf16[8,2,2,8,16,256]{5,4,3,2,1,0:T(8,128)(2,1)} %copy-done.1), custom_call_target="tpu_custom_call" | custom-call | tf_op jit(solution)/shard_map/pallas_call | solution.py:60
  65.9 100.2 %all-to-all-done.1.x_ref = bf16[8,2,2,40,16,256]{5,4,3,2,1,0:T(8,128)(2,1)} async-done(((bf16[8,2,2,40,16,256]{5,4,3,2,1,0:T(8,128)(2,1)}), bf16[8,2,2,40,16,256]{5,4,3,2,1,0:T(8,128)(2,1)}, u32[]{:S(2)}, u32[]{:S(2)}) %all-to-all-start.1) | async-done | bytes 10485792 | tf_op jit(solution)/shard_map/all_to_all | solution.py:98
  166.2 4.6 %all-to-all-start.2 = ((bf16[8,2,2,16,16,256]{5,4,3,2,1,0:T(8,128)(2,1)}), bf16[8,2,2,16,16,256]{5,4,3,2,1,0:T(8,128)(2,1)}, u32[]{:S(2)}, u32[]{:S(2)}) async-start(bf16[8,2,2,16,16,256]{5,4,3,2,1,0:T(8,128)(2,1)} %maximum_bitcast_fusion.1), calls=%async_computation.2 | async-start | bytes 8388608 | tf_op jit(solution)/shard_map/all_to_all | solution.py:98
  170.7 0.1 add_subtract_fusion
  170.8 0.7 fusion.1
  179.3 0.0 copy-start.2
  179.3 33.7 %shard_map.38 = f32[2,2,40,33,128]{4,3,2,1,0:T(8,128)} custom-call(bf16[8,2,2,40,16,256]{5,4,3,2,1,0:T(8,128)(2,1)} %all-to-all-done.1.x_ref), custom_call_target="tpu_custom_call" | custom-call | tf_op jit(solution)/shard_map/pallas_call | solution.py:60
  213.0 0.1 add_bitcast_fusion.5
  213.1 2.3 add_bitcast_fusion
  215.3 0.1 pad_maximum_fusion.2
  215.4 1.0 pad_maximum_fusion.1
  216.5 1.1 copy-done
  217.6 0.2 add_bitcast_fusion.2
  217.8 0.1 pad_maximum_fusion
  217.9 0.1 all-to-all-done.2.x_ref
  218.0 0.2 copy.17
  218.2 5.1 %collective-permute-start = (f32[48,33,128]{2,0,1:T(8,128)S(1)}, f32[48,33,128]{2,0,1:T(8,128)S(1)}, u32[]{:S(2)}, u32[]{:S(2)}) collective-permute-start(f32[48,33,128]{2,0,1:T(8,128)S(1)} %copy.17), channel_id=1, source_target_pairs={{8,0},{16,8},{24,16},{32,24},{40,32},{48,40},{56,48},{64,56},{72,6... | collective-permute-start | bytes 2433032 | tf_op jit(solution)/shard_map/ppermute | solution.py:19
  223.2 1.0 copy.19
  224.3 4.4 %collective-permute-start.1 = (f32[48,33,128]{2,0,1:T(8,128)}, f32[48,33,128]{2,0,1:T(8,128)S(1)}, u32[]{:S(2)}, u32[]{:S(2)}) collective-permute-start(f32[48,33,128]{2,0,1:T(8,128)} %copy.19), channel_id=1, source_target_pairs={{0,8},{8,16},{16,24},{24,32},{32,40},{40,48},{48,56},{56,64},{64,7... | collective-permute-start | bytes 2433032 | tf_op jit(solution)/shard_map/ppermute | solution.py:19
  228.7 14.6 %shard_map.39 = f32[2,2,16,33,128]{4,3,2,1,0:T(8,128)} custom-call(bf16[8,2,2,16,16,256]{5,4,3,2,1,0:T(8,128)(2,1)} %all-to-all-done.2.x_ref), custom_call_target="tpu_custom_call" | custom-call | tf_op jit(solution)/shard_map/pallas_call | solution.py:60
  243.3 1.5 add_bitcast_fusion.4
  244.8 1.9 collective-permute-start.2
  246.8 5.1 %collective-permute-start.3 = (f32[16,33,128]{2,1,0:T(8,128)S(1)}, f32[16,33,128]{2,1,0:T(8,128)S(1)}, u32[]{:S(2)}, u32[]{:S(2)}) collective-permute-start(f32[16,33,128]{2,1,0:T(8,128)S(1)} %get-tuple-element.28), channel_id=1, source_target_pairs={{0,8},{8,16},{16,24},{24,32},{32,40},{40,48},{48,56},{56,64},{64,7... | collective-permute-start | bytes 811016 | tf_op jit(solution)/shard_map/ppermute | solution.py:19
  251.9 2.8 %collective-permute-done.2 = f32[16,33,128]{2,1,0:T(8,128)S(1)} collective-permute-done((f32[16,33,128]{2,1,0:T(8,128)S(1)}, f32[16,33,128]{2,1,0:T(8,128)S(1)}, u32[]{:S(2)}, u32[]{:S(2)}) %collective-permute-start.2) | collective-permute-done | bytes 270368 | tf_op jit(solution)/shard_map/ppermute | solution.py:19
  254.7 2.2 collective-permute-done.3
  257.0 1.4 fusion
  258.4 0.0 collective-permute-done
  258.4 0.6 copy_add_fusion
  259.0 0.1 maximum_bitcast_fusion.3
  259.1 1.2 copy.21
  (11 shorter events, 0.1 us)
Async XLA Ops:
  0.0 1.2 slice-start
  0.0 1.5 slice-start.2
  4.3 39.6 %all-to-all-start = ((bf16[8,2,2,8,16,256]{5,4,3,2,1,0:T(8,128)(2,1)}), bf16[8,2,2,8,16,256]{5,4,3,2,1,0:T(8,128)(2,1)S(1)}, u32[]{:S(2)}, u32[]{:S(2)}) async-start(bf16[8,2,2,8,16,256]{5,4,3,2,1,0:T(8,128)(2,1)} %maximum_bitcast_fusion.2), calls=%async_computation | async-start | bytes 4194304 | tf_op jit(solution)/shard_map/all_to_all | solution.py:98
  43.9 1.4 copy-start.1
  45.3 120.9 %all-to-all-start.1 = ((bf16[8,2,2,40,16,256]{5,4,3,2,1,0:T(8,128)(2,1)}), bf16[8,2,2,40,16,256]{5,4,3,2,1,0:T(8,128)(2,1)}, u32[]{:S(2)}, u32[]{:S(2)}) async-start(bf16[8,2,2,40,16,256]{5,4,3,2,1,0:T(8,128)(2,1)} %maximum_bitcast_fusion), calls=%async_computation.1 | async-start | bytes 20971520 | tf_op jit(solution)/shard_map/all_to_all | solution.py:98
  50.6 1.6 slice-start.1
  50.7 2.2 slice-start.3
  65.9 104.8 %copy-start.4 = (s32[2]{0:T(128)S(1)}, s32[2]{0:T(128)}, u32[]{:S(2)}) copy-start(s32[2]{0:T(128)} %param.5) | copy-start | bytes 28
  166.2 51.9 %all-to-all-start.2 = ((bf16[8,2,2,16,16,256]{5,4,3,2,1,0:T(8,128)(2,1)}), bf16[8,2,2,16,16,256]{5,4,3,2,1,0:T(8,128)(2,1)}, u32[]{:S(2)}, u32[]{:S(2)}) async-start(bf16[8,2,2,16,16,256]{5,4,3,2,1,0:T(8,128)(2,1)} %maximum_bitcast_fusion.1), calls=%async_computation.2 | async-start | bytes 8388608 | tf_op jit(solution)/shard_map/all_to_all | solution.py:98
  179.3 33.7 %copy-start.2 = (f32[2,2,8,33,128]{4,3,2,1,0:T(8,128)S(1)}, f32[2,2,8,33,128]{4,3,2,1,0:T(8,128)}, u32[]{:S(2)}) copy-start(f32[2,2,8,33,128]{4,3,2,1,0:T(8,128)} %shard_map.37) | copy-start | bytes 1622020
  215.3 2.3 copy-start
  218.2 40.2 %collective-permute-start = (f32[48,33,128]{2,0,1:T(8,128)S(1)}, f32[48,33,128]{2,0,1:T(8,128)S(1)}, u32[]{:S(2)}, u32[]{:S(2)}) collective-permute-start(f32[48,33,128]{2,0,1:T(8,128)S(1)} %copy.17), channel_id=1, source_target_pairs={{8,0},{16,8},{24,16},{32,24},{40,32},{48,40},{56,48},{64,56},{72,6... | collective-permute-start | bytes 2433032 | tf_op jit(solution)/shard_map/ppermute | solution.py:19
  224.3 34.2 %collective-permute-start.1 = (f32[48,33,128]{2,0,1:T(8,128)}, f32[48,33,128]{2,0,1:T(8,128)S(1)}, u32[]{:S(2)}, u32[]{:S(2)}) collective-permute-start(f32[48,33,128]{2,0,1:T(8,128)} %copy.19), channel_id=1, source_target_pairs={{0,8},{8,16},{16,24},{24,32},{32,40},{40,48},{48,56},{56,64},{64,7... | collective-permute-start | bytes 2433032 | tf_op jit(solution)/shard_map/ppermute | solution.py:19
  243.3 15.1 %copy-start.3 = (f32[48,33,128]{2,1,0:T(8,128)S(1)}, f32[48,33,128]{2,1,0:T(8,128)}, u32[]{:S(2)}) copy-start(f32[48,33,128]{2,1,0:T(8,128)} %pad_maximum_fusion.1) | copy-start | bytes 2433028
  244.8 9.9 %collective-permute-start.2 = (f32[16,33,128]{2,1,0:T(8,128)S(1)}, f32[16,33,128]{2,1,0:T(8,128)S(1)}, u32[]{:S(2)}, u32[]{:S(2)}) collective-permute-start(f32[16,33,128]{2,1,0:T(8,128)S(1)} %get-tuple-element.27), channel_id=1, source_target_pairs={{8,0},{16,8},{24,16},{32,24},{40,32},{48,40},{56,48},{64,56},{72,6... | collective-permute-start | bytes 811016 | tf_op jit(solution)/shard_map/ppermute | solution.py:19
  246.8 10.2 %collective-permute-start.3 = (f32[16,33,128]{2,1,0:T(8,128)S(1)}, f32[16,33,128]{2,1,0:T(8,128)S(1)}, u32[]{:S(2)}, u32[]{:S(2)}) collective-permute-start(f32[16,33,128]{2,1,0:T(8,128)S(1)} %get-tuple-element.28), channel_id=1, source_target_pairs={{0,8},{8,16},{16,24},{24,32},{32,40},{40,48},{48,56},{56,64},{64,7... | collective-permute-start | bytes 811016 | tf_op jit(solution)/shard_map/ppermute | solution.py:19

commit v11 on v10

--- a/solution.py
+++ b/solution.py
@@ -10,7 +10,7 @@
 LAGS = 33
 TILE = 128
 CB = 8
-CHUNKS = (8, 40, 16)
+CHUNKS = (16, 40, 8)
 
 
 def passed_along(block, axis, distance):

time: 263 us -> 276 us (1.049)
  waiting for transfers between devices: 105 us -> 116 us
  other arithmetic: 20.2 us -> 23.3 us
    all_to_all x3, waiting for transfers between devices: 100 us -> 111 us  [body(): lax.all_to_all(pair, 'tm', split_axis=0, concat_axis=0, tiled=True)]
    optimization_barrier x2, local copies, waits for them, and re-layouts: 1.19 us -> 4.27 us  [body(): early, received[-1] = lax.optimization_barrier((early, received[-1]))]
  transfers between devices with their start and end apart: 7 -> 7, of which waited for: 4 -> 4; matrix products, arithmetic and copies ran while one was open for 18% -> 17% of each run, Pallas kernels for 22% -> 21%
where the time goes in v11:
time: 276 us; the launch traced here: 273 us
  waiting for transfers between devices  116 us (42%)
  Pallas kernels  56.5 us (20%)
  local copies, waits for them, and re-layouts  39.3 us (14%)
  starting transfers between devices  31.2 us (11%)
  other arithmetic  23.3 us (8%)
  between operations  7.29 us (3%)
    all_to_all x3, waiting for transfers between devices, body(): lax.all_to_all(pair, 'tm', split_axis=0, concat_axis=0, tiled=True)  111 us
    pallas_call x3, Pallas kernels, lag_images(): pl.pallas_call(lag_kernel, grid=(shots, chans // cb), in_specs=[pl.BlockS...  56.5 us
    another operation x3, local copies, waits for them, and re-layouts, body(): pair = jnp.stack([source_snap[:, :, cs], receiver_snap[:, :, cs]])  17.7 us
    all_to_all x3, starting transfers between devices, body(): lax.all_to_all(pair, 'tm', split_axis=0, concat_axis=0, tiled=True)  16 us
    ppermute x4, starting transfers between devices, passed_along(): return lax.ppermute(block, axis, route)  15.2 us
    slice x10, local copies, waits for them, and re-layouts, body(): pair = jnp.stack([source_snap[:, :, cs], receiver_snap[:, :, cs]])  14.4 us
    transpose x3, other arithmetic, body(): pair = jnp.transpose(pair, (4, 0, 1, 3, 2, 5))  12.8 us
  transfers between devices with their start and end apart: 7, of which 4 were waited for; matrix products, arithmetic and copies ran while one was open for 17% of the time, Pallas kernels for 21%

profile of v11, /device:TPU:3, one launch (start us, length us, event | category | flops | bytes accessed | tf_op | source)
XLA Modules:
  0.0 273.4 jit_solution(10308623943171027165)
XLA Ops:
  0.0 1.6 slice-done
  1.6 0.6 slice-done.2
  2.2 2.4 copy_bitcast_fusion.2
  4.6 2.4 maximum_bitcast_fusion.1
  7.0 6.0 %all-to-all-start = ((bf16[8,2,2,16,16,256]{5,4,3,2,1,0:T(8,128)(2,1)}), bf16[8,2,2,16,16,256]{5,4,3,2,1,0:T(8,128)(2,1)}, u32[]{:S(2)}, u32[]{:S(2)}) async-start(bf16[8,2,2,16,16,256]{5,4,3,2,1,0:T(8,128)(2,1)} %maximum_bitcast_fusion.1), calls=%async_computation | async-start | bytes 8388608 | tf_op jit(solution)/shard_map/all_to_all | solution.py:98
  13.0 5.3 %slice.47 = bf16[2,16,40,8,256]{4,3,2,1,0:T(8,128)(2,1)} slice(bf16[2,16,64,8,256]{4,3,2,1,0:T(8,128)(2,1)} %param.3), slice={[0:2], [0:16], [16:56], [0:8], [0:256]} | slice | bytes 10485760 | tf_op jit(solution)/shard_map/slice | solution.py:92
  18.3 5.4 %slice.48 = bf16[2,16,40,8,256]{4,3,2,1,0:T(8,128)(2,1)} slice(bf16[2,16,64,8,256]{4,3,2,1,0:T(8,128)(2,1)} %param.4), slice={[0:2], [0:16], [16:56], [0:8], [0:256]} | slice | bytes 10485760 | tf_op jit(solution)/shard_map/slice | solution.py:92
  23.7 14.1 %copy_bitcast_fusion = (bf16[1,2,16,40,8,256]{5,2,3,1,0,4:T(8,128)(2,1)}, bf16[1,2,16,40,8,256]{5,2,3,1,0,4:T(8,128)(2,1)}) fusion(bf16[2,16,40,8,256]{4,3,2,1,0:T(8,128)(2,1)} %slice.48, bf16[2,16,40,8,256]{4,3,2,1,0:T(8,128)(2,1)} %slice.47), kind=kLoop, calls=%fused_computation.1 | loop fusion | bytes 20971520 | tf_op jit(solution)/shard_map/stack | solution.py:92
  37.8 8.9 %maximum_bitcast_fusion = bf16[8,2,2,40,16,256]{5,4,3,2,1,0:T(8,128)(2,1)} fusion(bf16[1,2,16,40,8,256]{5,2,3,1,0,4:T(8,128)(2,1)} %get-tuple-element.37, bf16[1,2,16,40,8,256]{5,2,3,1,0,4:T(8,128)(2,1)} %get-tuple-element.38), kind=kLoop, calls=%fused_computation | loop fusion | flops 5242880 | bytes 20971520 | tf_op jit(solution)/shard_map/transpose | solution.py:93
  46.7 15.1 %all-to-all-done.x_ref = bf16[8,2,2,16,16,256]{5,4,3,2,1,0:T(8,128)(2,1)} async-done(((bf16[8,2,2,16,16,256]{5,4,3,2,1,0:T(8,128)(2,1)}), bf16[8,2,2,16,16,256]{5,4,3,2,1,0:T(8,128)(2,1)}, u32[]{:S(2)}, u32[]{:S(2)}) %all-to-all-start) | async-done | bytes 4194336 | tf_op jit(solution)/shard_map/all_to_all | solution.py:98
  61.7 5.3 %all-to-all-start.1 = ((bf16[8,2,2,40,16,256]{5,4,3,2,1,0:T(8,128)(2,1)}), bf16[8,2,2,40,16,256]{5,4,3,2,1,0:T(8,128)(2,1)}, u32[]{:S(2)}, u32[]{:S(2)}) async-start(bf16[8,2,2,40,16,256]{5,4,3,2,1,0:T(8,128)(2,1)} %maximum_bitcast_fusion), calls=%async_computation.1 | async-start | bytes 20971520 | tf_op jit(solution)/shard_map/all_to_all | solution.py:98
  67.1 0.0 slice-start.1
  67.1 0.0 slice-start.3
  67.1 1.2 slice-done.1
  68.3 0.3 slice-done.3
  68.6 1.2 copy_bitcast_fusion.4
  69.8 1.6 maximum_bitcast_fusion.2
  71.4 14.6 %shard_map.37 = f32[2,2,16,33,128]{4,3,2,1,0:T(8,128)} custom-call(bf16[8,2,2,16,16,256]{5,4,3,2,1,0:T(8,128)(2,1)} %all-to-all-done.x_ref), custom_call_target="tpu_custom_call" | custom-call | tf_op jit(solution)/shard_map/pallas_call | solution.py:60
  86.0 96.1 %all-to-all-done.1.x_ref = bf16[8,2,2,40,16,256]{5,4,3,2,1,0:T(8,128)(2,1)} async-done(((bf16[8,2,2,40,16,256]{5,4,3,2,1,0:T(8,128)(2,1)}), bf16[8,2,2,40,16,256]{5,4,3,2,1,0:T(8,128)(2,1)}, u32[]{:S(2)}, u32[]{:S(2)}) %all-to-all-start.1) | async-done | bytes 10485792 | tf_op jit(solution)/shard_map/all_to_all | solution.py:98
  182.1 4.6 %all-to-all-start.2 = ((bf16[8,2,2,8,16,256]{5,4,3,2,1,0:T(8,128)(2,1)}), bf16[8,2,2,8,16,256]{5,4,3,2,1,0:T(8,128)(2,1)S(1)}, u32[]{:S(2)}, u32[]{:S(2)}) async-start(bf16[8,2,2,8,16,256]{5,4,3,2,1,0:T(8,128)(2,1)} %maximum_bitcast_fusion.2), calls=%async_computation.2 | async-start | bytes 4194304 | tf_op jit(solution)/shard_map/all_to_all | solution.py:98
  186.6 0.1 add_subtract_fusion
  186.7 0.6 fusion.1
  194.5 33.7 %shard_map.38 = f32[2,2,40,33,128]{4,3,2,1,0:T(8,128)} custom-call(bf16[8,2,2,40,16,256]{5,4,3,2,1,0:T(8,128)(2,1)} %all-to-all-done.1.x_ref), custom_call_target="tpu_custom_call" | custom-call | tf_op jit(solution)/shard_map/pallas_call | solution.py:60
  228.2 0.2 add_bitcast_fusion.3
  228.3 2.3 add_bitcast_fusion
  230.6 1.1 pad_maximum_fusion.2
  231.7 1.1 pad_maximum_fusion.1
  232.8 0.1 add_bitcast_fusion.5
  232.9 1.2 copy-done
  234.0 0.2 add_bitcast_fusion.2
  234.2 1.1 pad_maximum_fusion
  235.4 0.0 all-to-all-done.2.x_ref
  235.4 3.2 %copy.17 = f32[56,33,128]{2,0,1:T(8,128)} copy(f32[56,33,128]{2,1,0:T(8,128)} %pad_maximum_fusion) | data formatting | bytes 1892352 | tf_op jit(solution)/shard_map/optimization_barrier | solution.py:103
  238.5 3.7 %collective-permute-start = (f32[56,33,128]{2,0,1:T(8,128)}, f32[56,33,128]{2,0,1:T(8,128)}, u32[]{:S(2)}, u32[]{:S(2)}) collective-permute-start(f32[56,33,128]{2,0,1:T(8,128)} %copy.17), channel_id=1, source_target_pairs={{8,0},{16,8},{24,16},{32,24},{40,32},{48,40},{56,48},{64,56},{72,6... | collective-permute-start | bytes 2838536 | tf_op jit(solution)/shard_map/ppermute | solution.py:19
  242.2 1.1 copy.19
  243.3 4.5 %collective-permute-start.1 = (f32[56,33,128]{2,0,1:T(8,128)}, f32[56,33,128]{2,0,1:T(8,128)}, u32[]{:S(2)}, u32[]{:S(2)}) collective-permute-start(f32[56,33,128]{2,0,1:T(8,128)} %copy.19), channel_id=1, source_target_pairs={{0,8},{8,16},{16,24},{24,32},{32,40},{40,48},{48,56},{56,64},{64,7... | collective-permute-start | bytes 2838536 | tf_op jit(solution)/shard_map/ppermute | solution.py:19
  247.9 8.2 %shard_map.39 = f32[2,2,8,33,128]{4,3,2,1,0:T(8,128)} custom-call(bf16[8,2,2,8,16,256]{5,4,3,2,1,0:T(8,128)(2,1)} %copy-done.2), custom_call_target="tpu_custom_call" | custom-call | tf_op jit(solution)/shard_map/pallas_call | solution.py:60
  256.1 1.2 add_bitcast_fusion.7
  257.3 1.9 collective-permute-start.2
  259.3 5.1 %collective-permute-start.3 = (f32[8,33,128]{2,1,0:T(8,128)S(1)}, f32[8,33,128]{2,1,0:T(8,128)S(1)}, u32[]{:S(2)}, u32[]{:S(2)}) collective-permute-start(f32[8,33,128]{2,1,0:T(8,128)S(1)} %get-tuple-element.30), channel_id=1, source_target_pairs={{0,8},{8,16},{16,24},{24,32},{32,40},{40,48},{48,56},{56,64},{64,7... | collective-permute-start | bytes 405512 | tf_op jit(solution)/shard_map/ppermute | solution.py:19
  264.4 3.8 %collective-permute-done.2 = f32[8,33,128]{2,1,0:T(8,128)S(1)} collective-permute-done((f32[8,33,128]{2,1,0:T(8,128)S(1)}, f32[8,33,128]{2,1,0:T(8,128)S(1)}, u32[]{:S(2)}, u32[]{:S(2)}) %collective-permute-start.2) | collective-permute-done | bytes 135200 | tf_op jit(solution)/shard_map/ppermute | solution.py:19
  268.2 0.9 collective-permute-done.3
  269.0 1.2 fusion
  270.2 0.0 collective-permute-done
  270.3 0.0 collective-permute-done.1
  270.3 1.8 copy_add_fusion
  272.1 0.1 maximum_bitcast_fusion.3
  272.2 1.2 copy.21
  (13 shorter events, 0.0 us)
Async XLA Ops:
  0.0 1.6 slice-start
  0.0 2.2 slice-start.2
  7.0 54.7 %all-to-all-start = ((bf16[8,2,2,16,16,256]{5,4,3,2,1,0:T(8,128)(2,1)}), bf16[8,2,2,16,16,256]{5,4,3,2,1,0:T(8,128)(2,1)}, u32[]{:S(2)}, u32[]{:S(2)}) async-start(bf16[8,2,2,16,16,256]{5,4,3,2,1,0:T(8,128)(2,1)} %maximum_bitcast_fusion.1), calls=%async_computation | async-start | bytes 8388608 | tf_op jit(solution)/shard_map/all_to_all | solution.py:98
  61.7 120.3 %all-to-all-start.1 = ((bf16[8,2,2,40,16,256]{5,4,3,2,1,0:T(8,128)(2,1)}), bf16[8,2,2,40,16,256]{5,4,3,2,1,0:T(8,128)(2,1)}, u32[]{:S(2)}, u32[]{:S(2)}) async-start(bf16[8,2,2,40,16,256]{5,4,3,2,1,0:T(8,128)(2,1)} %maximum_bitcast_fusion), calls=%async_computation.1 | async-start | bytes 20971520 | tf_op jit(solution)/shard_map/all_to_all | solution.py:98
  67.1 1.2 slice-start.1
  67.1 1.5 slice-start.3
  86.0 100.6 %copy-start.5 = (s32[2]{0:T(128)S(1)}, s32[2]{0:T(128)}, u32[]{:S(2)}) copy-start(s32[2]{0:T(128)} %param.5) | copy-start | bytes 28
  182.1 53.3 %all-to-all-start.2 = ((bf16[8,2,2,8,16,256]{5,4,3,2,1,0:T(8,128)(2,1)}), bf16[8,2,2,8,16,256]{5,4,3,2,1,0:T(8,128)(2,1)S(1)}, u32[]{:S(2)}, u32[]{:S(2)}) async-start(bf16[8,2,2,8,16,256]{5,4,3,2,1,0:T(8,128)(2,1)} %maximum_bitcast_fusion.2), calls=%async_computation.2 | async-start | bytes 4194304 | tf_op jit(solution)/shard_map/all_to_all | solution.py:98
  194.4 33.7 %copy-start.1 = (f32[2,2,16,33,128]{4,3,2,1,0:T(8,128)S(1)}, f32[2,2,16,33,128]{4,3,2,1,0:T(8,128)}, u32[]{:S(2)}) copy-start(f32[2,2,16,33,128]{4,3,2,1,0:T(8,128)} %shard_map.37) | copy-start | bytes 3244036
  231.7 2.3 copy-start
  234.2 8.0 %copy-start.3 = (f32[56,33,128]{2,1,0:T(8,128)S(1)}, f32[56,33,128]{2,1,0:T(8,128)}, u32[]{:S(2)}) copy-start(f32[56,33,128]{2,1,0:T(8,128)} %pad_maximum_fusion.2) | copy-start | bytes 2838532
  235.4 12.5 %copy-start.2 = (bf16[8,2,2,8,16,256]{5,4,3,2,1,0:T(8,128)(2,1)}, bf16[8,2,2,8,16,256]{5,4,3,2,1,0:T(8,128)(2,1)S(1)}, u32[]{:S(2)}) copy-start(bf16[8,2,2,8,16,256]{5,4,3,2,1,0:T(8,128)(2,1)S(1)} %all-to-all-done.2.x_ref) | copy-start | bytes 6291460
  238.5 31.7 %collective-permute-start = (f32[56,33,128]{2,0,1:T(8,128)}, f32[56,33,128]{2,0,1:T(8,128)}, u32[]{:S(2)}, u32[]{:S(2)}) collective-permute-start(f32[56,33,128]{2,0,1:T(8,128)} %copy.17), channel_id=1, source_target_pairs={{8,0},{16,8},{24,16},{32,24},{40,32},{48,40},{56,48},{64,56},{72,6... | collective-permute-start | bytes 2838536 | tf_op jit(solution)/shard_map/ppermute | solution.py:19
  243.3 26.9 %copy-start.4 = (f32[56,33,128]{2,1,0:T(8,128)S(1)}, f32[56,33,128]{2,1,0:T(8,128)}, u32[]{:S(2)}) copy-start(f32[56,33,128]{2,1,0:T(8,128)} %pad_maximum_fusion.1) | copy-start | bytes 2838532
  243.3 26.9 %collective-permute-start.1 = (f32[56,33,128]{2,0,1:T(8,128)}, f32[56,33,128]{2,0,1:T(8,128)}, u32[]{:S(2)}, u32[]{:S(2)}) collective-permute-start(f32[56,33,128]{2,0,1:T(8,128)} %copy.19), channel_id=1, source_target_pairs={{0,8},{8,16},{16,24},{24,32},{32,40},{40,48},{48,56},{56,64},{64,7... | collective-permute-start | bytes 2838536 | tf_op jit(solution)/shard_map/ppermute | solution.py:19
  257.3 10.8 %collective-permute-start.2 = (f32[8,33,128]{2,1,0:T(8,128)S(1)}, f32[8,33,128]{2,1,0:T(8,128)S(1)}, u32[]{:S(2)}, u32[]{:S(2)}) collective-permute-start(f32[8,33,128]{2,1,0:T(8,128)S(1)} %get-tuple-element.29), channel_id=1, source_target_pairs={{8,0},{16,8},{24,16},{32,24},{40,32},{48,40},{56,48},{64,56},{72,6... | collective-permute-start | bytes 405512 | tf_op jit(solution)/shard_map/ppermute | solution.py:19
  259.3 9.8 %collective-permute-start.3 = (f32[8,33,128]{2,1,0:T(8,128)S(1)}, f32[8,33,128]{2,1,0:T(8,128)S(1)}, u32[]{:S(2)}, u32[]{:S(2)}) collective-permute-start(f32[8,33,128]{2,1,0:T(8,128)S(1)} %get-tuple-element.30), channel_id=1, source_target_pairs={{0,8},{8,16},{16,24},{24,32},{32,40},{40,48},{48,56},{56,64},{64,7... | collective-permute-start | bytes 405512 | tf_op jit(solution)/shard_map/ppermute | solution.py:19

commit v12 on v10

--- a/solution.py
+++ b/solution.py
@@ -26,12 +26,12 @@
     u_i = lax.broadcasted_iota(jnp.int32, (width, width), 0)
     k_i = lax.broadcasted_iota(jnp.int32, (width, width), 1)
     v_ok = (u_i - k_i + 2 * half >= 0) & (u_i - k_i + 2 * half < width)
-    x_i = lax.broadcasted_iota(jnp.int32, (1, width), 1)
+    x_i = lax.broadcasted_iota(jnp.int32, (cb, width), 1)
     a_i = lax.broadcasted_iota(jnp.int32, (TILE, TILE), 0)
     b_i = lax.broadcasted_iota(jnp.int32, (TILE, TILE), 1)
     anti = jnp.where(a_i + b_i == TILE - 1, 1.0, 0.0).astype(jnp.bfloat16)
 
-    def one_channel(c, carry):
+    for c in range(cb):
         s_t = x_ref[:, 0, 0, c, :, :].reshape(src * t16, width)
         r_t = x_ref[:, 1, 0, c, :, :].reshape(src * t16, width)
         swapped = jnp.concatenate([r_t[:, TILE:], r_t[:, :TILE]], axis=0)
@@ -41,17 +41,14 @@
                             preferred_element_type=jnp.float32)
         q = pltpu.roll(g, 2 * half + 1, 1, stride=1, stride_axis=0)
         q = jnp.where(v_ok, q, 0.0)
-        band_ref[...] = q[:, :TILE].T[:rows, :]
-        for j in range(LAGS):
-            d = half - j
-            w = band_ref[2 * j:2 * j + 1, :]
-            out = pltpu.roll(w, d % width, 1)
-            out = jnp.where((x_i - d >= 0) & (x_i - d < width), out, 0.0)
-            o_ref[0, 0, c, pl.ds(half + d, 1), :] = out[:, :TILE]
-            o_ref[0, 1, c, pl.ds(half + d, 1), :] = out[:, TILE:]
-        return carry
-
-    lax.fori_loop(0, cb, one_channel, 0, unroll=2)
+        band_ref[:, c, :] = q[:, :TILE].T[:rows, :]
+    for j in range(LAGS):
+        d = half - j
+        w = band_ref[2 * j]
+        out = pltpu.roll(w, d % width, 1)
+        out = jnp.where((x_i - d >= 0) & (x_i - d < width), out, 0.0)
+        o_ref[0, 0, half + d] = out[:, :TILE]
+        o_ref[0, 1, half + d] = out[:, TILE:]
 
 
 def lag_images(pair):
@@ -61,9 +58,9 @@
         lag_kernel,
         grid=(shots, chans // cb),
         in_specs=[pl.BlockSpec((n_src, 2, 1, cb, t16, width), lambda i, j: (0, 0, i, j, 0, 0))],
-        out_specs=pl.BlockSpec((1, 2, cb, LAGS, TILE), lambda i, j: (i, 0, j, 0, 0)),
-        out_shape=jax.ShapeDtypeStruct((shots, 2, chans, LAGS, TILE), jnp.float32),
-        scratch_shapes=[pltpu.VMEM((72, width), jnp.float32)],
+        out_specs=pl.BlockSpec((1, 2, LAGS, cb, TILE), lambda i, j: (i, 0, 0, j, 0)),
+        out_shape=jax.ShapeDtypeStruct((shots, 2, LAGS, chans, TILE), jnp.float32),
+        scratch_shapes=[pltpu.VMEM((72, cb, width), jnp.float32)],
     )(pair)
 
 
@@ -99,7 +96,7 @@
         if g >= 1:
             images.append(lag_images(received[g - 1]))
     early = [place_tiles(image, start_tile, owner - 1, 3) for image in images]
-    early = [jnp.concatenate([p[k] for p in early], axis=0) for k in range(3)]
+    early = [jnp.concatenate([p[k] for p in early], axis=1) for k in range(3)]
     early, received[-1] = lax.optimization_barrier((early, received[-1]))
     parts = [early, place_tiles(lag_images(received[-1]), start_tile, owner - 1, 3)]
     out = []
@@ -107,7 +104,7 @@
         right_part = passed_along(slots[0], "space", -1)
         left_part = passed_along(slots[2], "space", 1)
         out.append(slots[1] + right_part + left_part)
-    return jnp.concatenate(out, axis=0)[None]
+    return jnp.transpose(jnp.concatenate(out, axis=1), (1, 0, 2))[None]
 
 
 def solution(mesh):

time: 263 us -> 257 us (0.977)
  Pallas kernels: 56.5 us -> 36.8 us
  waiting for transfers between devices: 105 us -> 120 us
    pallas_call x3, Pallas kernels: 56.5 us -> 36.8 us  [lag_images(): pl.pallas_call(lag_kernel, grid=(shots, chans // cb), in_specs=[pl.BlockS...]
    all_to_all x3, waiting for transfers between devices: 100 us -> 116 us  [body(): lax.all_to_all(pair, 'tm', split_axis=0, concat_axis=0, tiled=True)]
  transfers between devices with their start and end apart: 7 -> 7, of which waited for: 4 -> 4; matrix products, arithmetic and copies ran while one was open for 18% -> 17% of each run, Pallas kernels for 22% -> 15%
where the time goes in v12:
time: 257 us; the launch traced here: 253 us
  waiting for transfers between devices  120 us (47%)
  Pallas kernels  36.8 us (14%)
  local copies, waits for them, and re-layouts  35.8 us (14%)
  starting transfers between devices  32.5 us (13%)
  other arithmetic  20.6 us (8%)
  between operations  7.87 us (3%)
    all_to_all x3, waiting for transfers between devices, body(): lax.all_to_all(pair, 'tm', split_axis=0, concat_axis=0, tiled=True)  116 us
    pallas_call x3, Pallas kernels, lag_images(): pl.pallas_call(lag_kernel, grid=(shots, chans // cb), in_specs=[pl.BlockS...  36.8 us
    another operation x3, local copies, waits for them, and re-layouts, body(): pair = jnp.stack([source_snap[:, :, cs], receiver_snap[:, :, cs]])  17.7 us
    ppermute x4, starting transfers between devices, passed_along(): return lax.ppermute(block, axis, route)  16.5 us
    all_to_all x3, starting transfers between devices, body(): lax.all_to_all(pair, 'tm', split_axis=0, concat_axis=0, tiled=True)  15.9 us
    slice x10, local copies, waits for them, and re-layouts, body(): pair = jnp.stack([source_snap[:, :, cs], receiver_snap[:, :, cs]])  14.4 us
    transpose x3, other arithmetic, body(): pair = jnp.transpose(pair, (4, 0, 1, 3, 2, 5))  12.8 us
  transfers between devices with their start and end apart: 7, of which 4 were waited for; matrix products, arithmetic and copies ran while one was open for 17% of the time, Pallas kernels for 15%

profile of v12, /device:TPU:3, one launch (start us, length us, event | category | flops | bytes accessed | tf_op | source)
XLA Modules:
  0.0 253.4 jit_solution(13220339458883249205)
XLA Ops:
  0.0 1.2 slice-done
  1.2 0.3 slice-done.2
  1.5 1.2 copy_bitcast_fusion.4
  2.7 1.5 maximum_bitcast_fusion.2
  4.3 6.0 %all-to-all-start = ((bf16[8,2,2,8,16,256]{5,4,3,2,1,0:T(8,128)(2,1)}), bf16[8,2,2,8,16,256]{5,4,3,2,1,0:T(8,128)(2,1)S(1)}, u32[]{:S(2)}, u32[]{:S(2)}) async-start(bf16[8,2,2,8,16,256]{5,4,3,2,1,0:T(8,128)(2,1)} %maximum_bitcast_fusion.2), calls=%async_computation | async-start | bytes 4194304 | tf_op jit(solution)/shard_map/all_to_all | solution.py:95
  10.3 5.3 %slice.47 = bf16[2,16,40,8,256]{4,3,2,1,0:T(8,128)(2,1)} slice(bf16[2,16,64,8,256]{4,3,2,1,0:T(8,128)(2,1)} %param.3), slice={[0:2], [0:16], [8:48], [0:8], [0:256]} | slice | bytes 10485760 | tf_op jit(solution)/shard_map/slice | solution.py:89
  15.6 5.4 %slice.48 = bf16[2,16,40,8,256]{4,3,2,1,0:T(8,128)(2,1)} slice(bf16[2,16,64,8,256]{4,3,2,1,0:T(8,128)(2,1)} %param.4), slice={[0:2], [0:16], [8:48], [0:8], [0:256]} | slice | bytes 10485760 | tf_op jit(solution)/shard_map/slice | solution.py:89
  21.0 14.1 %copy_bitcast_fusion = (bf16[1,2,16,40,8,256]{5,2,3,1,0,4:T(8,128)(2,1)}, bf16[1,2,16,40,8,256]{5,2,3,1,0,4:T(8,128)(2,1)}) fusion(bf16[2,16,40,8,256]{4,3,2,1,0:T(8,128)(2,1)} %slice.48, bf16[2,16,40,8,256]{4,3,2,1,0:T(8,128)(2,1)} %slice.47), kind=kLoop, calls=%fused_computation.1 | loop fusion | bytes 20971520 | tf_op jit(solution)/shard_map/stack | solution.py:89
  35.0 8.9 %maximum_bitcast_fusion = bf16[8,2,2,40,16,256]{5,4,3,2,1,0:T(8,128)(2,1)} fusion(bf16[1,2,16,40,8,256]{5,2,3,1,0,4:T(8,128)(2,1)} %get-tuple-element.37, bf16[1,2,16,40,8,256]{5,2,3,1,0,4:T(8,128)(2,1)} %get-tuple-element.38), kind=kLoop, calls=%fused_computation | loop fusion | flops 5242880 | bytes 20971520 | tf_op jit(solution)/shard_map/transpose | solution.py:90
  43.9 0.0 all-to-all-done.x_ref
  43.9 1.4 copy-done.1
  45.3 5.3 %all-to-all-start.1 = ((bf16[8,2,2,40,16,256]{5,4,3,2,1,0:T(8,128)(2,1)}), bf16[8,2,2,40,16,256]{5,4,3,2,1,0:T(8,128)(2,1)}, u32[]{:S(2)}, u32[]{:S(2)}) async-start(bf16[8,2,2,40,16,256]{5,4,3,2,1,0:T(8,128)(2,1)} %maximum_bitcast_fusion), calls=%async_computation.1 | async-start | bytes 20971520 | tf_op jit(solution)/shard_map/all_to_all | solution.py:95
  50.7 0.0 slice-start.1
  50.7 0.0 slice-start.3
  50.7 1.6 slice-done.1
  52.2 0.6 slice-done.3
  52.9 2.4 copy_bitcast_fusion.2
  55.3 2.4 maximum_bitcast_fusion.1
  57.7 5.8 %shard_map.37 = f32[2,2,33,8,128]{4,3,2,1,0:T(8,128)} custom-call(bf16[8,2,2,8,16,256]{5,4,3,2,1,0:T(8,128)(2,1)} %copy-done.1), custom_call_target="tpu_custom_call" | custom-call | tf_op jit(solution)/shard_map/pallas_call | solution.py:57
  63.5 102.7 %all-to-all-done.1.x_ref = bf16[8,2,2,40,16,256]{5,4,3,2,1,0:T(8,128)(2,1)} async-done(((bf16[8,2,2,40,16,256]{5,4,3,2,1,0:T(8,128)(2,1)}), bf16[8,2,2,40,16,256]{5,4,3,2,1,0:T(8,128)(2,1)}, u32[]{:S(2)}, u32[]{:S(2)}) %all-to-all-start.1) | async-done | bytes 10485792 | tf_op jit(solution)/shard_map/all_to_all | solution.py:95
  166.2 4.6 %all-to-all-start.2 = ((bf16[8,2,2,16,16,256]{5,4,3,2,1,0:T(8,128)(2,1)}), bf16[8,2,2,16,16,256]{5,4,3,2,1,0:T(8,128)(2,1)}, u32[]{:S(2)}, u32[]{:S(2)}) async-start(bf16[8,2,2,16,16,256]{5,4,3,2,1,0:T(8,128)(2,1)} %maximum_bitcast_fusion.1), calls=%async_computation.2 | async-start | bytes 8388608 | tf_op jit(solution)/shard_map/all_to_all | solution.py:95
  170.8 0.0 copy-done.3
  170.8 0.1 add_subtract_fusion
  170.8 0.7 fusion.1
  179.2 0.0 copy-start.2
  179.2 21.4 %shard_map.38 = f32[2,2,33,40,128]{4,3,2,1,0:T(8,128)} custom-call(bf16[8,2,2,40,16,256]{5,4,3,2,1,0:T(8,128)(2,1)} %all-to-all-done.1.x_ref), custom_call_target="tpu_custom_call" | custom-call | tf_op jit(solution)/shard_map/pallas_call | solution.py:57
  200.6 0.0 copy-done.2
  200.6 0.1 add_bitcast_fusion.5
  200.7 2.0 add_bitcast_fusion
  202.7 0.1 pad_maximum_fusion.2
  202.8 0.1 pad_maximum_fusion.1
  202.9 1.6 copy-done
  204.4 0.2 add_bitcast_fusion.2
  204.6 0.1 pad_maximum_fusion
  204.7 13.4 %all-to-all-done.2.x_ref = bf16[8,2,2,16,16,256]{5,4,3,2,1,0:T(8,128)(2,1)} async-done(((bf16[8,2,2,16,16,256]{5,4,3,2,1,0:T(8,128)(2,1)}), bf16[8,2,2,16,16,256]{5,4,3,2,1,0:T(8,128)(2,1)}, u32[]{:S(2)}, u32[]{:S(2)}) %all-to-all-start.2) | async-done | bytes 4194336 | tf_op jit(solution)/shard_map/all_to_all | solution.py:95
  218.0 5.0 %collective-permute-start = (f32[33,48,128]{2,1,0:T(8,128)S(1)}, f32[33,48,128]{2,1,0:T(8,128)}, u32[]{:S(2)}, u32[]{:S(2)}) collective-permute-start(f32[33,48,128]{2,1,0:T(8,128)S(1)} %pad_maximum_fusion), channel_id=1, source_target_pairs={{8,0},{16,8},{24,16},{32,24},{40,32},{48,40},{56,48},{64,56},{72,6... | collective-permute-start | bytes 2433032 | tf_op jit(solution)/shard_map/ppermute | solution.py:19
  223.1 4.4 %collective-permute-start.1 = (f32[33,48,128]{2,1,0:T(8,128)S(1)}, f32[33,48,128]{2,1,0:T(8,128)}, u32[]{:S(2)}, u32[]{:S(2)}) collective-permute-start(f32[33,48,128]{2,1,0:T(8,128)S(1)} %pad_maximum_fusion.2), channel_id=1, source_target_pairs={{0,8},{8,16},{16,24},{24,32},{32,40},{40,48},{48,56},{56,64},{64,7... | collective-permute-start | bytes 2433032 | tf_op jit(solution)/shard_map/ppermute | solution.py:19
  227.5 9.7 %shard_map.39 = f32[2,2,33,16,128]{4,3,2,1,0:T(8,128)} custom-call(bf16[8,2,2,16,16,256]{5,4,3,2,1,0:T(8,128)(2,1)} %all-to-all-done.2.x_ref), custom_call_target="tpu_custom_call" | custom-call | tf_op jit(solution)/shard_map/pallas_call | solution.py:57
  237.2 1.3 add_bitcast_fusion.4
  238.5 1.9 collective-permute-start.2
  240.4 5.1 %collective-permute-start.3 = (f32[33,16,128]{2,1,0:T(8,128)S(1)}, f32[33,16,128]{2,1,0:T(8,128)S(1)}, u32[]{:S(2)}, u32[]{:S(2)}) collective-permute-start(f32[33,16,128]{2,1,0:T(8,128)S(1)} %get-tuple-element.28), channel_id=1, source_target_pairs={{0,8},{8,16},{16,24},{24,32},{32,40},{40,48},{48,56},{56,64},{64,7... | collective-permute-start | bytes 811016 | tf_op jit(solution)/shard_map/ppermute | solution.py:19
  245.6 2.2 collective-permute-done.2
  247.8 1.7 collective-permute-done.3
  249.5 1.3 fusion
  250.8 0.0 collective-permute-done
  250.8 0.0 collective-permute-done.1
  250.8 1.5 add_add_fusion
  252.3 1.1 maximum_bitcast_fusion.3
  (6 shorter events, 0.0 us)
Async XLA Ops:
  0.0 1.2 slice-start
  0.0 1.5 slice-start.2
  4.3 39.7 %all-to-all-start = ((bf16[8,2,2,8,16,256]{5,4,3,2,1,0:T(8,128)(2,1)}), bf16[8,2,2,8,16,256]{5,4,3,2,1,0:T(8,128)(2,1)S(1)}, u32[]{:S(2)}, u32[]{:S(2)}) async-start(bf16[8,2,2,8,16,256]{5,4,3,2,1,0:T(8,128)(2,1)} %maximum_bitcast_fusion.2), calls=%async_computation | async-start | bytes 4194304 | tf_op jit(solution)/shard_map/all_to_all | solution.py:95
  43.9 1.4 copy-start.1
  45.3 120.9 %all-to-all-start.1 = ((bf16[8,2,2,40,16,256]{5,4,3,2,1,0:T(8,128)(2,1)}), bf16[8,2,2,40,16,256]{5,4,3,2,1,0:T(8,128)(2,1)}, u32[]{:S(2)}, u32[]{:S(2)}) async-start(bf16[8,2,2,40,16,256]{5,4,3,2,1,0:T(8,128)(2,1)} %maximum_bitcast_fusion), calls=%async_computation.1 | async-start | bytes 20971520 | tf_op jit(solution)/shard_map/all_to_all | solution.py:95
  50.7 1.6 slice-start.1
  50.7 2.2 slice-start.3
  63.5 107.3 %copy-start.3 = (s32[2]{0:T(128)S(1)}, s32[2]{0:T(128)}, u32[]{:S(2)}) copy-start(s32[2]{0:T(128)} %param.5) | copy-start | bytes 28
  166.2 51.8 %all-to-all-start.2 = ((bf16[8,2,2,16,16,256]{5,4,3,2,1,0:T(8,128)(2,1)}), bf16[8,2,2,16,16,256]{5,4,3,2,1,0:T(8,128)(2,1)}, u32[]{:S(2)}, u32[]{:S(2)}) async-start(bf16[8,2,2,16,16,256]{5,4,3,2,1,0:T(8,128)(2,1)} %maximum_bitcast_fusion.1), calls=%async_computation.2 | async-start | bytes 8388608 | tf_op jit(solution)/shard_map/all_to_all | solution.py:95
  179.2 21.4 %copy-start.2 = (f32[2,2,33,8,128]{4,3,2,1,0:T(8,128)S(1)}, f32[2,2,33,8,128]{4,3,2,1,0:T(8,128)}, u32[]{:S(2)}) copy-start(f32[2,2,33,8,128]{4,3,2,1,0:T(8,128)} %shard_map.37) | copy-start | bytes 1622020
  202.7 1.8 copy-start
  218.0 32.8 %collective-permute-start = (f32[33,48,128]{2,1,0:T(8,128)S(1)}, f32[33,48,128]{2,1,0:T(8,128)}, u32[]{:S(2)}, u32[]{:S(2)}) collective-permute-start(f32[33,48,128]{2,1,0:T(8,128)S(1)} %pad_maximum_fusion), channel_id=1, source_target_pairs={{8,0},{16,8},{24,16},{32,24},{40,32},{48,40},{56,48},{64,56},{72,6... | collective-permute-start | bytes 2433032 | tf_op jit(solution)/shard_map/ppermute | solution.py:19
  223.1 27.7 %collective-permute-start.1 = (f32[33,48,128]{2,1,0:T(8,128)S(1)}, f32[33,48,128]{2,1,0:T(8,128)}, u32[]{:S(2)}, u32[]{:S(2)}) collective-permute-start(f32[33,48,128]{2,1,0:T(8,128)S(1)} %pad_maximum_fusion.2), channel_id=1, source_target_pairs={{0,8},{8,16},{16,24},{24,32},{32,40},{40,48},{48,56},{56,64},{64,7... | collective-permute-start | bytes 2433032 | tf_op jit(solution)/shard_map/ppermute | solution.py:19
  238.5 9.3 %collective-permute-start.2 = (f32[33,16,128]{2,1,0:T(8,128)S(1)}, f32[33,16,128]{2,1,0:T(8,128)S(1)}, u32[]{:S(2)}, u32[]{:S(2)}) collective-permute-start(f32[33,16,128]{2,1,0:T(8,128)S(1)} %get-tuple-element.27), channel_id=1, source_target_pairs={{8,0},{16,8},{24,16},{32,24},{40,32},{48,40},{56,48},{64,56},{72,6... | collective-permute-start | bytes 811016 | tf_op jit(solution)/shard_map/ppermute | solution.py:19
  240.4 9.0 %collective-permute-start.3 = (f32[33,16,128]{2,1,0:T(8,128)S(1)}, f32[33,16,128]{2,1,0:T(8,128)S(1)}, u32[]{:S(2)}, u32[]{:S(2)}) collective-permute-start(f32[33,16,128]{2,1,0:T(8,128)S(1)} %get-tuple-element.28), channel_id=1, source_target_pairs={{0,8},{8,16},{16,24},{24,32},{32,40},{40,48},{48,56},{56,64},{64,7... | collective-permute-start | bytes 811016 | tf_op jit(solution)/shard_map/ppermute | solution.py:19

commit v13 on v12

--- a/solution.py
+++ b/solution.py
@@ -10,7 +10,7 @@
 LAGS = 33
 TILE = 128
 CB = 8
-CHUNKS = (8, 40, 16)
+CHUNKS = (8, 48, 8)
 
 
 def passed_along(block, axis, distance):

time: 257 us -> 263 us (1.023)
  waiting for transfers between devices: 120 us -> 147 us
  local copies, waits for them, and re-layouts: 35.8 us -> 21.8 us
    all_to_all x3, waiting for transfers between devices: 116 us -> 137 us  [body(): lax.all_to_all(pair, 'tm', split_axis=0, concat_axis=0, tiled=True)]
    another operation x3, local copies, waits for them, and re-layouts: 17.7 us -> 10.8 us  [body(): pair = jnp.stack([source_snap[:, :, cs], receiver_snap[:, :, cs]])]
    ppermute x4, waiting for transfers between devices: 3.87 us -> 9.58 us  [passed_along(): return lax.ppermute(block, axis, route)]
    slice x10 -> x6, local copies, waits for them, and re-layouts: 14.4 us -> 8.98 us  [body(): pair = jnp.stack([source_snap[:, :, cs], receiver_snap[:, :, cs]])]
    transpose x3, other arithmetic: 12.8 us -> 8.32 us  [body(): pair = jnp.transpose(pair, (4, 0, 1, 3, 2, 5))]
  transfers between devices with their start and end apart: 7 -> 7, of which waited for: 4 -> 4; matrix products, arithmetic and copies ran while one was open for 17% -> 9% of each run, Pallas kernels for 15% -> 14%
where the time goes in v13:
time: 263 us; the launch traced here: 262 us
  waiting for transfers between devices  147 us (56%)
  Pallas kernels  36.8 us (14%)
  starting transfers between devices  31.1 us (12%)
  local copies, waits for them, and re-layouts  21.8 us (8%)
  other arithmetic  18.2 us (7%)
  between operations  7.42 us (3%)
    all_to_all x3, waiting for transfers between devices, body(): lax.all_to_all(pair, 'tm', split_axis=0, concat_axis=0, tiled=True)  137 us
    pallas_call x3, Pallas kernels, lag_images(): pl.pallas_call(lag_kernel, grid=(shots, chans // cb), in_specs=[pl.BlockS...  36.8 us
    all_to_all x3, starting transfers between devices, body(): lax.all_to_all(pair, 'tm', split_axis=0, concat_axis=0, tiled=True)  16 us
    ppermute x4, starting transfers between devices, passed_along(): return lax.ppermute(block, axis, route)  15.1 us
    another operation x3, local copies, waits for them, and re-layouts, body(): pair = jnp.stack([source_snap[:, :, cs], receiver_snap[:, :, cs]])  10.8 us
    ppermute x4, waiting for transfers between devices, passed_along(): return lax.ppermute(block, axis, route)  9.58 us
    slice x6, local copies, waits for them, and re-layouts, body(): pair = jnp.stack([source_snap[:, :, cs], receiver_snap[:, :, cs]])  8.98 us
    transpose x3, other arithmetic, body(): pair = jnp.transpose(pair, (4, 0, 1, 3, 2, 5))  8.32 us
  transfers between devices with their start and end apart: 7, of which 4 were waited for; matrix products, arithmetic and copies ran while one was open for 9% of the time, Pallas kernels for 14%

profile of v13, /device:TPU:3, one launch (start us, length us, event | category | flops | bytes accessed | tf_op | source)
XLA Modules:
  0.0 261.9 jit_solution(13665731068935079567)
XLA Ops:
  0.0 1.7 fusion.2
  1.7 2.7 %fusion.1 = (bf16[2,16,8,8,256]{4,3,2,1,0:T(8,128)(2,1)S(1)}, bf16[2,16,8,8,256]{4,3,2,1,0:T(8,128)(2,1)}) fusion(bf16[2,16,64,8,256]{4,3,2,1,0:T(8,128)(2,1)} %param.3), kind=kLoop, calls=%fused_computation.25 | loop fusion | bytes 4194304 | tf_op jit(solution)/shard_map/slice | solution.py:89
  4.4 1.2 copy_bitcast_fusion.2
  5.6 1.5 maximum_bitcast_fusion.2
  7.1 6.0 %all-to-all-start = ((bf16[8,2,2,8,16,256]{5,4,3,2,1,0:T(8,128)(2,1)}), bf16[8,2,2,8,16,256]{5,4,3,2,1,0:T(8,128)(2,1)S(1)}, u32[]{:S(2)}, u32[]{:S(2)}) async-start(bf16[8,2,2,8,16,256]{5,4,3,2,1,0:T(8,128)(2,1)} %maximum_bitcast_fusion.2), calls=%async_computation | async-start | bytes 4194304 | tf_op jit(solution)/shard_map/all_to_all | solution.py:95
  13.1 0.0 slice-start
  13.2 0.0 slice-start.1
  13.2 2.8 %slice-done = bf16[2,16,48,8,256]{4,3,2,1,0:T(8,128)(2,1)S(1)} async-done(((bf16[2,16,64,8,256]{4,3,2,1,0:T(8,128)(2,1)}), bf16[2,16,48,8,256]{4,3,2,1,0:T(8,128)(2,1)S(1)}, s32[]{:S(2)}) %slice-start) | async-done | bytes 6291480 | tf_op jit(solution)/shard_map/slice | solution.py:89
  15.9 1.8 slice-done.1
  17.8 7.2 %copy_bitcast_fusion = (bf16[1,2,16,48,8,256]{5,2,3,1,0,4:T(8,128)(2,1)S(1)}, bf16[1,2,16,48,8,256]{5,2,3,1,0,4:T(8,128)(2,1)S(1)}) fusion(bf16[2,16,48,8,256]{4,3,2,1,0:T(8,128)(2,1)S(1)} %slice-done, bf16[2,16,48,8,256]{4,3,2,1,0:T(8,128)(2,1)S(1)} %slice-done.1), kind=kLoop, calls=%fused_computation.1 | loop fusion | bytes 25165824 | tf_op jit(solution)/shard_map/stack | solution.py:89
  25.0 5.2 %maximum_bitcast_fusion = bf16[8,2,2,48,16,256]{5,4,3,2,1,0:T(8,128)(2,1)} fusion(bf16[1,2,16,48,8,256]{5,2,3,1,0,4:T(8,128)(2,1)S(1)} %get-tuple-element.41, bf16[1,2,16,48,8,256]{5,2,3,1,0,4:T(8,128)(2,1)S(1)} %get-tuple-element.42), kind=kLoop, calls=%fused_computation | loop fusion | flops 6291456 | bytes 25165824 | tf_op jit(solution)/shard_map/transpose | solution.py:90
  30.2 9.1 %all-to-all-done.x_ref = bf16[8,2,2,8,16,256]{5,4,3,2,1,0:T(8,128)(2,1)S(1)} async-done(((bf16[8,2,2,8,16,256]{5,4,3,2,1,0:T(8,128)(2,1)}), bf16[8,2,2,8,16,256]{5,4,3,2,1,0:T(8,128)(2,1)S(1)}, u32[]{:S(2)}, u32[]{:S(2)}) %all-to-all-start) | async-done | bytes 2097184 | tf_op jit(solution)/shard_map/all_to_all | solution.py:95
  39.3 1.3 copy-done.2
  40.6 5.4 %all-to-all-start.1 = ((bf16[8,2,2,48,16,256]{5,4,3,2,1,0:T(8,128)(2,1)}), bf16[8,2,2,48,16,256]{5,4,3,2,1,0:T(8,128)(2,1)}, u32[]{:S(2)}, u32[]{:S(2)}) async-start(bf16[8,2,2,48,16,256]{5,4,3,2,1,0:T(8,128)(2,1)} %maximum_bitcast_fusion), calls=%async_computation.1 | async-start | bytes 25165824 | tf_op jit(solution)/shard_map/all_to_all | solution.py:95
  46.0 2.4 copy_bitcast_fusion.4
  48.4 0.0 copy-start.4
  48.4 1.6 maximum_bitcast_fusion.1
  50.0 5.8 %shard_map.37 = f32[2,2,33,8,128]{4,3,2,1,0:T(8,128)} custom-call(bf16[8,2,2,8,16,256]{5,4,3,2,1,0:T(8,128)(2,1)} %copy-done.2), custom_call_target="tpu_custom_call" | custom-call | tf_op jit(solution)/shard_map/pallas_call | solution.py:57
  55.8 127.9 %all-to-all-done.1.x_ref = bf16[8,2,2,48,16,256]{5,4,3,2,1,0:T(8,128)(2,1)} async-done(((bf16[8,2,2,48,16,256]{5,4,3,2,1,0:T(8,128)(2,1)}), bf16[8,2,2,48,16,256]{5,4,3,2,1,0:T(8,128)(2,1)}, u32[]{:S(2)}, u32[]{:S(2)}) %all-to-all-start.1) | async-done | bytes 12582944 | tf_op jit(solution)/shard_map/all_to_all | solution.py:95
  183.6 4.6 %all-to-all-start.2 = ((bf16[8,2,2,8,16,256]{5,4,3,2,1,0:T(8,128)(2,1)}), bf16[8,2,2,8,16,256]{5,4,3,2,1,0:T(8,128)(2,1)S(1)}, u32[]{:S(2)}, u32[]{:S(2)}) async-start(bf16[8,2,2,8,16,256]{5,4,3,2,1,0:T(8,128)(2,1)} %maximum_bitcast_fusion.1), calls=%async_computation.2 | async-start | bytes 4194304 | tf_op jit(solution)/shard_map/all_to_all | solution.py:95
  188.2 0.0 copy-done.4
  188.2 0.1 add_subtract_fusion
  188.3 0.7 fusion.3
  196.2 0.0 copy-start.3
  196.2 25.3 %shard_map.38 = f32[2,2,33,48,128]{4,3,2,1,0:T(8,128)} custom-call(bf16[8,2,2,48,16,256]{5,4,3,2,1,0:T(8,128)(2,1)} %all-to-all-done.1.x_ref), custom_call_target="tpu_custom_call" | custom-call | tf_op jit(solution)/shard_map/pallas_call | solution.py:57
  221.5 0.0 copy-done.3
  221.5 2.2 add_bitcast_fusion.2
  223.7 1.0 pad_maximum_fusion
  224.7 0.1 add_bitcast_fusion.5
  224.8 0.0 copy-done
  224.8 0.4 add_bitcast_fusion
  225.2 0.1 pad_maximum_fusion.1
  225.3 1.0 pad_maximum_fusion.2
  226.3 0.0 all-to-all-done.2.x_ref
  226.3 6.1 %collective-permute-start.1 = (f32[33,56,128]{2,1,0:T(8,128)}, f32[33,56,128]{2,1,0:T(8,128)}, u32[]{:S(2)}, u32[]{:S(2)}) collective-permute-start(f32[33,56,128]{2,1,0:T(8,128)} %pad_maximum_fusion.2), channel_id=1, source_target_pairs={{0,8},{8,16},{16,24},{24,32},{32,40},{40,48},{48,56},{56,64},{64,7... | collective-permute-start | bytes 2838536 | tf_op jit(solution)/shard_map/ppermute | solution.py:19
  232.4 1.9 collective-permute-start
  234.3 0.0 copy-done.1
  234.4 5.8 %shard_map.39 = f32[2,2,33,8,128]{4,3,2,1,0:T(8,128)} custom-call(bf16[8,2,2,8,16,256]{5,4,3,2,1,0:T(8,128)(2,1)} %copy-done.1), custom_call_target="tpu_custom_call" | custom-call | tf_op jit(solution)/shard_map/pallas_call | solution.py:57
  240.1 1.2 add_bitcast_fusion.4
  241.3 5.1 %collective-permute-start.3 = (f32[33,8,128]{2,1,0:T(8,128)S(1)}, f32[33,8,128]{2,1,0:T(8,128)S(1)}, u32[]{:S(2)}, u32[]{:S(2)}) collective-permute-start(f32[33,8,128]{2,1,0:T(8,128)S(1)} %get-tuple-element.32), channel_id=1, source_target_pairs={{0,8},{8,16},{16,24},{24,32},{32,40},{40,48},{48,56},{56,64},{64,7... | collective-permute-start | bytes 405512 | tf_op jit(solution)/shard_map/ppermute | solution.py:19
  246.5 1.9 collective-permute-start.2
  248.4 7.9 %collective-permute-done.3 = f32[33,8,128]{2,1,0:T(8,128)S(1)} collective-permute-done((f32[33,8,128]{2,1,0:T(8,128)S(1)}, f32[33,8,128]{2,1,0:T(8,128)S(1)}, u32[]{:S(2)}, u32[]{:S(2)}) %collective-permute-start.3) | collective-permute-done | bytes 135200 | tf_op jit(solution)/shard_map/ppermute | solution.py:19
  256.3 1.7 collective-permute-done.2
  258.0 1.1 fusion
  259.1 0.0 collective-permute-done.1
  259.1 0.0 collective-permute-done
  259.1 1.6 add_add_fusion
  260.7 1.1 maximum_bitcast_fusion.3
  (4 shorter events, 0.0 us)
Async XLA Ops:
  7.1 32.2 %all-to-all-start = ((bf16[8,2,2,8,16,256]{5,4,3,2,1,0:T(8,128)(2,1)}), bf16[8,2,2,8,16,256]{5,4,3,2,1,0:T(8,128)(2,1)S(1)}, u32[]{:S(2)}, u32[]{:S(2)}) async-start(bf16[8,2,2,8,16,256]{5,4,3,2,1,0:T(8,128)(2,1)} %maximum_bitcast_fusion.2), calls=%async_computation | async-start | bytes 4194304 | tf_op jit(solution)/shard_map/all_to_all | solution.py:95
  13.1 2.8 %slice-start = ((bf16[2,16,64,8,256]{4,3,2,1,0:T(8,128)(2,1)}), bf16[2,16,48,8,256]{4,3,2,1,0:T(8,128)(2,1)S(1)}, s32[]{:S(2)}) async-start(bf16[2,16,64,8,256]{4,3,2,1,0:T(8,128)(2,1)} %param.4), calls=%async_computation.3 | async-start | bytes 12582912 | tf_op jit(solution)/shard_map/slice | solution.py:89
  13.2 4.6 %slice-start.1 = ((bf16[2,16,64,8,256]{4,3,2,1,0:T(8,128)(2,1)}), bf16[2,16,48,8,256]{4,3,2,1,0:T(8,128)(2,1)S(1)}, s32[]{:S(2)}) async-start(bf16[2,16,64,8,256]{4,3,2,1,0:T(8,128)(2,1)} %param.3), calls=%async_computation.4 | async-start | bytes 12582912 | tf_op jit(solution)/shard_map/slice | solution.py:89
  39.3 1.3 copy-start.2
  40.6 143.0 %all-to-all-start.1 = ((bf16[8,2,2,48,16,256]{5,4,3,2,1,0:T(8,128)(2,1)}), bf16[8,2,2,48,16,256]{5,4,3,2,1,0:T(8,128)(2,1)}, u32[]{:S(2)}, u32[]{:S(2)}) async-start(bf16[8,2,2,48,16,256]{5,4,3,2,1,0:T(8,128)(2,1)} %maximum_bitcast_fusion), calls=%async_computation.1 | async-start | bytes 25165824 | tf_op jit(solution)/shard_map/all_to_all | solution.py:95
  48.4 139.8 %copy-start.4 = (s32[2]{0:T(128)S(1)}, s32[2]{0:T(128)}, u32[]{:S(2)}) copy-start(s32[2]{0:T(128)} %param.5) | copy-start | bytes 28
  183.6 42.6 %all-to-all-start.2 = ((bf16[8,2,2,8,16,256]{5,4,3,2,1,0:T(8,128)(2,1)}), bf16[8,2,2,8,16,256]{5,4,3,2,1,0:T(8,128)(2,1)S(1)}, u32[]{:S(2)}, u32[]{:S(2)}) async-start(bf16[8,2,2,8,16,256]{5,4,3,2,1,0:T(8,128)(2,1)} %maximum_bitcast_fusion.1), calls=%async_computation.2 | async-start | bytes 4194304 | tf_op jit(solution)/shard_map/all_to_all | solution.py:95
  196.2 25.3 %copy-start.3 = (f32[2,2,33,8,128]{4,3,2,1,0:T(8,128)S(1)}, f32[2,2,33,8,128]{4,3,2,1,0:T(8,128)}, u32[]{:S(2)}) copy-start(f32[2,2,33,8,128]{4,3,2,1,0:T(8,128)} %shard_map.37) | copy-start | bytes 1622020
  221.5 3.4 %copy-start = (f32[2,2,33,48,128]{4,3,2,1,0:T(8,128)S(1)}, f32[2,2,33,48,128]{4,3,2,1,0:T(8,128)}, u32[]{:S(2)}) copy-start(f32[2,2,33,48,128]{4,3,2,1,0:T(8,128)} %shard_map.38) | copy-start | bytes 9732100
  226.3 8.1 %copy-start.1 = (bf16[8,2,2,8,16,256]{5,4,3,2,1,0:T(8,128)(2,1)}, bf16[8,2,2,8,16,256]{5,4,3,2,1,0:T(8,128)(2,1)S(1)}, u32[]{:S(2)}) copy-start(bf16[8,2,2,8,16,256]{5,4,3,2,1,0:T(8,128)(2,1)S(1)} %all-to-all-done.2.x_ref) | copy-start | bytes 6291460
  226.3 32.8 %collective-permute-start.1 = (f32[33,56,128]{2,1,0:T(8,128)}, f32[33,56,128]{2,1,0:T(8,128)}, u32[]{:S(2)}, u32[]{:S(2)}) collective-permute-start(f32[33,56,128]{2,1,0:T(8,128)} %pad_maximum_fusion.2), channel_id=1, source_target_pairs={{0,8},{8,16},{16,24},{24,32},{32,40},{40,48},{48,56},{56,64},{64,7... | collective-permute-start | bytes 2838536 | tf_op jit(solution)/shard_map/ppermute | solution.py:19
  232.4 26.7 %collective-permute-start = (f32[33,56,128]{2,1,0:T(8,128)}, f32[33,56,128]{2,1,0:T(8,128)}, u32[]{:S(2)}, u32[]{:S(2)}) collective-permute-start(f32[33,56,128]{2,1,0:T(8,128)} %pad_maximum_fusion), channel_id=1, source_target_pairs={{8,0},{16,8},{24,16},{32,24},{40,32},{48,40},{56,48},{64,56},{72,6... | collective-permute-start | bytes 2838536 | tf_op jit(solution)/shard_map/ppermute | solution.py:19
  241.3 15.0 %collective-permute-start.3 = (f32[33,8,128]{2,1,0:T(8,128)S(1)}, f32[33,8,128]{2,1,0:T(8,128)S(1)}, u32[]{:S(2)}, u32[]{:S(2)}) collective-permute-start(f32[33,8,128]{2,1,0:T(8,128)S(1)} %get-tuple-element.32), channel_id=1, source_target_pairs={{0,8},{8,16},{16,24},{24,32},{32,40},{40,48},{48,56},{56,64},{64,7... | collective-permute-start | bytes 405512 | tf_op jit(solution)/shard_map/ppermute | solution.py:19
  246.5 11.5 %collective-permute-start.2 = (f32[33,8,128]{2,1,0:T(8,128)S(1)}, f32[33,8,128]{2,1,0:T(8,128)S(1)}, u32[]{:S(2)}, u32[]{:S(2)}) collective-permute-start(f32[33,8,128]{2,1,0:T(8,128)S(1)} %get-tuple-element.31), channel_id=1, source_target_pairs={{8,0},{16,8},{24,16},{32,24},{40,32},{48,40},{56,48},{64,56},{72,6... | collective-permute-start | bytes 405512 | tf_op jit(solution)/shard_map/ppermute | solution.py:19

commit v14 on v12

--- a/solution.py
+++ b/solution.py
@@ -97,7 +97,6 @@
             images.append(lag_images(received[g - 1]))
     early = [place_tiles(image, start_tile, owner - 1, 3) for image in images]
     early = [jnp.concatenate([p[k] for p in early], axis=1) for k in range(3)]
-    early, received[-1] = lax.optimization_barrier((early, received[-1]))
     parts = [early, place_tiles(lag_images(received[-1]), start_tile, owner - 1, 3)]
     out = []
     for slots in parts:

time: 257 us -> 257 us (level)
  transfers between devices with their start and end apart: 7 -> 7, of which waited for: 4 -> 4; matrix products, arithmetic and copies ran while one was open for 17% -> 18% of each run, Pallas kernels for 15% -> 14%
where the time goes in v14:
time: 257 us; the launch traced here: 254 us
  waiting for transfers between devices  121 us (47%)
  Pallas kernels  36.8 us (14%)
  starting transfers between devices  34.3 us (13%)
  local copies, waits for them, and re-layouts  34.2 us (13%)
  other arithmetic  20.3 us (8%)
  between operations  8 us (3%)
    all_to_all x3, waiting for transfers between devices, body(): lax.all_to_all(pair, 'tm', split_axis=0, concat_axis=0, tiled=True)  117 us
    pallas_call x3, Pallas kernels, lag_images(): pl.pallas_call(lag_kernel, grid=(shots, chans // cb), in_specs=[pl.BlockS...  36.8 us
    ppermute x4, starting transfers between devices, passed_along(): return lax.ppermute(block, axis, route)  18.3 us
    another operation x3, local copies, waits for them, and re-layouts, body(): pair = jnp.stack([source_snap[:, :, cs], receiver_snap[:, :, cs]])  17.7 us
    all_to_all x3, starting transfers between devices, body(): lax.all_to_all(pair, 'tm', split_axis=0, concat_axis=0, tiled=True)  16 us
    slice x10, local copies, waits for them, and re-layouts, body(): pair = jnp.stack([source_snap[:, :, cs], receiver_snap[:, :, cs]])  14.4 us
    transpose x3, other arithmetic, body(): pair = jnp.transpose(pair, (4, 0, 1, 3, 2, 5))  12.8 us
  transfers between devices with their start and end apart: 7, of which 4 were waited for; matrix products, arithmetic and copies ran while one was open for 18% of the time, Pallas kernels for 14%

profile of v14, /device:TPU:3, one launch (start us, length us, event | category | flops | bytes accessed | tf_op | source)
XLA Modules:
  0.0 254.2 jit_solution(8904845857816559451)
XLA Ops:
  0.0 1.2 slice-done
  1.2 0.3 slice-done.2
  1.5 1.2 copy_bitcast_fusion.4
  2.7 1.5 maximum_bitcast_fusion.2
  4.3 6.0 %all-to-all-start = ((bf16[8,2,2,8,16,256]{5,4,3,2,1,0:T(8,128)(2,1)}), bf16[8,2,2,8,16,256]{5,4,3,2,1,0:T(8,128)(2,1)S(1)}, u32[]{:S(2)}, u32[]{:S(2)}) async-start(bf16[8,2,2,8,16,256]{5,4,3,2,1,0:T(8,128)(2,1)} %maximum_bitcast_fusion.2), calls=%async_computation | async-start | bytes 4194304 | tf_op jit(solution)/shard_map/all_to_all | solution.py:95
  10.3 5.3 %slice.47 = bf16[2,16,40,8,256]{4,3,2,1,0:T(8,128)(2,1)} slice(bf16[2,16,64,8,256]{4,3,2,1,0:T(8,128)(2,1)} %param.3), slice={[0:2], [0:16], [8:48], [0:8], [0:256]} | slice | bytes 10485760 | tf_op jit(solution)/shard_map/slice | solution.py:89
  15.6 5.4 %slice.48 = bf16[2,16,40,8,256]{4,3,2,1,0:T(8,128)(2,1)} slice(bf16[2,16,64,8,256]{4,3,2,1,0:T(8,128)(2,1)} %param.4), slice={[0:2], [0:16], [8:48], [0:8], [0:256]} | slice | bytes 10485760 | tf_op jit(solution)/shard_map/slice | solution.py:89
  21.0 14.1 %copy_bitcast_fusion = (bf16[1,2,16,40,8,256]{5,2,3,1,0,4:T(8,128)(2,1)}, bf16[1,2,16,40,8,256]{5,2,3,1,0,4:T(8,128)(2,1)}) fusion(bf16[2,16,40,8,256]{4,3,2,1,0:T(8,128)(2,1)} %slice.48, bf16[2,16,40,8,256]{4,3,2,1,0:T(8,128)(2,1)} %slice.47), kind=kLoop, calls=%fused_computation.1 | loop fusion | bytes 20971520 | tf_op jit(solution)/shard_map/stack | solution.py:89
  35.1 8.9 %maximum_bitcast_fusion = bf16[8,2,2,40,16,256]{5,4,3,2,1,0:T(8,128)(2,1)} fusion(bf16[1,2,16,40,8,256]{5,2,3,1,0,4:T(8,128)(2,1)} %get-tuple-element.29, bf16[1,2,16,40,8,256]{5,2,3,1,0,4:T(8,128)(2,1)} %get-tuple-element.30), kind=kLoop, calls=%fused_computation | loop fusion | flops 5242880 | bytes 20971520 | tf_op jit(solution)/shard_map/transpose | solution.py:90
  43.9 0.0 all-to-all-done.x_ref
  43.9 1.4 copy-done.2
  45.3 5.3 %all-to-all-start.1 = ((bf16[8,2,2,40,16,256]{5,4,3,2,1,0:T(8,128)(2,1)}), bf16[8,2,2,40,16,256]{5,4,3,2,1,0:T(8,128)(2,1)}, u32[]{:S(2)}, u32[]{:S(2)}) async-start(bf16[8,2,2,40,16,256]{5,4,3,2,1,0:T(8,128)(2,1)} %maximum_bitcast_fusion), calls=%async_computation.1 | async-start | bytes 20971520 | tf_op jit(solution)/shard_map/all_to_all | solution.py:95
  50.6 0.0 slice-start.1
  50.7 0.0 slice-start.3
  50.7 1.6 slice-done.1
  52.2 0.6 slice-done.3
  52.9 2.4 copy_bitcast_fusion.2
  55.3 2.4 maximum_bitcast_fusion.1
  57.7 5.8 %shard_map.37 = f32[2,2,33,8,128]{4,3,2,1,0:T(8,128)} custom-call(bf16[8,2,2,8,16,256]{5,4,3,2,1,0:T(8,128)(2,1)} %copy-done.2), custom_call_target="tpu_custom_call" | custom-call | tf_op jit(solution)/shard_map/pallas_call | solution.py:57
  63.5 102.7 %all-to-all-done.1.x_ref = bf16[8,2,2,40,16,256]{5,4,3,2,1,0:T(8,128)(2,1)} async-done(((bf16[8,2,2,40,16,256]{5,4,3,2,1,0:T(8,128)(2,1)}), bf16[8,2,2,40,16,256]{5,4,3,2,1,0:T(8,128)(2,1)}, u32[]{:S(2)}, u32[]{:S(2)}) %all-to-all-start.1) | async-done | bytes 10485792 | tf_op jit(solution)/shard_map/all_to_all | solution.py:95
  166.2 4.6 %all-to-all-start.2 = ((bf16[8,2,2,16,16,256]{5,4,3,2,1,0:T(8,128)(2,1)}), bf16[8,2,2,16,16,256]{5,4,3,2,1,0:T(8,128)(2,1)}, u32[]{:S(2)}, u32[]{:S(2)}) async-start(bf16[8,2,2,16,16,256]{5,4,3,2,1,0:T(8,128)(2,1)} %maximum_bitcast_fusion.1), calls=%async_computation.2 | async-start | bytes 8388608 | tf_op jit(solution)/shard_map/all_to_all | solution.py:95
  170.7 0.0 copy-done.4
  170.8 0.1 add_subtract_fusion
  170.8 0.7 fusion.2
  179.3 0.0 copy-start.3
  179.3 21.4 %shard_map.38 = f32[2,2,33,40,128]{4,3,2,1,0:T(8,128)} custom-call(bf16[8,2,2,40,16,256]{5,4,3,2,1,0:T(8,128)(2,1)} %all-to-all-done.1.x_ref), custom_call_target="tpu_custom_call" | custom-call | tf_op jit(solution)/shard_map/pallas_call | solution.py:57
  200.7 0.0 copy-done.3
  200.7 0.1 add_bitcast_fusion.7
  200.8 0.0 copy-start
  200.8 2.2 add_bitcast_fusion.2
  203.0 0.1 pad_maximum_fusion
  203.0 4.2 %collective-permute-start = (f32[33,48,128]{2,1,0:T(8,128)S(1)}, f32[33,48,128]{2,1,0:T(8,128)S(1)}, u32[]{:S(2)}, u32[]{:S(2)}) collective-permute-start(f32[33,48,128]{2,1,0:T(8,128)S(1)} %pad_maximum_fusion), channel_id=1, source_target_pairs={{8,0},{16,8},{24,16},{32,24},{40,32},{48,40},{56,48},{64,56},{72,6... | collective-permute-start | bytes 2433032 | tf_op jit(solution)/shard_map/ppermute | solution.py:19
  207.3 0.0 copy-done
  207.3 0.2 add_bitcast_fusion
  207.5 1.0 pad_maximum_fusion.1
  208.4 4.4 %collective-permute-start.1 = (f32[33,48,128]{2,1,0:T(8,128)}, f32[33,48,128]{2,1,0:T(8,128)}, u32[]{:S(2)}, u32[]{:S(2)}) collective-permute-start(f32[33,48,128]{2,1,0:T(8,128)} %pad_maximum_fusion.1), channel_id=1, source_target_pairs={{0,8},{8,16},{16,24},{24,32},{32,40},{40,48},{48,56},{56,64},{64,7... | collective-permute-start | bytes 2433032 | tf_op jit(solution)/shard_map/ppermute | solution.py:19
  212.8 13.9 %all-to-all-done.2.x_ref = bf16[8,2,2,16,16,256]{5,4,3,2,1,0:T(8,128)(2,1)} async-done(((bf16[8,2,2,16,16,256]{5,4,3,2,1,0:T(8,128)(2,1)}), bf16[8,2,2,16,16,256]{5,4,3,2,1,0:T(8,128)(2,1)}, u32[]{:S(2)}, u32[]{:S(2)}) %all-to-all-start.2) | async-done | bytes 4194336 | tf_op jit(solution)/shard_map/all_to_all | solution.py:95
  226.7 9.7 %shard_map.39 = f32[2,2,33,16,128]{4,3,2,1,0:T(8,128)} custom-call(bf16[8,2,2,16,16,256]{5,4,3,2,1,0:T(8,128)(2,1)} %all-to-all-done.2.x_ref), custom_call_target="tpu_custom_call" | custom-call | tf_op jit(solution)/shard_map/pallas_call | solution.py:57
  236.4 1.4 add_bitcast_fusion.4
  237.8 7.8 %collective-permute-start.2 = (f32[33,16,128]{2,1,0:T(8,128)S(1)}, f32[33,16,128]{2,1,0:T(8,128)S(1)}, u32[]{:S(2)}, u32[]{:S(2)}) collective-permute-start(f32[33,16,128]{2,1,0:T(8,128)S(1)} %get-tuple-element.19), channel_id=1, source_target_pairs={{8,0},{16,8},{24,16},{32,24},{40,32},{48,40},{56,48},{64,56},{72,6... | collective-permute-start | bytes 811016 | tf_op jit(solution)/shard_map/ppermute | solution.py:19
  245.6 1.9 collective-permute-start.3
  247.5 0.0 collective-permute-done
  247.5 0.0 collective-permute-done.1
  247.5 1.3 fusion
  248.8 0.6 collective-permute-done.2
  249.5 3.5 %collective-permute-done.3 = f32[33,16,128]{2,1,0:T(8,128)S(1)} collective-permute-done((f32[33,16,128]{2,1,0:T(8,128)S(1)}, f32[33,16,128]{2,1,0:T(8,128)S(1)}, u32[]{:S(2)}, u32[]{:S(2)}) %collective-permute-start.3) | collective-permute-done | bytes 270368 | tf_op jit(solution)/shard_map/ppermute | solution.py:19
  253.0 0.1 fusion.1
  253.1 1.1 maximum_bitcast_fusion.3
  (7 shorter events, 0.0 us)
Async XLA Ops:
  0.0 1.2 slice-start
  0.0 1.5 slice-start.2
  4.3 39.6 %all-to-all-start = ((bf16[8,2,2,8,16,256]{5,4,3,2,1,0:T(8,128)(2,1)}), bf16[8,2,2,8,16,256]{5,4,3,2,1,0:T(8,128)(2,1)S(1)}, u32[]{:S(2)}, u32[]{:S(2)}) async-start(bf16[8,2,2,8,16,256]{5,4,3,2,1,0:T(8,128)(2,1)} %maximum_bitcast_fusion.2), calls=%async_computation | async-start | bytes 4194304 | tf_op jit(solution)/shard_map/all_to_all | solution.py:95
  43.9 1.4 copy-start.2
  45.3 120.9 %all-to-all-start.1 = ((bf16[8,2,2,40,16,256]{5,4,3,2,1,0:T(8,128)(2,1)}), bf16[8,2,2,40,16,256]{5,4,3,2,1,0:T(8,128)(2,1)}, u32[]{:S(2)}, u32[]{:S(2)}) async-start(bf16[8,2,2,40,16,256]{5,4,3,2,1,0:T(8,128)(2,1)} %maximum_bitcast_fusion), calls=%async_computation.1 | async-start | bytes 20971520 | tf_op jit(solution)/shard_map/all_to_all | solution.py:95
  50.6 1.6 slice-start.1
  50.7 2.2 slice-start.3
  63.5 107.3 %copy-start.4 = (s32[2]{0:T(128)S(1)}, s32[2]{0:T(128)}, u32[]{:S(2)}) copy-start(s32[2]{0:T(128)} %param.5) | copy-start | bytes 28
  166.2 60.5 %all-to-all-start.2 = ((bf16[8,2,2,16,16,256]{5,4,3,2,1,0:T(8,128)(2,1)}), bf16[8,2,2,16,16,256]{5,4,3,2,1,0:T(8,128)(2,1)}, u32[]{:S(2)}, u32[]{:S(2)}) async-start(bf16[8,2,2,16,16,256]{5,4,3,2,1,0:T(8,128)(2,1)} %maximum_bitcast_fusion.1), calls=%async_computation.2 | async-start | bytes 8388608 | tf_op jit(solution)/shard_map/all_to_all | solution.py:95
  179.3 21.4 %copy-start.3 = (f32[2,2,33,8,128]{4,3,2,1,0:T(8,128)S(1)}, f32[2,2,33,8,128]{4,3,2,1,0:T(8,128)}, u32[]{:S(2)}) copy-start(f32[2,2,33,8,128]{4,3,2,1,0:T(8,128)} %shard_map.37) | copy-start | bytes 1622020
  200.8 6.5 %copy-start = (f32[2,2,33,40,128]{4,3,2,1,0:T(8,128)S(1)}, f32[2,2,33,40,128]{4,3,2,1,0:T(8,128)}, u32[]{:S(2)}) copy-start(f32[2,2,33,40,128]{4,3,2,1,0:T(8,128)} %shard_map.38) | copy-start | bytes 8110084
  203.0 44.5 %collective-permute-start = (f32[33,48,128]{2,1,0:T(8,128)S(1)}, f32[33,48,128]{2,1,0:T(8,128)S(1)}, u32[]{:S(2)}, u32[]{:S(2)}) collective-permute-start(f32[33,48,128]{2,1,0:T(8,128)S(1)} %pad_maximum_fusion), channel_id=1, source_target_pairs={{8,0},{16,8},{24,16},{32,24},{40,32},{48,40},{56,48},{64,56},{72,6... | collective-permute-start | bytes 2433032 | tf_op jit(solution)/shard_map/ppermute | solution.py:19
  208.4 39.1 %collective-permute-start.1 = (f32[33,48,128]{2,1,0:T(8,128)}, f32[33,48,128]{2,1,0:T(8,128)}, u32[]{:S(2)}, u32[]{:S(2)}) collective-permute-start(f32[33,48,128]{2,1,0:T(8,128)} %pad_maximum_fusion.1), channel_id=1, source_target_pairs={{0,8},{8,16},{16,24},{24,32},{32,40},{40,48},{48,56},{56,64},{64,7... | collective-permute-start | bytes 2433032 | tf_op jit(solution)/shard_map/ppermute | solution.py:19
  236.4 16.6 %copy-start.1 = (f32[2,2,33,16,128]{4,3,2,1,0:T(8,128)S(1)}, f32[2,2,33,16,128]{4,3,2,1,0:T(8,128)}, u32[]{:S(2)}) copy-start(f32[2,2,33,16,128]{4,3,2,1,0:T(8,128)} %shard_map.39) | copy-start | bytes 3244036
  237.8 11.7 %collective-permute-start.2 = (f32[33,16,128]{2,1,0:T(8,128)S(1)}, f32[33,16,128]{2,1,0:T(8,128)S(1)}, u32[]{:S(2)}, u32[]{:S(2)}) collective-permute-start(f32[33,16,128]{2,1,0:T(8,128)S(1)} %get-tuple-element.19), channel_id=1, source_target_pairs={{8,0},{16,8},{24,16},{32,24},{40,32},{48,40},{56,48},{64,56},{72,6... | collective-permute-start | bytes 811016 | tf_op jit(solution)/shard_map/ppermute | solution.py:19
  245.6 7.4 %collective-permute-start.3 = (f32[33,16,128]{2,1,0:T(8,128)S(1)}, f32[33,16,128]{2,1,0:T(8,128)S(1)}, u32[]{:S(2)}, u32[]{:S(2)}) collective-permute-start(f32[33,16,128]{2,1,0:T(8,128)S(1)} %get-tuple-element.20), channel_id=1, source_target_pairs={{0,8},{8,16},{16,24},{24,32},{32,40},{40,48},{48,56},{56,64},{64,7... | collective-permute-start | bytes 811016 | tf_op jit(solution)/shard_map/ppermute | solution.py:19

commit v15 on v12

--- a/solution.py
+++ b/solution.py
@@ -53,7 +53,7 @@
 
 def lag_images(pair):
     n_src, _, shots, chans, t16, width = pair.shape
-    cb = min(CB, chans)
+    cb = 2 * CB if chans % (2 * CB) == 0 else min(CB, chans)
     return pl.pallas_call(
         lag_kernel,
         grid=(shots, chans // cb),

time: 257 us -> 259 us (level)
  no operation moved by 1% of the time
where the time goes in v15:
time: 259 us; the launch traced here: 256 us
  waiting for transfers between devices  120 us (46%)
  Pallas kernels  39 us (15%)
  local copies, waits for them, and re-layouts  35.8 us (14%)
  starting transfers between devices  32.5 us (13%)
  other arithmetic  20.6 us (8%)
  between operations  7.87 us (3%)
    all_to_all x3, waiting for transfers between devices, body(): lax.all_to_all(pair, 'tm', split_axis=0, concat_axis=0, tiled=True)  116 us
    pallas_call x3, Pallas kernels, lag_images(): pl.pallas_call(lag_kernel, grid=(shots, chans // cb), in_specs=[pl.BlockS...  39 us
    another operation x3, local copies, waits for them, and re-layouts, body(): pair = jnp.stack([source_snap[:, :, cs], receiver_snap[:, :, cs]])  17.7 us
    ppermute x4, starting transfers between devices, passed_along(): return lax.ppermute(block, axis, route)  16.5 us
    all_to_all x3, starting transfers between devices, body(): lax.all_to_all(pair, 'tm', split_axis=0, concat_axis=0, tiled=True)  15.9 us
    slice x10, local copies, waits for them, and re-layouts, body(): pair = jnp.stack([source_snap[:, :, cs], receiver_snap[:, :, cs]])  14.4 us
    transpose x3, other arithmetic, body(): pair = jnp.transpose(pair, (4, 0, 1, 3, 2, 5))  12.8 us
  transfers between devices with their start and end apart: 7, of which 4 were waited for; matrix products, arithmetic and copies ran while one was open for 17% of the time, Pallas kernels for 15%

profile of v15, /device:TPU:3, one launch (start us, length us, event | category | flops | bytes accessed | tf_op | source)
XLA Modules:
  0.0 255.7 jit_solution(8314075714947695632)
XLA Ops:
  0.0 1.2 slice-done
  1.2 0.3 slice-done.2
  1.5 1.2 copy_bitcast_fusion.4
  2.7 1.5 maximum_bitcast_fusion.2
  4.3 6.0 %all-to-all-start = ((bf16[8,2,2,8,16,256]{5,4,3,2,1,0:T(8,128)(2,1)}), bf16[8,2,2,8,16,256]{5,4,3,2,1,0:T(8,128)(2,1)S(1)}, u32[]{:S(2)}, u32[]{:S(2)}) async-start(bf16[8,2,2,8,16,256]{5,4,3,2,1,0:T(8,128)(2,1)} %maximum_bitcast_fusion.2), calls=%async_computation | async-start | bytes 4194304 | tf_op jit(solution)/shard_map/all_to_all | solution.py:95
  10.3 5.3 %slice.47 = bf16[2,16,40,8,256]{4,3,2,1,0:T(8,128)(2,1)} slice(bf16[2,16,64,8,256]{4,3,2,1,0:T(8,128)(2,1)} %param.3), slice={[0:2], [0:16], [8:48], [0:8], [0:256]} | slice | bytes 10485760 | tf_op jit(solution)/shard_map/slice | solution.py:89
  15.6 5.4 %slice.48 = bf16[2,16,40,8,256]{4,3,2,1,0:T(8,128)(2,1)} slice(bf16[2,16,64,8,256]{4,3,2,1,0:T(8,128)(2,1)} %param.4), slice={[0:2], [0:16], [8:48], [0:8], [0:256]} | slice | bytes 10485760 | tf_op jit(solution)/shard_map/slice | solution.py:89
  21.0 14.1 %copy_bitcast_fusion = (bf16[1,2,16,40,8,256]{5,2,3,1,0,4:T(8,128)(2,1)}, bf16[1,2,16,40,8,256]{5,2,3,1,0,4:T(8,128)(2,1)}) fusion(bf16[2,16,40,8,256]{4,3,2,1,0:T(8,128)(2,1)} %slice.48, bf16[2,16,40,8,256]{4,3,2,1,0:T(8,128)(2,1)} %slice.47), kind=kLoop, calls=%fused_computation.1 | loop fusion | bytes 20971520 | tf_op jit(solution)/shard_map/stack | solution.py:89
  35.0 8.9 %maximum_bitcast_fusion = bf16[8,2,2,40,16,256]{5,4,3,2,1,0:T(8,128)(2,1)} fusion(bf16[1,2,16,40,8,256]{5,2,3,1,0,4:T(8,128)(2,1)} %get-tuple-element.37, bf16[1,2,16,40,8,256]{5,2,3,1,0,4:T(8,128)(2,1)} %get-tuple-element.38), kind=kLoop, calls=%fused_computation | loop fusion | flops 5242880 | bytes 20971520 | tf_op jit(solution)/shard_map/transpose | solution.py:90
  43.9 0.0 all-to-all-done.x_ref
  43.9 1.4 copy-done.1
  45.3 5.3 %all-to-all-start.1 = ((bf16[8,2,2,40,16,256]{5,4,3,2,1,0:T(8,128)(2,1)}), bf16[8,2,2,40,16,256]{5,4,3,2,1,0:T(8,128)(2,1)}, u32[]{:S(2)}, u32[]{:S(2)}) async-start(bf16[8,2,2,40,16,256]{5,4,3,2,1,0:T(8,128)(2,1)} %maximum_bitcast_fusion), calls=%async_computation.1 | async-start | bytes 20971520 | tf_op jit(solution)/shard_map/all_to_all | solution.py:95
  50.7 0.0 slice-start.1
  50.7 0.0 slice-start.3
  50.7 1.6 slice-done.1
  52.2 0.6 slice-done.3
  52.9 2.4 copy_bitcast_fusion.2
  55.3 2.4 maximum_bitcast_fusion.1
  57.7 5.8 %shard_map.37 = f32[2,2,33,8,128]{4,3,2,1,0:T(8,128)} custom-call(bf16[8,2,2,8,16,256]{5,4,3,2,1,0:T(8,128)(2,1)} %copy-done.1), custom_call_target="tpu_custom_call" | custom-call | tf_op jit(solution)/shard_map/pallas_call | solution.py:57
  63.5 102.7 %all-to-all-done.1.x_ref = bf16[8,2,2,40,16,256]{5,4,3,2,1,0:T(8,128)(2,1)} async-done(((bf16[8,2,2,40,16,256]{5,4,3,2,1,0:T(8,128)(2,1)}), bf16[8,2,2,40,16,256]{5,4,3,2,1,0:T(8,128)(2,1)}, u32[]{:S(2)}, u32[]{:S(2)}) %all-to-all-start.1) | async-done | bytes 10485792 | tf_op jit(solution)/shard_map/all_to_all | solution.py:95
  166.2 4.6 %all-to-all-start.2 = ((bf16[8,2,2,16,16,256]{5,4,3,2,1,0:T(8,128)(2,1)}), bf16[8,2,2,16,16,256]{5,4,3,2,1,0:T(8,128)(2,1)}, u32[]{:S(2)}, u32[]{:S(2)}) async-start(bf16[8,2,2,16,16,256]{5,4,3,2,1,0:T(8,128)(2,1)} %maximum_bitcast_fusion.1), calls=%async_computation.2 | async-start | bytes 8388608 | tf_op jit(solution)/shard_map/all_to_all | solution.py:95
  170.8 0.0 copy-done.3
  170.8 0.1 add_subtract_fusion
  170.8 0.7 fusion.1
  179.2 0.0 copy-start.2
  179.2 21.4 %shard_map.38 = f32[2,2,33,40,128]{4,3,2,1,0:T(8,128)} custom-call(bf16[8,2,2,40,16,256]{5,4,3,2,1,0:T(8,128)(2,1)} %all-to-all-done.1.x_ref), custom_call_target="tpu_custom_call" | custom-call | tf_op jit(solution)/shard_map/pallas_call | solution.py:57
  200.6 0.0 copy-done.2
  200.6 0.1 add_bitcast_fusion.5
  200.7 2.0 add_bitcast_fusion
  202.7 0.1 pad_maximum_fusion.2
  202.8 0.1 pad_maximum_fusion.1
  202.9 1.6 copy-done
  204.4 0.2 add_bitcast_fusion.2
  204.6 0.1 pad_maximum_fusion
  204.7 13.4 %all-to-all-done.2.x_ref = bf16[8,2,2,16,16,256]{5,4,3,2,1,0:T(8,128)(2,1)} async-done(((bf16[8,2,2,16,16,256]{5,4,3,2,1,0:T(8,128)(2,1)}), bf16[8,2,2,16,16,256]{5,4,3,2,1,0:T(8,128)(2,1)}, u32[]{:S(2)}, u32[]{:S(2)}) %all-to-all-start.2) | async-done | bytes 4194336 | tf_op jit(solution)/shard_map/all_to_all | solution.py:95
  218.0 5.0 %collective-permute-start = (f32[33,48,128]{2,1,0:T(8,128)S(1)}, f32[33,48,128]{2,1,0:T(8,128)}, u32[]{:S(2)}, u32[]{:S(2)}) collective-permute-start(f32[33,48,128]{2,1,0:T(8,128)S(1)} %pad_maximum_fusion), channel_id=1, source_target_pairs={{8,0},{16,8},{24,16},{32,24},{40,32},{48,40},{56,48},{64,56},{72,6... | collective-permute-start | bytes 2433032 | tf_op jit(solution)/shard_map/ppermute | solution.py:19
  223.1 4.4 %collective-permute-start.1 = (f32[33,48,128]{2,1,0:T(8,128)S(1)}, f32[33,48,128]{2,1,0:T(8,128)}, u32[]{:S(2)}, u32[]{:S(2)}) collective-permute-start(f32[33,48,128]{2,1,0:T(8,128)S(1)} %pad_maximum_fusion.2), channel_id=1, source_target_pairs={{0,8},{8,16},{16,24},{24,32},{32,40},{40,48},{48,56},{56,64},{64,7... | collective-permute-start | bytes 2433032 | tf_op jit(solution)/shard_map/ppermute | solution.py:19
  227.5 11.9 %shard_map.39 = f32[2,2,33,16,128]{4,3,2,1,0:T(8,128)} custom-call(bf16[8,2,2,16,16,256]{5,4,3,2,1,0:T(8,128)(2,1)} %all-to-all-done.2.x_ref), custom_call_target="tpu_custom_call" | custom-call | tf_op jit(solution)/shard_map/pallas_call | solution.py:57
  239.4 1.3 add_bitcast_fusion.4
  240.7 1.9 collective-permute-start.2
  242.7 5.1 %collective-permute-start.3 = (f32[33,16,128]{2,1,0:T(8,128)S(1)}, f32[33,16,128]{2,1,0:T(8,128)S(1)}, u32[]{:S(2)}, u32[]{:S(2)}) collective-permute-start(f32[33,16,128]{2,1,0:T(8,128)S(1)} %get-tuple-element.28), channel_id=1, source_target_pairs={{0,8},{8,16},{16,24},{24,32},{32,40},{40,48},{48,56},{56,64},{64,7... | collective-permute-start | bytes 811016 | tf_op jit(solution)/shard_map/ppermute | solution.py:19
  247.8 2.2 collective-permute-done.2
  250.0 1.7 collective-permute-done.3
  251.7 1.3 fusion
  253.0 0.0 collective-permute-done
  253.0 0.0 collective-permute-done.1
  253.0 1.5 add_add_fusion
  254.6 1.1 maximum_bitcast_fusion.3
  (6 shorter events, 0.0 us)
Async XLA Ops:
  0.0 1.2 slice-start
  0.0 1.5 slice-start.2
  4.3 39.7 %all-to-all-start = ((bf16[8,2,2,8,16,256]{5,4,3,2,1,0:T(8,128)(2,1)}), bf16[8,2,2,8,16,256]{5,4,3,2,1,0:T(8,128)(2,1)S(1)}, u32[]{:S(2)}, u32[]{:S(2)}) async-start(bf16[8,2,2,8,16,256]{5,4,3,2,1,0:T(8,128)(2,1)} %maximum_bitcast_fusion.2), calls=%async_computation | async-start | bytes 4194304 | tf_op jit(solution)/shard_map/all_to_all | solution.py:95
  43.9 1.4 copy-start.1
  45.3 120.9 %all-to-all-start.1 = ((bf16[8,2,2,40,16,256]{5,4,3,2,1,0:T(8,128)(2,1)}), bf16[8,2,2,40,16,256]{5,4,3,2,1,0:T(8,128)(2,1)}, u32[]{:S(2)}, u32[]{:S(2)}) async-start(bf16[8,2,2,40,16,256]{5,4,3,2,1,0:T(8,128)(2,1)} %maximum_bitcast_fusion), calls=%async_computation.1 | async-start | bytes 20971520 | tf_op jit(solution)/shard_map/all_to_all | solution.py:95
  50.7 1.6 slice-start.1
  50.7 2.2 slice-start.3
  63.5 107.3 %copy-start.3 = (s32[2]{0:T(128)S(1)}, s32[2]{0:T(128)}, u32[]{:S(2)}) copy-start(s32[2]{0:T(128)} %param.5) | copy-start | bytes 28
  166.2 51.8 %all-to-all-start.2 = ((bf16[8,2,2,16,16,256]{5,4,3,2,1,0:T(8,128)(2,1)}), bf16[8,2,2,16,16,256]{5,4,3,2,1,0:T(8,128)(2,1)}, u32[]{:S(2)}, u32[]{:S(2)}) async-start(bf16[8,2,2,16,16,256]{5,4,3,2,1,0:T(8,128)(2,1)} %maximum_bitcast_fusion.1), calls=%async_computation.2 | async-start | bytes 8388608 | tf_op jit(solution)/shard_map/all_to_all | solution.py:95
  179.2 21.4 %copy-start.2 = (f32[2,2,33,8,128]{4,3,2,1,0:T(8,128)S(1)}, f32[2,2,33,8,128]{4,3,2,1,0:T(8,128)}, u32[]{:S(2)}) copy-start(f32[2,2,33,8,128]{4,3,2,1,0:T(8,128)} %shard_map.37) | copy-start | bytes 1622020
  202.7 1.8 copy-start
  218.0 35.0 %collective-permute-start = (f32[33,48,128]{2,1,0:T(8,128)S(1)}, f32[33,48,128]{2,1,0:T(8,128)}, u32[]{:S(2)}, u32[]{:S(2)}) collective-permute-start(f32[33,48,128]{2,1,0:T(8,128)S(1)} %pad_maximum_fusion), channel_id=1, source_target_pairs={{8,0},{16,8},{24,16},{32,24},{40,32},{48,40},{56,48},{64,56},{72,6... | collective-permute-start | bytes 2433032 | tf_op jit(solution)/shard_map/ppermute | solution.py:19
  223.1 30.0 %collective-permute-start.1 = (f32[33,48,128]{2,1,0:T(8,128)S(1)}, f32[33,48,128]{2,1,0:T(8,128)}, u32[]{:S(2)}, u32[]{:S(2)}) collective-permute-start(f32[33,48,128]{2,1,0:T(8,128)S(1)} %pad_maximum_fusion.2), channel_id=1, source_target_pairs={{0,8},{8,16},{16,24},{24,32},{32,40},{40,48},{48,56},{56,64},{64,7... | collective-permute-start | bytes 2433032 | tf_op jit(solution)/shard_map/ppermute | solution.py:19
  240.7 9.3 %collective-permute-start.2 = (f32[33,16,128]{2,1,0:T(8,128)S(1)}, f32[33,16,128]{2,1,0:T(8,128)S(1)}, u32[]{:S(2)}, u32[]{:S(2)}) collective-permute-start(f32[33,16,128]{2,1,0:T(8,128)S(1)} %get-tuple-element.27), channel_id=1, source_target_pairs={{8,0},{16,8},{24,16},{32,24},{40,32},{48,40},{56,48},{64,56},{72,6... | collective-permute-start | bytes 811016 | tf_op jit(solution)/shard_map/ppermute | solution.py:19
  242.7 9.0 %collective-permute-start.3 = (f32[33,16,128]{2,1,0:T(8,128)S(1)}, f32[33,16,128]{2,1,0:T(8,128)S(1)}, u32[]{:S(2)}, u32[]{:S(2)}) collective-permute-start(f32[33,16,128]{2,1,0:T(8,128)S(1)} %get-tuple-element.28), channel_id=1, source_target_pairs={{0,8},{8,16},{16,24},{24,32},{32,40},{40,48},{48,56},{56,64},{64,7... | collective-permute-start | bytes 811016 | tf_op jit(solution)/shard_map/ppermute | solution.py:19

commit v16 on v13

--- a/solution.py
+++ b/solution.py
@@ -10,7 +10,7 @@
 LAGS = 33
 TILE = 128
 CB = 8
-CHUNKS = (8, 48, 8)
+CHUNKS = (16, 40, 8)
 
 
 def passed_along(block, axis, distance):

time: 263 us -> 257 us (0.977)
  waiting for transfers between devices: 147 us -> 125 us
  local copies, waits for them, and re-layouts: 21.8 us -> 32.9 us
  other arithmetic: 18.2 us -> 23.3 us
    all_to_all x3, waiting for transfers between devices: 137 us -> 116 us  [body(): lax.all_to_all(pair, 'tm', split_axis=0, concat_axis=0, tiled=True)]
    another operation x3, local copies, waits for them, and re-layouts: 10.8 us -> 17.7 us  [body(): pair = jnp.stack([source_snap[:, :, cs], receiver_snap[:, :, cs]])]
    slice x6 -> x10, local copies, waits for them, and re-layouts: 8.98 us -> 14.4 us  [body(): pair = jnp.stack([source_snap[:, :, cs], receiver_snap[:, :, cs]])]
    transpose x3, other arithmetic: 8.32 us -> 12.8 us  [body(): pair = jnp.transpose(pair, (4, 0, 1, 3, 2, 5))]
  transfers between devices with their start and end apart: 7 -> 7, of which waited for: 4 -> 3; matrix products, arithmetic and copies ran while one was open for 9% -> 17% of each run, Pallas kernels for 14% -> 14%
where the time goes in v16:
time: 257 us; the launch traced here: 256 us
  waiting for transfers between devices  125 us (49%)
  Pallas kernels  36.9 us (14%)
  local copies, waits for them, and re-layouts  32.9 us (13%)
  starting transfers between devices  31.1 us (12%)
  other arithmetic  23.3 us (9%)
  between operations  7.25 us (3%)
    all_to_all x3, waiting for transfers between devices, body(): lax.all_to_all(pair, 'tm', split_axis=0, concat_axis=0, tiled=True)  116 us
    pallas_call x3, Pallas kernels, lag_images(): pl.pallas_call(lag_kernel, grid=(shots, chans // cb), in_specs=[pl.BlockS...  36.9 us
    another operation x3, local copies, waits for them, and re-layouts, body(): pair = jnp.stack([source_snap[:, :, cs], receiver_snap[:, :, cs]])  17.7 us
    all_to_all x3, starting transfers between devices, body(): lax.all_to_all(pair, 'tm', split_axis=0, concat_axis=0, tiled=True)  15.9 us
    ppermute x4, starting transfers between devices, passed_along(): return lax.ppermute(block, axis, route)  15.1 us
    slice x10, local copies, waits for them, and re-layouts, body(): pair = jnp.stack([source_snap[:, :, cs], receiver_snap[:, :, cs]])  14.4 us
    transpose x3, other arithmetic, body(): pair = jnp.transpose(pair, (4, 0, 1, 3, 2, 5))  12.8 us
    ppermute x4, waiting for transfers between devices, passed_along(): return lax.ppermute(block, axis, route)  8.63 us
  transfers between devices with their start and end apart: 7, of which 3 were waited for; matrix products, arithmetic and copies ran while one was open for 17% of the time, Pallas kernels for 14%

profile of v16, /device:TPU:3, one launch (start us, length us, event | category | flops | bytes accessed | tf_op | source)
XLA Modules:
  0.0 256.2 jit_solution(4848382120445236136)
XLA Ops:
  0.0 1.6 slice-done
  1.6 0.6 slice-done.2
  2.2 2.4 copy_bitcast_fusion.2
  4.6 2.3 maximum_bitcast_fusion.1
  7.0 6.0 %all-to-all-start = ((bf16[8,2,2,16,16,256]{5,4,3,2,1,0:T(8,128)(2,1)}), bf16[8,2,2,16,16,256]{5,4,3,2,1,0:T(8,128)(2,1)}, u32[]{:S(2)}, u32[]{:S(2)}) async-start(bf16[8,2,2,16,16,256]{5,4,3,2,1,0:T(8,128)(2,1)} %maximum_bitcast_fusion.1), calls=%async_computation | async-start | bytes 8388608 | tf_op jit(solution)/shard_map/all_to_all | solution.py:95
  13.0 5.3 %slice.47 = bf16[2,16,40,8,256]{4,3,2,1,0:T(8,128)(2,1)} slice(bf16[2,16,64,8,256]{4,3,2,1,0:T(8,128)(2,1)} %param.3), slice={[0:2], [0:16], [16:56], [0:8], [0:256]} | slice | bytes 10485760 | tf_op jit(solution)/shard_map/slice | solution.py:89
  18.3 5.4 %slice.48 = bf16[2,16,40,8,256]{4,3,2,1,0:T(8,128)(2,1)} slice(bf16[2,16,64,8,256]{4,3,2,1,0:T(8,128)(2,1)} %param.4), slice={[0:2], [0:16], [16:56], [0:8], [0:256]} | slice | bytes 10485760 | tf_op jit(solution)/shard_map/slice | solution.py:89
  23.7 14.1 %copy_bitcast_fusion = (bf16[1,2,16,40,8,256]{5,2,3,1,0,4:T(8,128)(2,1)}, bf16[1,2,16,40,8,256]{5,2,3,1,0,4:T(8,128)(2,1)}) fusion(bf16[2,16,40,8,256]{4,3,2,1,0:T(8,128)(2,1)} %slice.48, bf16[2,16,40,8,256]{4,3,2,1,0:T(8,128)(2,1)} %slice.47), kind=kLoop, calls=%fused_computation.1 | loop fusion | bytes 20971520 | tf_op jit(solution)/shard_map/stack | solution.py:89
  37.8 8.9 %maximum_bitcast_fusion = bf16[8,2,2,40,16,256]{5,4,3,2,1,0:T(8,128)(2,1)} fusion(bf16[1,2,16,40,8,256]{5,2,3,1,0,4:T(8,128)(2,1)} %get-tuple-element.37, bf16[1,2,16,40,8,256]{5,2,3,1,0,4:T(8,128)(2,1)} %get-tuple-element.38), kind=kLoop, calls=%fused_computation | loop fusion | flops 5242880 | bytes 20971520 | tf_op jit(solution)/shard_map/transpose | solution.py:90
  46.6 15.1 %all-to-all-done.x_ref = bf16[8,2,2,16,16,256]{5,4,3,2,1,0:T(8,128)(2,1)} async-done(((bf16[8,2,2,16,16,256]{5,4,3,2,1,0:T(8,128)(2,1)}), bf16[8,2,2,16,16,256]{5,4,3,2,1,0:T(8,128)(2,1)}, u32[]{:S(2)}, u32[]{:S(2)}) %all-to-all-start) | async-done | bytes 4194336 | tf_op jit(solution)/shard_map/all_to_all | solution.py:95
  61.7 5.3 %all-to-all-start.1 = ((bf16[8,2,2,40,16,256]{5,4,3,2,1,0:T(8,128)(2,1)}), bf16[8,2,2,40,16,256]{5,4,3,2,1,0:T(8,128)(2,1)}, u32[]{:S(2)}, u32[]{:S(2)}) async-start(bf16[8,2,2,40,16,256]{5,4,3,2,1,0:T(8,128)(2,1)} %maximum_bitcast_fusion), calls=%async_computation.1 | async-start | bytes 20971520 | tf_op jit(solution)/shard_map/all_to_all | solution.py:95
  67.1 0.0 slice-start.1
  67.1 0.0 slice-start.3
  67.1 1.2 slice-done.1
  68.3 0.3 slice-done.3
  68.6 1.2 copy_bitcast_fusion.4
  69.8 1.6 maximum_bitcast_fusion.2
  71.4 9.6 %shard_map.37 = f32[2,2,33,16,128]{4,3,2,1,0:T(8,128)} custom-call(bf16[8,2,2,16,16,256]{5,4,3,2,1,0:T(8,128)(2,1)} %all-to-all-done.x_ref), custom_call_target="tpu_custom_call" | custom-call | tf_op jit(solution)/shard_map/pallas_call | solution.py:57
  81.0 101.0 %all-to-all-done.1.x_ref = bf16[8,2,2,40,16,256]{5,4,3,2,1,0:T(8,128)(2,1)} async-done(((bf16[8,2,2,40,16,256]{5,4,3,2,1,0:T(8,128)(2,1)}), bf16[8,2,2,40,16,256]{5,4,3,2,1,0:T(8,128)(2,1)}, u32[]{:S(2)}, u32[]{:S(2)}) %all-to-all-start.1) | async-done | bytes 10485792 | tf_op jit(solution)/shard_map/all_to_all | solution.py:95
  182.1 4.6 %all-to-all-start.2 = ((bf16[8,2,2,8,16,256]{5,4,3,2,1,0:T(8,128)(2,1)}), bf16[8,2,2,8,16,256]{5,4,3,2,1,0:T(8,128)(2,1)S(1)}, u32[]{:S(2)}, u32[]{:S(2)}) async-start(bf16[8,2,2,8,16,256]{5,4,3,2,1,0:T(8,128)(2,1)} %maximum_bitcast_fusion.2), calls=%async_computation.2 | async-start | bytes 4194304 | tf_op jit(solution)/shard_map/all_to_all | solution.py:95
  186.6 0.0 copy-done.4
  186.6 0.1 add_subtract_fusion
  186.7 0.6 fusion.1
  194.4 0.0 copy-start.1
  194.4 21.4 %shard_map.38 = f32[2,2,33,40,128]{4,3,2,1,0:T(8,128)} custom-call(bf16[8,2,2,40,16,256]{5,4,3,2,1,0:T(8,128)(2,1)} %all-to-all-done.1.x_ref), custom_call_target="tpu_custom_call" | custom-call | tf_op jit(solution)/shard_map/pallas_call | solution.py:57
  215.8 0.1 add_bitcast_fusion.3
  216.0 2.0 add_bitcast_fusion
  218.0 1.0 pad_maximum_fusion.2
  219.0 1.0 pad_maximum_fusion.1
  220.0 0.1 add_bitcast_fusion.5
  220.1 0.2 copy-done
  220.3 0.2 add_bitcast_fusion.2
  220.5 1.0 pad_maximum_fusion
  221.5 0.0 all-to-all-done.2.x_ref
  221.5 3.6 %collective-permute-start = (f32[33,56,128]{2,1,0:T(8,128)}, f32[33,56,128]{2,1,0:T(8,128)}, u32[]{:S(2)}, u32[]{:S(2)}) collective-permute-start(f32[33,56,128]{2,1,0:T(8,128)} %pad_maximum_fusion), channel_id=1, source_target_pairs={{8,0},{16,8},{24,16},{32,24},{40,32},{48,40},{56,48},{64,56},{72,6... | collective-permute-start | bytes 2838536 | tf_op jit(solution)/shard_map/ppermute | solution.py:19
  225.1 4.4 %collective-permute-start.1 = (f32[33,56,128]{2,1,0:T(8,128)}, f32[33,56,128]{2,1,0:T(8,128)}, u32[]{:S(2)}, u32[]{:S(2)}) collective-permute-start(f32[33,56,128]{2,1,0:T(8,128)} %pad_maximum_fusion.2), channel_id=1, source_target_pairs={{0,8},{8,16},{16,24},{24,32},{32,40},{40,48},{48,56},{56,64},{64,7... | collective-permute-start | bytes 2838536 | tf_op jit(solution)/shard_map/ppermute | solution.py:19
  229.6 0.0 copy-done.2
  229.6 5.8 %shard_map.39 = f32[2,2,33,8,128]{4,3,2,1,0:T(8,128)} custom-call(bf16[8,2,2,8,16,256]{5,4,3,2,1,0:T(8,128)(2,1)} %copy-done.2), custom_call_target="tpu_custom_call" | custom-call | tf_op jit(solution)/shard_map/pallas_call | solution.py:57
  235.4 1.2 add_bitcast_fusion.7
  236.6 1.9 collective-permute-start.2
  238.5 5.1 %collective-permute-start.3 = (f32[33,8,128]{2,1,0:T(8,128)S(1)}, f32[33,8,128]{2,1,0:T(8,128)S(1)}, u32[]{:S(2)}, u32[]{:S(2)}) collective-permute-start(f32[33,8,128]{2,1,0:T(8,128)S(1)} %get-tuple-element.30), channel_id=1, source_target_pairs={{0,8},{8,16},{16,24},{24,32},{32,40},{40,48},{48,56},{56,64},{64,7... | collective-permute-start | bytes 405512 | tf_op jit(solution)/shard_map/ppermute | solution.py:19
  243.6 8.6 %collective-permute-done.2 = f32[33,8,128]{2,1,0:T(8,128)S(1)} collective-permute-done((f32[33,8,128]{2,1,0:T(8,128)S(1)}, f32[33,8,128]{2,1,0:T(8,128)S(1)}, u32[]{:S(2)}, u32[]{:S(2)}) %collective-permute-start.2) | collective-permute-done | bytes 135200 | tf_op jit(solution)/shard_map/ppermute | solution.py:19
  252.3 0.0 collective-permute-done.3
  252.3 1.2 fusion
  253.4 0.0 collective-permute-done
  253.4 0.0 collective-permute-done.1
  253.5 1.6 add_add_fusion
  255.1 1.1 maximum_bitcast_fusion.3
  (8 shorter events, 0.0 us)
Async XLA Ops:
  0.0 1.6 slice-start
  0.0 2.2 slice-start.2
  7.0 54.7 %all-to-all-start = ((bf16[8,2,2,16,16,256]{5,4,3,2,1,0:T(8,128)(2,1)}), bf16[8,2,2,16,16,256]{5,4,3,2,1,0:T(8,128)(2,1)}, u32[]{:S(2)}, u32[]{:S(2)}) async-start(bf16[8,2,2,16,16,256]{5,4,3,2,1,0:T(8,128)(2,1)} %maximum_bitcast_fusion.1), calls=%async_computation | async-start | bytes 8388608 | tf_op jit(solution)/shard_map/all_to_all | solution.py:95
  61.7 120.3 %all-to-all-start.1 = ((bf16[8,2,2,40,16,256]{5,4,3,2,1,0:T(8,128)(2,1)}), bf16[8,2,2,40,16,256]{5,4,3,2,1,0:T(8,128)(2,1)}, u32[]{:S(2)}, u32[]{:S(2)}) async-start(bf16[8,2,2,40,16,256]{5,4,3,2,1,0:T(8,128)(2,1)} %maximum_bitcast_fusion), calls=%async_computation.1 | async-start | bytes 20971520 | tf_op jit(solution)/shard_map/all_to_all | solution.py:95
  67.1 1.2 slice-start.1
  67.1 1.5 slice-start.3
  81.0 105.6 %copy-start.4 = (s32[2]{0:T(128)S(1)}, s32[2]{0:T(128)}, u32[]{:S(2)}) copy-start(s32[2]{0:T(128)} %param.5) | copy-start | bytes 28
  182.1 39.4 %all-to-all-start.2 = ((bf16[8,2,2,8,16,256]{5,4,3,2,1,0:T(8,128)(2,1)}), bf16[8,2,2,8,16,256]{5,4,3,2,1,0:T(8,128)(2,1)S(1)}, u32[]{:S(2)}, u32[]{:S(2)}) async-start(bf16[8,2,2,8,16,256]{5,4,3,2,1,0:T(8,128)(2,1)} %maximum_bitcast_fusion.2), calls=%async_computation.2 | async-start | bytes 4194304 | tf_op jit(solution)/shard_map/all_to_all | solution.py:95
  194.4 21.4 %copy-start.1 = (f32[2,2,33,16,128]{4,3,2,1,0:T(8,128)S(1)}, f32[2,2,33,16,128]{4,3,2,1,0:T(8,128)}, u32[]{:S(2)}) copy-start(f32[2,2,33,16,128]{4,3,2,1,0:T(8,128)} %shard_map.37) | copy-start | bytes 3244036
  218.0 2.3 copy-start
  220.5 33.0 %copy-start.3 = (f32[33,56,128]{2,1,0:T(8,128)S(1)}, f32[33,56,128]{2,1,0:T(8,128)}, u32[]{:S(2)}) copy-start(f32[33,56,128]{2,1,0:T(8,128)} %pad_maximum_fusion.1) | copy-start | bytes 2838532
  221.5 8.1 %copy-start.2 = (bf16[8,2,2,8,16,256]{5,4,3,2,1,0:T(8,128)(2,1)}, bf16[8,2,2,8,16,256]{5,4,3,2,1,0:T(8,128)(2,1)S(1)}, u32[]{:S(2)}) copy-start(bf16[8,2,2,8,16,256]{5,4,3,2,1,0:T(8,128)(2,1)S(1)} %all-to-all-done.2.x_ref) | copy-start | bytes 6291460
  221.5 31.9 %collective-permute-start = (f32[33,56,128]{2,1,0:T(8,128)}, f32[33,56,128]{2,1,0:T(8,128)}, u32[]{:S(2)}, u32[]{:S(2)}) collective-permute-start(f32[33,56,128]{2,1,0:T(8,128)} %pad_maximum_fusion), channel_id=1, source_target_pairs={{8,0},{16,8},{24,16},{32,24},{40,32},{48,40},{56,48},{64,56},{72,6... | collective-permute-start | bytes 2838536 | tf_op jit(solution)/shard_map/ppermute | solution.py:19
  225.1 28.3 %collective-permute-start.1 = (f32[33,56,128]{2,1,0:T(8,128)}, f32[33,56,128]{2,1,0:T(8,128)}, u32[]{:S(2)}, u32[]{:S(2)}) collective-permute-start(f32[33,56,128]{2,1,0:T(8,128)} %pad_maximum_fusion.2), channel_id=1, source_target_pairs={{0,8},{8,16},{16,24},{24,32},{32,40},{40,48},{48,56},{56,64},{64,7... | collective-permute-start | bytes 2838536 | tf_op jit(solution)/shard_map/ppermute | solution.py:19
  236.6 15.7 %collective-permute-start.2 = (f32[33,8,128]{2,1,0:T(8,128)S(1)}, f32[33,8,128]{2,1,0:T(8,128)S(1)}, u32[]{:S(2)}, u32[]{:S(2)}) collective-permute-start(f32[33,8,128]{2,1,0:T(8,128)S(1)} %get-tuple-element.29), channel_id=1, source_target_pairs={{8,0},{16,8},{24,16},{32,24},{40,32},{48,40},{56,48},{64,56},{72,6... | collective-permute-start | bytes 405512 | tf_op jit(solution)/shard_map/ppermute | solution.py:19
  238.5 13.8 %collective-permute-start.3 = (f32[33,8,128]{2,1,0:T(8,128)S(1)}, f32[33,8,128]{2,1,0:T(8,128)S(1)}, u32[]{:S(2)}, u32[]{:S(2)}) collective-permute-start(f32[33,8,128]{2,1,0:T(8,128)S(1)} %get-tuple-element.30), channel_id=1, source_target_pairs={{0,8},{8,16},{16,24},{24,32},{32,40},{40,48},{48,56},{56,64},{64,7... | collective-permute-start | bytes 405512 | tf_op jit(solution)/shard_map/ppermute | solution.py:19

commit v17 on v16

--- a/solution.py
+++ b/solution.py
@@ -10,7 +10,7 @@
 LAGS = 33
 TILE = 128
 CB = 8
-CHUNKS = (16, 40, 8)
+CHUNKS = (16, 32, 16)
 
 
 def passed_along(block, axis, distance):

time: 257 us -> 255 us (level)
  other arithmetic: 23.3 us -> 17.3 us
  waiting for transfers between devices: 125 us -> 129 us
  local copies, waits for them, and re-layouts: 32.9 us -> 29.4 us
    slice x10 -> x6, local copies, waits for them, and re-layouts: 14.4 us -> 8.07 us  [body(): pair = jnp.stack([source_snap[:, :, cs], receiver_snap[:, :, cs]])]
    all_to_all x3, waiting for transfers between devices: 116 us -> 122 us  [body(): lax.all_to_all(pair, 'tm', split_axis=0, concat_axis=0, tiled=True)]
    unnamed x10, local copies, waits for them, and re-layouts: 0.23 us -> 3.32 us
    concatenate x3, other arithmetic: 3.03 us -> 0.16 us  [body(): early = [jnp.concatenate([p[k] for p in early], axis=1) for k in range(3)]]
  transfers between devices with their start and end apart: 7 -> 7, of which waited for: 3 -> 5; matrix products, arithmetic and copies ran while one was open for 17% -> 11% of each run, Pallas kernels for 14% -> 15%
where the time goes in v17:
time: 255 us; the launch traced here: 253 us
  waiting for transfers between devices  129 us (51%)
  Pallas kernels  36.9 us (14%)
  starting transfers between devices  32.7 us (13%)
  local copies, waits for them, and re-layouts  29.4 us (12%)
  other arithmetic  17.3 us (7%)
  between operations  7.49 us (3%)
    all_to_all x3, waiting for transfers between devices, body(): lax.all_to_all(pair, 'tm', split_axis=0, concat_axis=0, tiled=True)  122 us
    pallas_call x3, Pallas kernels, lag_images(): pl.pallas_call(lag_kernel, grid=(shots, chans // cb), in_specs=[pl.BlockS...  36.9 us
    another operation x3, local copies, waits for them, and re-layouts, body(): pair = jnp.stack([source_snap[:, :, cs], receiver_snap[:, :, cs]])  17.3 us
    ppermute x4, starting transfers between devices, passed_along(): return lax.ppermute(block, axis, route)  16.9 us
    all_to_all x3, starting transfers between devices, body(): lax.all_to_all(pair, 'tm', split_axis=0, concat_axis=0, tiled=True)  15.8 us
    transpose x3, other arithmetic, body(): pair = jnp.transpose(pair, (4, 0, 1, 3, 2, 5))  10.9 us
    slice x6, local copies, waits for them, and re-layouts, body(): pair = jnp.stack([source_snap[:, :, cs], receiver_snap[:, :, cs]])  8.07 us
    ppermute x4, waiting for transfers between devices, passed_along(): return lax.ppermute(block, axis, route)  7.36 us
  transfers between devices with their start and end apart: 7, of which 5 were waited for; matrix products, arithmetic and copies ran while one was open for 11% of the time, Pallas kernels for 15%

profile of v17, /device:TPU:3, one launch (start us, length us, event | category | flops | bytes accessed | tf_op | source)
XLA Modules:
  0.0 253.2 jit_solution(6619625461538594985)
XLA Ops:
  0.0 2.7 %fusion.2 = (bf16[2,16,16,8,256]{4,3,2,1,0:T(8,128)(2,1)S(1)}, bf16[2,16,16,8,256]{4,3,2,1,0:T(8,128)(2,1)S(1)}) fusion(bf16[2,16,64,8,256]{4,3,2,1,0:T(8,128)(2,1)} %param.4), kind=kLoop, calls=%fused_computation.26 | loop fusion | bytes 8388608 | tf_op jit(solution)/shard_map/slice | solution.py:89
  2.7 1.9 copy-done.1
  4.6 1.9 fusion.1
  6.5 2.4 copy_bitcast_fusion.2
  9.0 2.3 maximum_bitcast_fusion.2
  11.3 6.0 %all-to-all-start = ((bf16[8,2,2,16,16,256]{5,4,3,2,1,0:T(8,128)(2,1)}), bf16[8,2,2,16,16,256]{5,4,3,2,1,0:T(8,128)(2,1)}, u32[]{:S(2)}, u32[]{:S(2)}) async-start(bf16[8,2,2,16,16,256]{5,4,3,2,1,0:T(8,128)(2,1)} %maximum_bitcast_fusion.2), calls=%async_computation | async-start | bytes 8388608 | tf_op jit(solution)/shard_map/all_to_all | solution.py:95
  17.3 0.0 slice-start.1
  17.3 2.2 slice-done
  19.5 1.3 slice-done.1
  20.8 10.9 %copy_bitcast_fusion = (bf16[1,2,16,32,8,256]{5,2,3,1,0,4:T(8,128)(2,1)S(1)}, bf16[1,2,16,32,8,256]{5,2,3,1,0,4:T(8,128)(2,1)}) fusion(bf16[2,16,32,8,256]{4,3,2,1,0:T(8,128)(2,1)S(1)} %slice-done, bf16[2,16,32,8,256]{4,3,2,1,0:T(8,128)(2,1)S(1)} %slice-done.1), kind=kLoop, calls=%fused_computation.3 | loop fusion | bytes 16777216 | tf_op jit(solution)/shard_map/stack | solution.py:89
  31.7 6.2 %maximum_bitcast_fusion = bf16[8,2,2,32,16,256]{5,4,3,2,1,0:T(8,128)(2,1)} fusion(bf16[1,2,16,32,8,256]{5,2,3,1,0,4:T(8,128)(2,1)S(1)} %get-tuple-element.41, bf16[1,2,16,32,8,256]{5,2,3,1,0,4:T(8,128)(2,1)} %get-tuple-element.42), kind=kLoop, calls=%fused_computation | loop fusion | flops 4194304 | bytes 16777216 | tf_op jit(solution)/shard_map/transpose | solution.py:90
  37.9 28.1 %all-to-all-done.x_ref = bf16[8,2,2,16,16,256]{5,4,3,2,1,0:T(8,128)(2,1)} async-done(((bf16[8,2,2,16,16,256]{5,4,3,2,1,0:T(8,128)(2,1)}), bf16[8,2,2,16,16,256]{5,4,3,2,1,0:T(8,128)(2,1)}, u32[]{:S(2)}, u32[]{:S(2)}) %all-to-all-start) | async-done | bytes 4194336 | tf_op jit(solution)/shard_map/all_to_all | solution.py:95
  66.0 5.2 %all-to-all-start.1 = ((bf16[8,2,2,32,16,256]{5,4,3,2,1,0:T(8,128)(2,1)}), bf16[8,2,2,32,16,256]{5,4,3,2,1,0:T(8,128)(2,1)}, u32[]{:S(2)}, u32[]{:S(2)}) async-start(bf16[8,2,2,32,16,256]{5,4,3,2,1,0:T(8,128)(2,1)} %maximum_bitcast_fusion), calls=%async_computation.1 | async-start | bytes 16777216 | tf_op jit(solution)/shard_map/all_to_all | solution.py:95
  71.2 4.0 %copy_bitcast_fusion.4 = (bf16[1,2,16,16,8,256]{5,2,3,1,0,4:T(8,128)(2,1)S(1)}, bf16[1,2,16,16,8,256]{5,2,3,1,0,4:T(8,128)(2,1)S(1)}) fusion(bf16[2,16,16,8,256]{4,3,2,1,0:T(8,128)(2,1)S(1)} %get-tuple-element.28, bf16[2,16,16,8,256]{4,3,2,1,0:T(8,128)(2,1)} %get-tuple-element.26), kind=kLoop, calls=%fused_computation.7 | loop fusion | bytes 8388608 | tf_op jit(solution)/shard_map/stack | solution.py:89
  75.2 2.3 maximum_bitcast_fusion.1
  77.5 9.7 %shard_map.37 = f32[2,2,33,16,128]{4,3,2,1,0:T(8,128)} custom-call(bf16[8,2,2,16,16,256]{5,4,3,2,1,0:T(8,128)(2,1)} %all-to-all-done.x_ref), custom_call_target="tpu_custom_call" | custom-call | tf_op jit(solution)/shard_map/pallas_call | solution.py:57
  87.2 76.5 %all-to-all-done.1.x_ref = bf16[8,2,2,32,16,256]{5,4,3,2,1,0:T(8,128)(2,1)} async-done(((bf16[8,2,2,32,16,256]{5,4,3,2,1,0:T(8,128)(2,1)}), bf16[8,2,2,32,16,256]{5,4,3,2,1,0:T(8,128)(2,1)}, u32[]{:S(2)}, u32[]{:S(2)}) %all-to-all-start.1) | async-done | bytes 8388640 | tf_op jit(solution)/shard_map/all_to_all | solution.py:95
  163.7 4.6 %all-to-all-start.2 = ((bf16[8,2,2,16,16,256]{5,4,3,2,1,0:T(8,128)(2,1)}), bf16[8,2,2,16,16,256]{5,4,3,2,1,0:T(8,128)(2,1)}, u32[]{:S(2)}, u32[]{:S(2)}) async-start(bf16[8,2,2,16,16,256]{5,4,3,2,1,0:T(8,128)(2,1)} %maximum_bitcast_fusion.1), calls=%async_computation.2 | async-start | bytes 8388608 | tf_op jit(solution)/shard_map/all_to_all | solution.py:95
  168.3 0.0 copy-done.4
  168.3 0.1 add_subtract_fusion
  168.4 0.7 fusion.3
  176.4 0.0 copy-start.2
  176.4 17.6 %shard_map.38 = f32[2,2,33,32,128]{4,3,2,1,0:T(8,128)} custom-call(bf16[8,2,2,32,16,256]{5,4,3,2,1,0:T(8,128)(2,1)} %all-to-all-done.1.x_ref), custom_call_target="tpu_custom_call" | custom-call | tf_op jit(solution)/shard_map/pallas_call | solution.py:57
  194.0 0.0 copy-done.2
  194.0 0.1 add_bitcast_fusion.7
  194.0 1.8 add_bitcast_fusion.2
  195.8 0.0 copy-start
  195.8 0.1 pad_maximum_fusion
  195.9 0.1 add_bitcast_fusion.5
  196.0 1.4 copy-done
  197.4 0.3 add_bitcast_fusion
  197.7 0.1 pad_maximum_fusion.1
  197.8 0.1 pad_maximum_fusion.2
  197.8 17.5 %all-to-all-done.2.x_ref = bf16[8,2,2,16,16,256]{5,4,3,2,1,0:T(8,128)(2,1)} async-done(((bf16[8,2,2,16,16,256]{5,4,3,2,1,0:T(8,128)(2,1)}), bf16[8,2,2,16,16,256]{5,4,3,2,1,0:T(8,128)(2,1)}, u32[]{:S(2)}, u32[]{:S(2)}) %all-to-all-start.2) | async-done | bytes 4194336 | tf_op jit(solution)/shard_map/all_to_all | solution.py:95
  215.3 7.9 %collective-permute-start.1 = (f32[33,48,128]{2,1,0:T(8,128)S(1)}, f32[33,48,128]{2,1,0:T(8,128)S(1)}, u32[]{:S(2)}, u32[]{:S(2)}) collective-permute-start(f32[33,48,128]{2,1,0:T(8,128)S(1)} %pad_maximum_fusion.2), channel_id=1, source_target_pairs={{0,8},{8,16},{16,24},{24,32},{32,40},{40,48},{48,56},{56,64},{64,7... | collective-permute-start | bytes 2433032 | tf_op jit(solution)/shard_map/ppermute | solution.py:19
  223.2 1.9 collective-permute-start
  225.1 9.7 %shard_map.39 = f32[2,2,33,16,128]{4,3,2,1,0:T(8,128)} custom-call(bf16[8,2,2,16,16,256]{5,4,3,2,1,0:T(8,128)(2,1)} %all-to-all-done.2.x_ref), custom_call_target="tpu_custom_call" | custom-call | tf_op jit(solution)/shard_map/pallas_call | solution.py:57
  234.8 1.4 add_bitcast_fusion.4
  236.2 5.2 %collective-permute-start.3 = (f32[33,16,128]{2,1,0:T(8,128)S(1)}, f32[33,16,128]{2,1,0:T(8,128)S(1)}, u32[]{:S(2)}, u32[]{:S(2)}) collective-permute-start(f32[33,16,128]{2,1,0:T(8,128)S(1)} %get-tuple-element.32), channel_id=1, source_target_pairs={{0,8},{8,16},{16,24},{24,32},{32,40},{40,48},{48,56},{56,64},{64,7... | collective-permute-start | bytes 811016 | tf_op jit(solution)/shard_map/ppermute | solution.py:19
  241.4 1.9 collective-permute-start.2
  243.3 1.5 collective-permute-done.3
  244.8 5.9 %collective-permute-done.2 = f32[33,16,128]{2,1,0:T(8,128)S(1)} collective-permute-done((f32[33,16,128]{2,1,0:T(8,128)S(1)}, f32[33,16,128]{2,1,0:T(8,128)S(1)}, u32[]{:S(2)}, u32[]{:S(2)}) %collective-permute-start.2) | collective-permute-done | bytes 270368 | tf_op jit(solution)/shard_map/ppermute | solution.py:19
  250.7 0.0 copy-done.3
  250.7 0.1 fusion
  250.8 0.0 collective-permute-done.1
  250.8 0.0 collective-permute-done
  250.8 1.3 add_add_fusion
  252.1 1.1 maximum_bitcast_fusion.3
  (4 shorter events, 0.0 us)
Async XLA Ops:
  0.0 4.6 %copy-start.1 = (bf16[2,16,64,8,256]{4,3,2,1,0:T(8,128)(2,1)S(1)}, bf16[2,16,64,8,256]{4,3,2,1,0:T(8,128)(2,1)}, u32[]{:S(2)}) copy-start(bf16[2,16,64,8,256]{4,3,2,1,0:T(8,128)(2,1)} %param.3) | copy-start | bytes 25165828
  11.3 54.7 %all-to-all-start = ((bf16[8,2,2,16,16,256]{5,4,3,2,1,0:T(8,128)(2,1)}), bf16[8,2,2,16,16,256]{5,4,3,2,1,0:T(8,128)(2,1)}, u32[]{:S(2)}, u32[]{:S(2)}) async-start(bf16[8,2,2,16,16,256]{5,4,3,2,1,0:T(8,128)(2,1)} %maximum_bitcast_fusion.2), calls=%async_computation | async-start | bytes 8388608 | tf_op jit(solution)/shard_map/all_to_all | solution.py:95
  17.3 2.2 slice-start
  17.3 3.5 %slice-start.1 = ((bf16[2,16,64,8,256]{4,3,2,1,0:T(8,128)(2,1)}), bf16[2,16,32,8,256]{4,3,2,1,0:T(8,128)(2,1)S(1)}, s32[]{:S(2)}) async-start(bf16[2,16,64,8,256]{4,3,2,1,0:T(8,128)(2,1)} %param.3), calls=%async_computation.4 | async-start | bytes 8388608 | tf_op jit(solution)/shard_map/slice | solution.py:89
  66.0 97.7 %all-to-all-start.1 = ((bf16[8,2,2,32,16,256]{5,4,3,2,1,0:T(8,128)(2,1)}), bf16[8,2,2,32,16,256]{5,4,3,2,1,0:T(8,128)(2,1)}, u32[]{:S(2)}, u32[]{:S(2)}) async-start(bf16[8,2,2,32,16,256]{5,4,3,2,1,0:T(8,128)(2,1)} %maximum_bitcast_fusion), calls=%async_computation.1 | async-start | bytes 16777216 | tf_op jit(solution)/shard_map/all_to_all | solution.py:95
  87.2 81.1 %copy-start.4 = (s32[2]{0:T(128)S(1)}, s32[2]{0:T(128)}, u32[]{:S(2)}) copy-start(s32[2]{0:T(128)} %param.5) | copy-start | bytes 28
  163.7 51.6 %all-to-all-start.2 = ((bf16[8,2,2,16,16,256]{5,4,3,2,1,0:T(8,128)(2,1)}), bf16[8,2,2,16,16,256]{5,4,3,2,1,0:T(8,128)(2,1)}, u32[]{:S(2)}, u32[]{:S(2)}) async-start(bf16[8,2,2,16,16,256]{5,4,3,2,1,0:T(8,128)(2,1)} %maximum_bitcast_fusion.1), calls=%async_computation.2 | async-start | bytes 8388608 | tf_op jit(solution)/shard_map/all_to_all | solution.py:95
  176.4 17.6 %copy-start.2 = (f32[2,2,33,16,128]{4,3,2,1,0:T(8,128)S(1)}, f32[2,2,33,16,128]{4,3,2,1,0:T(8,128)}, u32[]{:S(2)}) copy-start(f32[2,2,33,16,128]{4,3,2,1,0:T(8,128)} %shard_map.37) | copy-start | bytes 3244036
  195.8 1.6 copy-start
  215.3 35.5 %collective-permute-start.1 = (f32[33,48,128]{2,1,0:T(8,128)S(1)}, f32[33,48,128]{2,1,0:T(8,128)S(1)}, u32[]{:S(2)}, u32[]{:S(2)}) collective-permute-start(f32[33,48,128]{2,1,0:T(8,128)S(1)} %pad_maximum_fusion.2), channel_id=1, source_target_pairs={{0,8},{8,16},{16,24},{24,32},{32,40},{40,48},{48,56},{56,64},{64,7... | collective-permute-start | bytes 2433032 | tf_op jit(solution)/shard_map/ppermute | solution.py:19
  223.2 27.6 %collective-permute-start = (f32[33,48,128]{2,1,0:T(8,128)S(1)}, f32[33,48,128]{2,1,0:T(8,128)}, u32[]{:S(2)}, u32[]{:S(2)}) collective-permute-start(f32[33,48,128]{2,1,0:T(8,128)S(1)} %pad_maximum_fusion), channel_id=1, source_target_pairs={{8,0},{16,8},{24,16},{32,24},{40,32},{48,40},{56,48},{64,56},{72,6... | collective-permute-start | bytes 2433032 | tf_op jit(solution)/shard_map/ppermute | solution.py:19
  234.8 15.9 %copy-start.3 = (f32[2,2,33,16,128]{4,3,2,1,0:T(8,128)S(1)}, f32[2,2,33,16,128]{4,3,2,1,0:T(8,128)}, u32[]{:S(2)}) copy-start(f32[2,2,33,16,128]{4,3,2,1,0:T(8,128)} %shard_map.39) | copy-start | bytes 3244036
  236.2 8.5 %collective-permute-start.3 = (f32[33,16,128]{2,1,0:T(8,128)S(1)}, f32[33,16,128]{2,1,0:T(8,128)S(1)}, u32[]{:S(2)}, u32[]{:S(2)}) collective-permute-start(f32[33,16,128]{2,1,0:T(8,128)S(1)} %get-tuple-element.32), channel_id=1, source_target_pairs={{0,8},{8,16},{16,24},{24,32},{32,40},{40,48},{48,56},{56,64},{64,7... | collective-permute-start | bytes 811016 | tf_op jit(solution)/shard_map/ppermute | solution.py:19
  241.4 9.3 %collective-permute-start.2 = (f32[33,16,128]{2,1,0:T(8,128)S(1)}, f32[33,16,128]{2,1,0:T(8,128)S(1)}, u32[]{:S(2)}, u32[]{:S(2)}) collective-permute-start(f32[33,16,128]{2,1,0:T(8,128)S(1)} %get-tuple-element.31), channel_id=1, source_target_pairs={{8,0},{16,8},{24,16},{32,24},{40,32},{48,40},{56,48},{64,56},{72,6... | collective-permute-start | bytes 811016 | tf_op jit(solution)/shard_map/ppermute | solution.py:19
